TPU v7x, 256 devices: a whole 4x4x8 slice. The times are simulated.
256 devices in a mesh: dp: 32 (over y, z), expert: 8 (over x, core).
Axes of the slice: x: 4, y: 4, z: 8, core: 2. Of those that a mesh axis runs over, the one named last changes fastest.
Arguments:
- master: float32 [8, 4096, 1536], P('expert', 'dp'), may hold values from -0.109375 to 0.109375
- moment_one: float32 [8, 4096, 1536], P('expert', 'dp'), may hold values from -1.5 to 1.5
- moment_two: float32 [8, 4096, 1536], P('expert', 'dp'), may hold values from 0.0001 to 0.003
- saved_rows: bfloat16 [8, 12288, 1536], P('expert', 'dp'), may hold values from -6 to 6
- saved_grads: bfloat16 [8, 12288, 4096], P('expert', 'dp'), may hold values from -0.109375 to 0.109375
- slot_rows: bfloat16 [32768, 2, 1536], P(('dp', 'expert')), may hold values from -6 to 6
- routes: int32 [32768, 2], P(('dp', 'expert')), may hold values from 0 to 7, all different within a row; in each aligned block of 128 rows (0 to 127, 128 to 255, ...) at most 40 rows name the same one
- gates: float32 [32768, 2], P(('dp', 'expert')), may hold values from 0.1 to 1
Outputs:
- master_new: float32 [8, 4096, 1536], P('expert', 'dp')
- moment_one_new: float32 [8, 4096, 1536], P('expert', 'dp')
- moment_two_new: float32 [8, 4096, 1536], P('expert', 'dp')
- mixed: bfloat16 [32768, 4096], P(('dp', 'expert'))
Inputs may be any that keep to these rules, and one draw needn't show every extreme that they name: `routes`: each token names 2 different experts. Among the 128 tokens of one device (aligned blocks of rows in device order, dp slowest) at most 40 name the same expert, and in some device's block exactly 40 do.
All inputs are finite; a program needn't handle non-finite values.
Results may differ from a plain program's by a relative error of at most 0.034.
Values may be sent and summed in bfloat16 or wider, within the bound.
No kernel may reach another device: no remote copies, remote signals or barrier semaphores. Data moves between devices by JAX's collectives and lax.ppermute only.
A program may use at most 128 MiB of HBM per device.

v0:
```python
import jax
import jax.numpy as jnp
from jax import lax
from jax.sharding import PartitionSpec as P

beta_one = 0.9
beta_two = 0.999
learn_rate = 0.002
tiny_eps = 1e-08
steps_done = 100.0


def adam_update(master, moment_one, moment_two, grad):
    m_new = beta_one * moment_one + (1.0 - beta_one) * grad
    v_new = beta_two * moment_two + (1.0 - beta_two) * grad * grad
    fix_one = 1.0 - beta_one**steps_done
    fix_two = 1.0 - beta_two**steps_done
    step_size = m_new / fix_one / (jnp.sqrt(v_new / fix_two) + tiny_eps)
    return (master - learn_rate * step_size, m_new, v_new)


def slot_places(routes, experts):
    flat = routes.reshape(-1)
    onehot = (flat[:, None] == jnp.arange(experts, dtype=jnp.int32)[None, :]).astype(jnp.int32)
    place = jnp.sum((jnp.cumsum(onehot, axis=0) - onehot) * onehot, axis=1)
    return (flat, place)


def send_back(results):
    return lax.all_to_all(results, "expert", split_axis=0, concat_axis=0, tiled=True)


def body(master, moment_one, moment_two, saved_rows, saved_grads, slot_rows, routes, gates):
    rows_here = saved_rows[0]
    grads_here = saved_grads[0]
    grad = lax.psum_scatter(
        lax.dot_general(
            grads_here, rows_here, (((0,), (0,)), ((), ())), preferred_element_type=jnp.float32
        ).astype(jnp.bfloat16),
        "dp",
        scatter_dimension=0,
        tiled=True,
    ).astype(jnp.float32)
    master_new, m_new, v_new = adam_update(master[0], moment_one[0], moment_two[0], grad)
    weights_shard = master_new.astype(jnp.bfloat16)
    experts = lax.axis_size("expert")
    tok_count, top_count, width = slot_rows.shape
    capacity = tok_count * top_count * 5 // (4 * experts)
    flat, place = slot_places(routes, experts)
    outgoing = (
        jnp.zeros((experts, capacity, width), jnp.bfloat16)
        .at[flat, place]
        .set(slot_rows.reshape(-1, width))
    )
    weights = lax.all_gather(weights_shard, "dp", axis=0, tiled=True)
    out_width = weights.shape[0]
    received = lax.all_to_all(outgoing, "expert", split_axis=0, concat_axis=0, tiled=True)
    sources, count, _ = received.shape
    product = lax.dot_general(
        received.reshape(-1, width),
        weights,
        (((1,), (1,)), ((), ())),
        preferred_element_type=jnp.float32,
    )
    returned = send_back(product.astype(jnp.bfloat16).reshape(sources, count, out_width))
    out_width = returned.shape[2]
    picked = returned[flat, place].astype(jnp.float32).reshape(tok_count, top_count, out_width)
    mixed = jnp.sum(picked * gates[:, :, None], axis=1).astype(jnp.bfloat16)
    return (master_new[None], m_new[None], v_new[None], mixed)


def solution(mesh):
    placed = (
        P("expert", "dp", None),
        P("expert", "dp", None),
        P("expert", "dp", None),
        P("expert", "dp", None),
        P("expert", "dp", None),
        P(("dp", "expert"), None, None),
        P(("dp", "expert"), None),
        P(("dp", "expert"), None),
    )
    return jax.shard_map(
        body,
        mesh=mesh,
        in_specs=placed,
        out_specs=(
            P("expert", "dp", None),
            P("expert", "dp", None),
            P("expert", "dp", None),
            P(("dp", "expert"), None),
        ),
        check_vma=False,
    )
```

profile of v0, /device:TPU:1, one launch (start us, length us, event | category | flops | bytes accessed | tf_op | source)
XLA Modules:
  0.0 461.5 jit_solution(4875685492731966594)
XLA Ops:
  7.2 1.8 copy-done
  9.1 10.9 %convolution_convert_fusion = bf16[4096,1536]{1,0:T(8,128)(2,1)} fusion(bf16[1,384,4096]{2,1,0:T(8,128)(2,1)S(1)} %copy-done, bf16[1,384,1536]{2,1,0:T(8,128)(2,1)} %param.11), kind=kOutput, calls=%fused_computation.2 | convolution fusion | flops 4838129664 | bytes 16908288 | tf_op jit(solution)/shard_map/dot_general | solution.py:37
  20.0 0.0 all-gather.2.cloned.1.call-start
  20.0 238.8 %reduce-scatter.2.cloned.1.call-done = bf16[128,1536]{1,0:T(8,128)(2,1)} async-done(((bf16[4096,1536]{1,0:T(8,128)(2,1)}), bf16[128,1536]{1,0:T(8,128)(2,1)}) %reduce-scatter.2.cloned.1.call-update) | async-done | bytes 393232 | tf_op jit(solution)/shard_map/reduce_scatter | solution.py:36
  258.8 3.8 fusion.10
  262.6 0.1 copy.13
  262.8 0.1 reshape.87
  262.9 0.1 eq.29
  263.0 0.1 eq.25
  263.2 0.6 reduce-window.6
  263.8 0.2 slice_reduce_fusion
  264.0 3.0 reshape.101
  267.0 0.1 fusion.7
  267.1 1.0 broadcast_in_dim.21
  268.1 41.2 %scatter_fusion = bf16[8,40,1536]{2,1,0:T(8,128)(2,1)} fusion(bf16[8,40,1536]{2,1,0:T(8,128)(2,1)} %broadcast_in_dim.21, s32[256]{0:T(256)S(1)} %bitcast.44, bf16[256,1536]{1,0:T(8,128)(2,1)} %reshape.101), kind=kCustom, calls=%fused_computation.1 | custom fusion | bytes 2361344 | tf_op jit(solution)/shard_map/scatter | solution.py:53
  309.3 23.7 %all_to_all.10 = bf16[8,40,1536]{2,1,0:T(8,128)(2,1)} all-to-all(bf16[8,40,1536]{2,1,0:T(8,128)(2,1)} %scatter_fusion), channel_id=1, replica_groups=mesh['dp'=32,'expert'=8] {'expert'}, dimensions={0} | all-to-all | bytes 1966080 | tf_op jit(solution)/shard_map/all_to_all | solution.py:57
  333.0 50.8 %all-gather.2.cloned.1.call-done = bf16[4096,1536]{1,0:T(8,128)(2,1)} async-done(((bf16[128,1536]{1,0:T(8,128)(2,1)}), bf16[4096,1536]{1,0:T(8,128)(2,1)}) %all-gather.2.cloned.1.call-update) | async-done | bytes 12582928 | tf_op jit(solution)/shard_map/all_gather | solution.py:55
  383.9 10.6 %convolution_convert_fusion.1 = bf16[320,4096]{1,0:T(8,128)(2,1)} fusion(bf16[320,1536]{1,0:T(8,128)(2,1)} %bitcast.46, bf16[4096,1536]{1,0:T(8,128)(2,1)} %all-gather.2.cloned.1.call-done), kind=kOutput, calls=%fused_computation.3 | convolution fusion | flops 4027842560 | bytes 16187392 | tf_op jit(solution)/shard_map/dot_general | solution.py:59
  394.5 5.8 %all-to-all-start.1 = ((bf16[8,40,4096]{2,1,0:T(8,128)(2,1)}), bf16[8,40,4096]{2,1,0:T(8,128)(2,1)}, u32[]{:S(2)}, u32[]{:S(2)}) async-start(bf16[8,40,4096]{2,1,0:T(8,128)(2,1)} %bitcast.45), calls=%async_computation.2 | async-start | bytes 5242880 | tf_op jit(solution)/shard_map/all_to_all | solution.py:30
  400.3 0.1 copy.16
  400.4 31.8 %all-to-all-done.1 = bf16[8,40,4096]{2,1,0:T(8,128)(2,1)} async-done(((bf16[8,40,4096]{2,1,0:T(8,128)(2,1)}), bf16[8,40,4096]{2,1,0:T(8,128)(2,1)}, u32[]{:S(2)}, u32[]{:S(2)}) %all-to-all-start.1) | async-done | bytes 2621472 | tf_op jit(solution)/shard_map/all_to_all | solution.py:30
  432.2 7.4 %gather_fusion = bf16[256,4096]{1,0:T(8,128)(2,1)} fusion(bf16[8,40,4096]{2,1,0:T(8,128)(2,1)} %all-to-all-done.1, s32[256]{0:T(256)S(1)} %bitcast.43), kind=kCustom, calls=%fused_computation | custom fusion | bytes 4196352 | tf_op jit(solution)/shard_map/gather | solution.py:67
  439.6 5.4 %reshape.92 = f32[128,2,4096]{2,1,0:T(2,128)} reshape(bf16[256,4096]{1,0:T(8,128)(2,1)} %gather_fusion) | data formatting | bytes 6291456 | tf_op jit(solution)/shard_map/convert_element_type | solution.py:67
  445.0 9.6 %multiply_reduce_fusion = bf16[128,4096]{1,0:T(8,128)(2,1)} fusion(f32[128,2,4096]{2,1,0:T(2,128)} %reshape.92, f32[128,2]{1,0:T(8,128)S(1)} %copy.16), kind=kLoop, calls=%fused_computation.4 | loop fusion | flops 1572864 | bytes 5243904 | tf_op jit(solution)/shard_map/reduce_sum | solution.py:68
  (12 shorter events, 0.1 us)
Async XLA Ops:
  7.2 1.9 copy-start
  7.2 251.6 %reduce-scatter.2.cloned.1.call-start = ((), (), s32[]{:S(2)}) async-start(), calls=%async_computation.3 | async-start | bytes 12976128 | tf_op jit(solution)/shard_map/reduce_scatter | solution.py:36
  20.0 242.7 %copy-start.1 = (s32[128,2]{0,1:T(2,128)S(1)}, s32[128,2]{0,1:T(2,128)}, u32[]{:S(2)}) copy-start(s32[128,2]{0,1:T(2,128)} %param.14) | copy-start | bytes 3076
  20.0 363.9 %all-gather.2.cloned.1.call-start = ((), (), s32[]{:S(2)}) async-start(), calls=%async_computation.4 | async-start | bytes 12976128 | tf_op jit(solution)/shard_map/all_gather | solution.py:55
  394.5 5.8 %copy-start.2 = (f32[128,2]{0,1:T(2,128)S(1)}, f32[128,2]{0,1:T(2,128)}, u32[]{:S(2)}) copy-start(f32[128,2]{0,1:T(2,128)} %param.15) | copy-start | bytes 3076
  394.5 37.7 %all-to-all-start.1 = ((bf16[8,40,4096]{2,1,0:T(8,128)(2,1)}), bf16[8,40,4096]{2,1,0:T(8,128)(2,1)}, u32[]{:S(2)}, u32[]{:S(2)}) async-start(bf16[8,40,4096]{2,1,0:T(8,128)(2,1)} %bitcast.45), calls=%async_computation.2 | async-start | bytes 5242880 | tf_op jit(solution)/shard_map/all_to_all | solution.py:30
Sparse Core Ops, SparseCore 0:
  20.1 238.6 reduce-scatter.1
  262.7 121.0 all-gather.1
where the time goes:
time: 463 us; the launch traced here: 462 us
  waiting for transfers between devices  321 us (69%)
  local copies, waits for them, and re-layouts  60.7 us (13%)
  blocking collectives  23.7 us (5%)
  matrix products  21.5 us (5%)
  other arithmetic  14.2 us (3%)
  between operations  14.1 us (3%)
  starting transfers between devices  5.87 us (1%)
    reduce_scatter x1, waiting for transfers between devices, body(): lax.psum_scatter(lax.dot_general(grads_here, rows_here, (((0,), (0,)), ((...  239 us
    all_gather x1, waiting for transfers between devices, body(): weights = lax.all_gather(weights_shard, 'dp', axis=0, tiled=True)  50.8 us
    scatter x1, local copies, waits for them, and re-layouts, body(): outgoing = jnp.zeros((experts, capacity, width), jnp.bfloat16).at[flat, p...  41.2 us
    all_to_all x1, waiting for transfers between devices, send_back(): lax.all_to_all(results, 'expert', split_axis=0, concat_axis=0, tiled=True)  31.8 us
    all_to_all x1, blocking collectives, body(): lax.all_to_all(outgoing, 'expert', split_axis=0, concat_axis=0, tiled=True)  23.7 us
    dot_general x1, matrix products, body(): lax.dot_general(grads_here, rows_here, (((0,), (0,)), ((), ())), preferre...  10.9 us
    dot_general x1, matrix products, body(): lax.dot_general(received.reshape(-1, width), weights, (((1,), (1,)), ((),...  10.6 us
    reduce_sum x1, other arithmetic, body(): mixed = jnp.sum(picked * gates[:, :, None], axis=1).astype(jnp.bfloat16)  9.64 us
  transfers between devices with their start and end apart: 3, of which 3 were waited for; matrix products, arithmetic and copies ran while one was open for 10% of the time, Pallas kernels for 0%

commit v1 on v0

v1 whole, which is shorter than its diff:
```python
import jax
import jax.numpy as jnp
import numpy as np
from jax import lax
from jax.sharding import Mesh
from jax.sharding import PartitionSpec as P

beta_one = 0.9
beta_two = 0.999
learn_rate = 0.002
tiny_eps = 1e-08
steps_done = 100.0


def adam_update(master, moment_one, moment_two, grad):
    m_new = beta_one * moment_one + (1.0 - beta_one) * grad
    v_new = beta_two * moment_two + (1.0 - beta_two) * grad * grad
    fix_one = 1.0 - beta_one**steps_done
    fix_two = 1.0 - beta_two**steps_done
    step_size = m_new / fix_one / (jnp.sqrt(v_new / fix_two) + tiny_eps)
    return (master - learn_rate * step_size, m_new, v_new)


def slot_places(routes, experts):
    flat = routes.reshape(-1)
    onehot = (flat[:, None] == jnp.arange(experts, dtype=jnp.int32)[None, :]).astype(jnp.int32)
    place = jnp.sum((jnp.cumsum(onehot, axis=0) - onehot) * onehot, axis=1)
    return (flat, place)


def body(master, moment_one, moment_two, saved_rows, saved_grads, slot_rows, routes, gates):
    n_hi = lax.axis_size("dy")
    n_lo = lax.axis_size("dz")
    experts = lax.axis_size("expert")

    rows_here = saved_rows[0]
    grads_here = saved_grads[0]
    saved, d_model = grads_here.shape
    group_width = d_model // n_hi
    rows_group = lax.all_gather(rows_here, "dy", axis=0, tiled=True)
    grads_group = lax.all_to_all(
        grads_here.reshape(saved, n_hi, group_width).transpose(1, 0, 2),
        "dy",
        split_axis=0,
        concat_axis=0,
        tiled=True,
    ).reshape(n_hi * saved, group_width)
    partial = lax.dot_general(
        grads_group, rows_group, (((0,), (0,)), ((), ())), preferred_element_type=jnp.float32
    ).astype(jnp.bfloat16)
    grad = lax.psum_scatter(partial, "dz", scatter_dimension=0, tiled=True).astype(jnp.float32)
    master_new, m_new, v_new = adam_update(master[0], moment_one[0], moment_two[0], grad)
    weights_shard = master_new.astype(jnp.bfloat16)

    tok_count, top_count, width = slot_rows.shape
    capacity = tok_count * top_count * 5 // (4 * experts)
    flat, place = slot_places(routes, experts)
    slot_id = flat * capacity + place
    table = jnp.arange(experts * capacity, dtype=jnp.int32)
    select = (table[:, None] == slot_id[None, :]).astype(jnp.bfloat16)
    outgoing = lax.dot_general(
        select, slot_rows.reshape(-1, width), (((1,), (0,)), ((), ())),
        preferred_element_type=jnp.float32,
    ).astype(jnp.bfloat16).reshape(experts, capacity, width)
    received = lax.all_to_all(outgoing, "expert", split_axis=0, concat_axis=0, tiled=True)
    slots_group = lax.all_gather(received, "dy", axis=0, tiled=True).reshape(-1, width)

    weights_group = lax.all_gather(weights_shard, "dz", axis=0, tiled=True)
    product = lax.dot_general(
        slots_group, weights_group, (((1,), (1,)), ((), ())), preferred_element_type=jnp.float32
    ).astype(jnp.bfloat16)
    returned = lax.all_to_all(
        product, ("dy", "expert"), split_axis=0, concat_axis=0, tiled=True
    ).reshape(n_hi, experts * capacity, group_width)

    slot_pairs = slot_id.reshape(tok_count, top_count)
    combine = jnp.sum(
        (slot_pairs[:, :, None] == table[None, None, :]).astype(jnp.float32) * gates[:, :, None],
        axis=1,
    )
    mixed = jnp.einsum(
        "ts,hsf->thf",
        combine,
        returned.astype(jnp.float32),
        precision=lax.Precision.HIGHEST,
        preferred_element_type=jnp.float32,
    )
    mixed = mixed.reshape(tok_count, n_hi * group_width).astype(jnp.bfloat16)
    return (master_new[None], m_new[None], v_new[None], mixed)


def split_mesh(mesh):
    devices = mesh.devices
    dp_size, ex_size = devices.shape
    column = devices[:, 0]
    try:
        n_hi = len({d.coords[1] for d in column})
    except Exception:
        n_hi = 1
    if n_hi < 1 or dp_size % n_hi:
        n_hi = 1
    return Mesh(devices.reshape(n_hi, dp_size // n_hi, ex_size), ("dy", "dz", "expert"))


def solution(mesh):
    inner = split_mesh(mesh)
    dp = ("dy", "dz")
    placed = (
        P("expert", dp, None),
        P("expert", dp, None),
        P("expert", dp, None),
        P("expert", dp, None),
        P("expert", dp, None),
        P(dp + ("expert",), None, None),
        P(dp + ("expert",), None),
        P(dp + ("expert",), None),
    )
    return jax.shard_map(
        body,
        mesh=inner,
        in_specs=placed,
        out_specs=(
            P("expert", dp, None),
            P("expert", dp, None),
            P("expert", dp, None),
            P(dp + ("expert",), None),
        ),
        check_vma=False,
    )
```

time: 463 us -> 309 us (0.67)
  waiting for transfers between devices: 321 us -> 169 us
  blocking collectives: 23.7 us -> 82.1 us
  local copies, waits for them, and re-layouts: 60.7 us -> 9.6 us
  other arithmetic: 14.2 us -> 3.88 us
    reduce_scatter x1, waiting for transfers between devices: 239 us -> 23.2 us  [body(): lax.psum_scatter(partial, 'dz', scatter_dimension=0, tiled=True)]
    all_to_all x0 -> x1, blocking collectives: none -> 63.1 us  [body(): lax.all_to_all(grads_here.reshape(saved, n_hi, group_width).transpose(1,...]
    all_gather x1 -> x3, waiting for transfers between devices: 50.8 us -> 112 us  [the longest x1 49.7 us: body(): lax.all_gather(received, 'dy', axis=0, tiled=True).reshape(-1, width)]
    scatter x1 -> x0, local copies, waits for them, and re-layouts: 41.2 us -> none  [body(): outgoing = jnp.zeros((experts, capacity, width), jnp.bfloat16).at[flat, p...]
    reduce_sum x1, other arithmetic: 9.64 us -> 0.06 us  [body(): jnp.sum((slot_pairs[:, :, None] == table[None, None, :]).astype(jnp.float...]
    gather x1 -> x0, local copies, waits for them, and re-layouts: 7.37 us -> none  [body(): returned[flat, place].astype(jnp.float32)]
    convert_element_type x1 -> x0, local copies, waits for them, and re-layouts: 5.44 us -> none  [body(): returned[flat, place].astype(jnp.float32)]
    all_to_all x1, blocking collectives: 23.7 us -> 19 us  [body(): lax.all_to_all(outgoing, 'expert', split_axis=0, concat_axis=0, tiled=True)]
  transfers between devices with their start and end apart: 3 -> 5, of which waited for: 3 -> 5; matrix products, arithmetic and copies ran while one was open for 10% -> 4% of each run, Pallas kernels for 0% -> 0%
where the time goes in v1:
time: 309 us
  waiting for transfers between devices  169 us (55%)
  blocking collectives  82.1 us (27%)
  matrix products  21.4 us (7%)
  between operations  13.9 us (4%)
  local copies, waits for them, and re-layouts  9.6 us (3%)
  starting transfers between devices  8.39 us (3%)
  other arithmetic  3.88 us (1%)
    all_to_all x1, blocking collectives, body(): lax.all_to_all(grads_here.reshape(saved, n_hi, group_width).transpose(1,...  63.1 us
    all_gather x1, waiting for transfers between devices, body(): lax.all_gather(received, 'dy', axis=0, tiled=True).reshape(-1, width)  49.7 us
    all_gather x1, waiting for transfers between devices, body(): weights_group = lax.all_gather(weights_shard, 'dz', axis=0, tiled=True)  47.1 us
    all_to_all x1, waiting for transfers between devices, body(): lax.all_to_all(product, ('dy', 'expert'), split_axis=0, concat_axis=0, ti...  33.7 us
    reduce_scatter x1, waiting for transfers between devices, body(): lax.psum_scatter(partial, 'dz', scatter_dimension=0, tiled=True)  23.2 us
    all_to_all x1, blocking collectives, body(): lax.all_to_all(outgoing, 'expert', split_axis=0, concat_axis=0, tiled=True)  19 us
    all_gather x1, waiting for transfers between devices, body(): rows_group = lax.all_gather(rows_here, 'dy', axis=0, tiled=True)  14.9 us
    dot_general x1, matrix products, body(): lax.dot_general(grads_group, rows_group, (((0,), (0,)), ((), ())), prefer...  9.26 us
  transfers between devices with their start and end apart: 5, of which 5 were waited for; matrix products, arithmetic and copies ran while one was open for 4% of the time, Pallas kernels for 0%

profile of v1, /device:TPU:1, one launch (start us, length us, event | category | flops | bytes accessed | tf_op | source)
XLA Modules:
  0.0 308.7 jit_solution(367635270974102597)
XLA Ops:
  7.2 0.7 all-gather.9.cloned.1.call-update
  7.9 4.6 %copy.43 = bf16[1,384,4096]{1,2,0:T(8,128)(2,1)} copy(bf16[1,384,4096]{2,1,0:T(8,128)(2,1)} %param.12) | data formatting | bytes 6291456 | tf_op args[4]
  12.6 63.1 %all_to_all.19 = bf16[4,384,1024]{1,2,0:T(8,128)(2,1)S(1)} all-to-all(bf16[4,384,1024]{1,2,0:T(8,128)(2,1)} %bitcast.53), channel_id=1, replica_groups=mesh['dy'=4,'dz'=8,'expert'=8] {'dy'}, dimensions={0} | all-to-all | bytes 6291456 | tf_op jit(solution)/shard_map/all_to_all | solution.py:41
  75.7 3.0 copy.44
  78.7 14.9 %all-gather.9.cloned.1.call-done = bf16[1,1536,1536]{2,1,0:T(8,128)(2,1)} async-done(((bf16[1,384,1536]{2,1,0:T(8,128)(2,1)}), bf16[1,1536,1536]{2,1,0:T(8,128)(2,1)}) %all-gather.9.cloned.1.call-update) | async-done | bytes 4718608 | tf_op jit(solution)/shard_map/all_gather | solution.py:40
  93.6 9.3 %fusion.2 = bf16[1024,1536]{1,0:T(8,128)(2,1)} fusion(bf16[1536,1024]{1,0:T(8,128)(2,1)} %bitcast.57, bf16[1,1536,1536]{2,1,0:T(8,128)(2,1)} %all-gather.9.cloned.1.call-done), kind=kOutput, calls=%fused_computation.3 | convolution fusion | flops 4833411072 | bytes 11010048 | tf_op jit(solution)/shard_map/dot_general | solution.py:48
  102.9 0.6 copy-done.4
  103.6 0.1 eq.55
  103.8 0.1 eq.51
  103.9 0.6 reduce-window.6
  104.5 0.2 slice_reduce_fusion
  104.8 0.3 reshape.67
  105.2 0.4 convolution_convert_fusion.2
  105.6 19.0 %all_to_all.20 = bf16[8,40,1536]{2,1,0:T(8,128)(2,1)} all-to-all(bf16[8,40,1536]{2,1,0:T(8,128)(2,1)S(1)} %bitcast.56), channel_id=1, replica_groups=mesh['dy'=4,'dz'=8,'expert'=8] {'expert'}, dimensions={0} | all-to-all | bytes 1966080 | tf_op jit(solution)/shard_map/all_to_all | solution.py:65
  124.8 23.2 %reduce-scatter.2.cloned.1.call-done = bf16[128,1536]{1,0:T(8,128)(2,1)} async-done(((bf16[1024,1536]{1,0:T(8,128)(2,1)}), bf16[128,1536]{1,0:T(8,128)(2,1)}) %reduce-scatter.2.cloned.1.call-update) | async-done | bytes 393232 | tf_op jit(solution)/shard_map/reduce_scatter | solution.py:51
  148.0 3.1 %fusion.13 = (bf16[128,1536]{1,0:T(8,128)(2,1)}, f32[128,1536]{1,0:T(8,128)}, f32[1,128,1536]{2,1,0:T(8,128)}, f32[1,128,1536]{2,1,0:T(8,128)}) fusion(f32[1,128,1536]{2,1,0:T(8,128)S(1)} %copy-done.1, bf16[128,1536]{1,0:T(8,128)(2,1)} %reduce-scatter.2.cloned.1.call-done, f32[1,128,1536]{2,1,0:T(8,128)S(1)} %copy-done.2, f32[1,128,1536]{2,1,0:T(8,128)S(1)} %copy-done.3), kind=kLoop, calls=%fused_computation.26 | loop fusion | flops 2949120 | bytes 5505024 | tf_op jit(solution)/shard_map/convert_element_type | solution.py:53
  151.1 49.7 %all-gather.5.cloned.1.call-done = bf16[32,40,1536]{2,1,0:T(8,128)(2,1)} async-done(((bf16[8,40,1536]{2,1,0:T(8,128)(2,1)}), bf16[32,40,1536]{2,1,0:T(8,128)(2,1)}) %all-gather.5.cloned.1.call-update) | async-done | bytes 3932176 | tf_op jit(solution)/shard_map/all_gather | solution.py:66
  200.8 47.1 %all-gather.7.cloned.1.call-done = bf16[1024,1536]{1,0:T(8,128)(2,1)} async-done(((bf16[128,1536]{1,0:T(8,128)(2,1)}), bf16[1024,1536]{1,0:T(8,128)(2,1)}) %all-gather.7.cloned.1.call-update) | async-done | bytes 3145744 | tf_op jit(solution)/shard_map/all_gather | solution.py:68
  248.0 8.9 %convolution_convert_fusion.1 = bf16[1280,1024]{1,0:T(8,128)(2,1)} fusion(bf16[1280,1536]{1,0:T(8,128)(2,1)} %bitcast.60, bf16[1024,1536]{1,0:T(8,128)(2,1)} %all-gather.7.cloned.1.call-done), kind=kOutput, calls=%fused_computation.4 | convolution fusion | flops 4027842560 | bytes 9699328 | tf_op jit(solution)/shard_map/dot_general | solution.py:69
  256.9 8.2 %all-to-all-start.2 = ((bf16[32,40,1024]{2,1,0:T(8,128)(2,1)}), bf16[32,40,1024]{2,1,0:T(8,128)(2,1)S(1)}, u32[]{:S(2)}, u32[]{:S(2)}) async-start(bf16[32,40,1024]{2,1,0:T(8,128)(2,1)} %bitcast.58), calls=%async_computation.3 | async-start | bytes 5242880 | tf_op jit(solution)/shard_map/all_to_all | solution.py:72
  265.1 0.1 reduce_sum.21
  265.4 33.7 %all-to-all-done.2 = bf16[32,40,1024]{2,1,0:T(8,128)(2,1)S(1)} async-done(((bf16[32,40,1024]{2,1,0:T(8,128)(2,1)}), bf16[32,40,1024]{2,1,0:T(8,128)(2,1)S(1)}, u32[]{:S(2)}, u32[]{:S(2)}) %all-to-all-start.2) | async-done | bytes 2621472 | tf_op jit(solution)/shard_map/all_to_all | solution.py:72
  299.1 0.3 copy.49
  299.4 2.8 convolution_convert_fusion
  (27 shorter events, 0.6 us)
Async XLA Ops:
  7.2 86.4 %all-gather.9.cloned.1.call-start = ((), (), s32[]{:S(2)}) async-start(), calls=%async_computation.7 | async-start | bytes 5898240 | tf_op jit(solution)/shard_map/all_gather | solution.py:40
  7.9 140.1 %reduce-scatter.2.cloned.1.call-start = ((), (), s32[]{:S(2)}) async-start(), calls=%async_computation.4 | async-start | bytes 3538944 | tf_op jit(solution)/shard_map/reduce_scatter | solution.py:51
  102.8 0.7 copy-start.4
  102.8 1.9 copy-start
  102.9 97.9 %all-gather.5.cloned.1.call-start = ((), (), s32[]{:S(2)}) async-start(), calls=%async_computation.5 | async-start | bytes 4915200 | tf_op jit(solution)/shard_map/all_gather | solution.py:66
  104.8 43.2 %copy-start.1 = (f32[1,128,1536]{2,1,0:T(8,128)S(1)}, f32[1,128,1536]{2,1,0:T(8,128)}, u32[]{:S(2)}) copy-start(f32[1,128,1536]{2,1,0:T(8,128)} %param.10) | copy-start | bytes 2359300
  104.8 43.2 %copy-start.2 = (f32[1,128,1536]{2,1,0:T(8,128)S(1)}, f32[1,128,1536]{2,1,0:T(8,128)}, u32[]{:S(2)}) copy-start(f32[1,128,1536]{2,1,0:T(8,128)} %param.9) | copy-start | bytes 2359300
  105.1 42.9 %copy-start.3 = (f32[1,128,1536]{2,1,0:T(8,128)S(1)}, f32[1,128,1536]{2,1,0:T(8,128)}, u32[]{:S(2)}) copy-start(f32[1,128,1536]{2,1,0:T(8,128)} %param.8) | copy-start | bytes 2359300
  124.7 123.3 %all-gather.7.cloned.1.call-start = ((), (), s32[]{:S(2)}) async-start(), calls=%async_computation.6 | async-start | bytes 3538944 | tf_op jit(solution)/shard_map/all_gather | solution.py:68
  256.9 8.5 %copy-start.5 = (f32[128,2]{0,1:T(2,128)S(1)}, f32[128,2]{0,1:T(2,128)}, u32[]{:S(2)}) copy-start(f32[128,2]{0,1:T(2,128)} %param.15) | copy-start | bytes 3076
  256.9 42.2 %all-to-all-start.2 = ((bf16[32,40,1024]{2,1,0:T(8,128)(2,1)}), bf16[32,40,1024]{2,1,0:T(8,128)(2,1)S(1)}, u32[]{:S(2)}, u32[]{:S(2)}) async-start(bf16[32,40,1024]{2,1,0:T(8,128)(2,1)} %bitcast.58), calls=%async_computation.3 | async-start | bytes 5242880 | tf_op jit(solution)/shard_map/all_to_all | solution.py:72
Sparse Core Ops, SparseCore 0:
  9.8 83.7 all-gather.8
  103.0 44.9 reduce-scatter.1
  149.8 50.9 all-gather.4
  203.0 44.8 all-gather.6

commit v2 on v1

--- a/solution.py
+++ b/solution.py
@@ -48,9 +48,6 @@
     partial = lax.dot_general(
         grads_group, rows_group, (((0,), (0,)), ((), ())), preferred_element_type=jnp.float32
     ).astype(jnp.bfloat16)
-    grad = lax.psum_scatter(partial, "dz", scatter_dimension=0, tiled=True).astype(jnp.float32)
-    master_new, m_new, v_new = adam_update(master[0], moment_one[0], moment_two[0], grad)
-    weights_shard = master_new.astype(jnp.bfloat16)
 
     tok_count, top_count, width = slot_rows.shape
     capacity = tok_count * top_count * 5 // (4 * experts)
@@ -63,7 +60,18 @@
         preferred_element_type=jnp.float32,
     ).astype(jnp.bfloat16).reshape(experts, capacity, width)
     received = lax.all_to_all(outgoing, "expert", split_axis=0, concat_axis=0, tiled=True)
-    slots_group = lax.all_gather(received, "dy", axis=0, tiled=True).reshape(-1, width)
+    received, partial = lax.optimization_barrier((received, partial))
+    shifted = [received]
+    for step in range(1, n_hi):
+        pairs = [(j, (j + step) % n_hi) for j in range(n_hi)]
+        shifted.append(lax.ppermute(received, "dy", pairs))
+    me_hi = lax.axis_index("dy")
+    order = (me_hi - jnp.arange(n_hi, dtype=jnp.int32)) % n_hi
+    slots_group = jnp.take(jnp.stack(shifted), order, axis=0).reshape(-1, width)
+
+    grad = lax.psum_scatter(partial, "dz", scatter_dimension=0, tiled=True).astype(jnp.float32)
+    master_new, m_new, v_new = adam_update(master[0], moment_one[0], moment_two[0], grad)
+    weights_shard = master_new.astype(jnp.bfloat16)
 
     weights_group = lax.all_gather(weights_shard, "dz", axis=0, tiled=True)
     product = lax.dot_general(

time: 309 us -> 271 us (0.88)
  blocking collectives: 82.1 us -> 0 us
  starting transfers between devices: 8.39 us -> 30.3 us
  other arithmetic: 3.88 us -> 11.5 us
  local copies, waits for them, and re-layouts: 9.6 us -> 16.7 us
  waiting for transfers between devices: 169 us -> 175 us
    all_to_all x2 -> x0, blocking collectives: 82.1 us -> none  [the longest x1 63.1 us: body(): lax.all_to_all(grads_here.reshape(saved, n_hi, group_width).transpose(1,...]
    all_to_all x0 -> x2, waiting for transfers between devices: none -> 51.4 us  [the longest x1 51.4 us: body(): lax.all_to_all(grads_here.reshape(saved, n_hi, group_width).transpose(1,...]
    all_gather x1 -> x0, waiting for transfers between devices: 49.7 us -> none  [body(): lax.all_gather(received, 'dy', axis=0, tiled=True).reshape(-1, width)]
    all_gather x1, waiting for transfers between devices: 47.1 us -> 0.01 us  [body(): weights_group = lax.all_gather(weights_shard, 'dz', axis=0, tiled=True)]
    ppermute x0 -> x3, waiting for transfers between devices: none -> 40.8 us  [body(): shifted.append(lax.ppermute(received, 'dy', pairs))]
    reduce_scatter x1, waiting for transfers between devices: 23.2 us -> 45.1 us  [body(): lax.psum_scatter(partial, 'dz', scatter_dimension=0, tiled=True)]
    all_to_all x0 -> x2, starting transfers between devices: none -> 16.7 us  [the longest x1 11.5 us: body(): lax.all_to_all(outgoing, 'expert', split_axis=0, concat_axis=0, tiled=True)]
    all_gather x1, waiting for transfers between devices: 14.9 us -> 3.24 us  [body(): rows_group = lax.all_gather(rows_here, 'dy', axis=0, tiled=True)]
  transfers between devices with their start and end apart: 5 -> 9, of which waited for: 5 -> 7; matrix products, arithmetic and copies ran while one was open for 4% -> 14% of each run, Pallas kernels for 0% -> 0%
where the time goes in v2:
time: 271 us
  waiting for transfers between devices  175 us (65%)
  starting transfers between devices  30.3 us (11%)
  matrix products  23.6 us (9%)
  local copies, waits for them, and re-layouts  16.7 us (6%)
  between operations  13.8 us (5%)
  other arithmetic  11.5 us (4%)
    all_to_all x1, waiting for transfers between devices, body(): lax.all_to_all(grads_here.reshape(saved, n_hi, group_width).transpose(1,...  51.4 us
    reduce_scatter x1, waiting for transfers between devices, body(): lax.psum_scatter(partial, 'dz', scatter_dimension=0, tiled=True)  45.1 us
    ppermute x3, waiting for transfers between devices, body(): shifted.append(lax.ppermute(received, 'dy', pairs))  40.8 us
    all_to_all x1, waiting for transfers between devices, body(): lax.all_to_all(product, ('dy', 'expert'), split_axis=0, concat_axis=0, ti...  33.7 us
    all_to_all x1, starting transfers between devices, body(): lax.all_to_all(outgoing, 'expert', split_axis=0, concat_axis=0, tiled=True)  11.5 us
    dot_general x1, matrix products, body(): lax.dot_general(grads_group, rows_group, (((0,), (0,)), ((), ())), prefer...  9.4 us
    dot_general x1, matrix products, body(): lax.dot_general(slots_group, weights_group, (((1,), (1,)), ((), ())), pre...  8.86 us
    all_to_all x1, starting transfers between devices, body(): lax.all_to_all(product, ('dy', 'expert'), split_axis=0, concat_axis=0, ti...  8.67 us
  transfers between devices with their start and end apart: 9, of which 7 were waited for; matrix products, arithmetic and copies ran while one was open for 14% of the time, Pallas kernels for 0%

profile of v2, /device:TPU:1, one launch (start us, length us, event | category | flops | bytes accessed | tf_op | source)
XLA Modules:
  0.0 270.8 jit_solution(11917959454931758586)
XLA Ops:
  7.9 4.7 %copy.37 = bf16[1,384,4096]{1,2,0:T(8,128)(2,1)} copy(bf16[1,384,4096]{2,1,0:T(8,128)(2,1)} %param.12) | data formatting | bytes 6291456 | tf_op args[4]
  12.6 5.1 %all-to-all-start.1 = ((bf16[4,384,1024]{1,2,0:T(8,128)(2,1)}), bf16[4,384,1024]{1,2,0:T(8,128)(2,1)S(1)}, u32[]{:S(2)}, u32[]{:S(2)}) async-start(bf16[4,384,1024]{1,2,0:T(8,128)(2,1)} %bitcast.60), calls=%async_computation.1 | async-start | bytes 6291456 | tf_op jit(solution)/shard_map/all_to_all | solution.py:41
  19.0 3.0 %reshape.123 = bf16[256,1536]{1,0:T(8,128)(2,1)} reshape(bf16[128,2,1536]{2,1,0:T(2,128)(2,1)} %param.13) | data formatting | bytes 1572864 | tf_op jit(solution)/shard_map/reshape | solution.py:59
  22.0 2.5 convolution_convert_fusion.2
  24.5 51.4 %all-to-all-done.1 = bf16[4,384,1024]{1,2,0:T(8,128)(2,1)S(1)} async-done(((bf16[4,384,1024]{1,2,0:T(8,128)(2,1)}), bf16[4,384,1024]{1,2,0:T(8,128)(2,1)S(1)}, u32[]{:S(2)}, u32[]{:S(2)}) %all-to-all-start.1) | async-done | bytes 3145760 | tf_op jit(solution)/shard_map/all_to_all | solution.py:41
  75.9 11.5 %all-to-all-start = ((bf16[8,40,1536]{2,1,0:T(8,128)(2,1)}), bf16[8,40,1536]{2,1,0:T(8,128)(2,1)}, u32[]{:S(2)}, u32[]{:S(2)}) async-start(bf16[8,40,1536]{2,1,0:T(8,128)(2,1)} %bitcast.63), calls=%async_computation | async-start | bytes 1966080 | tf_op jit(solution)/shard_map/all_to_all | solution.py:62
  87.5 3.0 %copy.38 = bf16[4,384,1024]{2,1,0:T(8,128)(2,1)} copy(bf16[4,384,1024]{1,2,0:T(8,128)(2,1)S(1)} %all-to-all-done.1) | data formatting | bytes 6291456 | tf_op jit(solution)/shard_map/all_to_all | solution.py:41
  90.4 3.2 %all-gather.6.cloned.1.call-done = bf16[1,1536,1536]{2,1,0:T(8,128)(2,1)} async-done(((bf16[1,384,1536]{2,1,0:T(8,128)(2,1)}), bf16[1,1536,1536]{2,1,0:T(8,128)(2,1)}) %all-gather.6.cloned.1.call-update) | async-done | bytes 4718608 | tf_op jit(solution)/shard_map/all_gather | solution.py:40
  93.7 9.4 %fusion.2 = bf16[1024,1536]{1,0:T(8,128)(2,1)} fusion(bf16[1536,1024]{1,0:T(8,128)(2,1)} %bitcast.64, bf16[1,1536,1536]{2,1,0:T(8,128)(2,1)} %all-gather.6.cloned.1.call-done), kind=kOutput, calls=%fused_computation.6 | convolution fusion | flops 4833411072 | bytes 11010048 | tf_op jit(solution)/shard_map/dot_general | solution.py:48
  103.1 45.1 %reduce-scatter.2.cloned.1.call-done = bf16[128,1536]{1,0:T(8,128)(2,1)} async-done(((bf16[1024,1536]{1,0:T(8,128)(2,1)}), bf16[128,1536]{1,0:T(8,128)(2,1)}) %reduce-scatter.2.cloned.1.call-update) | async-done | bytes 393232 | tf_op jit(solution)/shard_map/reduce_scatter | solution.py:72
  148.2 3.1 %fusion.16 = (bf16[128,1536]{1,0:T(8,128)(2,1)}, f32[128,1536]{1,0:T(8,128)}, f32[1,128,1536]{2,1,0:T(8,128)}, f32[1,128,1536]{2,1,0:T(8,128)}) fusion(f32[1,128,1536]{2,1,0:T(8,128)S(1)} %copy-done, bf16[128,1536]{1,0:T(8,128)(2,1)} %reduce-scatter.2.cloned.1.call-done, f32[1,128,1536]{2,1,0:T(8,128)S(1)} %copy-done.1, f32[1,128,1536]{2,1,0:T(8,128)S(1)} %copy-done.2), kind=kLoop, calls=%fused_computation.42 | loop fusion | flops 2949120 | bytes 5505024 | tf_op jit(solution)/shard_map/convert_element_type | solution.py:74
  151.4 1.2 collective-permute-start
  152.6 2.6 collective-permute-start.1
  155.2 1.1 collective-permute-start.2
  156.5 15.8 %collective-permute-done = bf16[8,40,1536]{2,1,0:T(8,128)(2,1)S(1)} collective-permute-done((bf16[8,40,1536]{2,1,0:T(8,128)(2,1)}, bf16[8,40,1536]{2,1,0:T(8,128)(2,1)S(1)}, u32[]{:S(2)}, u32[]{:S(2)}) %collective-permute-start) | collective-permute-done | bytes 983072 | tf_op jit(solution)/shard_map/ppermute | solution.py:67
  172.3 22.5 %collective-permute-done.1 = bf16[8,40,1536]{2,1,0:T(8,128)(2,1)S(1)} collective-permute-done((bf16[8,40,1536]{2,1,0:T(8,128)(2,1)}, bf16[8,40,1536]{2,1,0:T(8,128)(2,1)S(1)}, u32[]{:S(2)}, u32[]{:S(2)}) %collective-permute-start.1) | collective-permute-done | bytes 983072 | tf_op jit(solution)/shard_map/ppermute | solution.py:67
  194.8 2.5 collective-permute-done.2
  197.3 3.1 %pad_maximum_fusion = bf16[4,8,40,1536]{3,2,1,0:T(8,128)(2,1)} fusion(bf16[1,8,40,1536]{3,2,1,0:T(8,128)(2,1)S(1)} %bitcast.68, bf16[1,8,40,1536]{3,2,1,0:T(8,128)(2,1)S(1)} %bitcast.67, bf16[1,8,40,1536]{3,2,1,0:T(8,128)(2,1)S(1)} %bitcast.66, bf16[1,8,40,1536]{3,2,1,0:T(8,128)(2,1)} %bitcast.13), kind=kLoop, calls=%fused_computation.4 | loop fusion | flops 5898240 | bytes 7864320 | tf_op jit(solution)/shard_map/stack | solution.py:70
  200.4 4.8 %gather_fusion = bf16[4,8,40,1536]{3,2,1,0:T(8,128)(2,1)} fusion(bf16[4,8,40,1536]{3,2,1,0:T(8,128)(2,1)} %pad_maximum_fusion, s32[1024]{0:T(1024)S(1)} %pad_clamp_fusion), kind=kCustom, calls=%fused_computation | custom fusion | bytes 7864336 | tf_op jit(solution)/shard_map/jit(_take)/gather | solution.py:70
  205.2 4.4 %bitcast_select_fusion = bf16[1280,1536]{1,0:T(8,128)(2,1)} fusion(bf16[4,8,40,1536]{3,2,1,0:T(8,128)(2,1)} %gather_fusion, pred[1280]{0:T(1024)(128)(4,1)S(1)} %broadcast_in_dim.32), kind=kLoop, calls=%fused_computation.5 | loop fusion | flops 1966080 | bytes 7865600 | tf_op jit(solution)/shard_map/jit(_take)/select_n | solution.py:70
  209.6 8.9 %convolution_convert_fusion.1 = bf16[1280,1024]{1,0:T(8,128)(2,1)} fusion(bf16[1280,1536]{1,0:T(8,128)(2,1)} %bitcast_select_fusion, bf16[1024,1536]{1,0:T(8,128)(2,1)} %all-gather.4.cloned.1.call-done), kind=kOutput, calls=%fused_computation.7 | convolution fusion | flops 4027842560 | bytes 9699328 | tf_op jit(solution)/shard_map/dot_general | solution.py:77
  218.5 8.7 %all-to-all-start.2 = ((bf16[32,40,1024]{2,1,0:T(8,128)(2,1)}), bf16[32,40,1024]{2,1,0:T(8,128)(2,1)S(1)}, u32[]{:S(2)}, u32[]{:S(2)}) async-start(bf16[32,40,1024]{2,1,0:T(8,128)(2,1)} %bitcast.65), calls=%async_computation.3 | async-start | bytes 5242880 | tf_op jit(solution)/shard_map/all_to_all | solution.py:80
  227.5 33.7 %all-to-all-done.2 = bf16[32,40,1024]{2,1,0:T(8,128)(2,1)S(1)} async-done(((bf16[32,40,1024]{2,1,0:T(8,128)(2,1)}), bf16[32,40,1024]{2,1,0:T(8,128)(2,1)S(1)}, u32[]{:S(2)}, u32[]{:S(2)}) %all-to-all-start.2) | async-done | bytes 2621472 | tf_op jit(solution)/shard_map/all_to_all | solution.py:80
  261.4 2.8 %convolution_convert_fusion = bf16[128,4096]{1,0:T(8,128)(2,1)} fusion(f32[128,320]{0,1:T(8,128)S(1)} %select_reduce_fusion, bf16[4096,320]{0,1:T(8,128)(2,1)S(1)} %bitcast.62), kind=kOutput, calls=%fused_computation.1 | convolution fusion | flops 2013790208 | bytes 3833856 | tf_op jit(solution)/shard_map/ts,hsf->thf/dot_general | solution.py:89
  (38 shorter events, 2.9 us)
Async XLA Ops:
  7.2 86.5 %all-gather.6.cloned.1.call-start = ((), (), s32[]{:S(2)}) async-start(), calls=%async_computation.6 | async-start | bytes 5898240 | tf_op jit(solution)/shard_map/all_gather | solution.py:40
  12.6 5.1 %copy-start.3 = (s32[128,2]{0,1:T(2,128)S(1)}, s32[128,2]{0,1:T(2,128)}, u32[]{:S(2)}) copy-start(s32[128,2]{0,1:T(2,128)} %param.14) | copy-start | bytes 3076
  12.6 63.4 %all-to-all-start.1 = ((bf16[4,384,1024]{1,2,0:T(8,128)(2,1)}), bf16[4,384,1024]{1,2,0:T(8,128)(2,1)S(1)}, u32[]{:S(2)}, u32[]{:S(2)}) async-start(bf16[4,384,1024]{1,2,0:T(8,128)(2,1)} %bitcast.60), calls=%async_computation.1 | async-start | bytes 6291456 | tf_op jit(solution)/shard_map/all_to_all | solution.py:41
  75.9 27.1 %all-to-all-start = ((bf16[8,40,1536]{2,1,0:T(8,128)(2,1)}), bf16[8,40,1536]{2,1,0:T(8,128)(2,1)}, u32[]{:S(2)}, u32[]{:S(2)}) async-start(bf16[8,40,1536]{2,1,0:T(8,128)(2,1)} %bitcast.63), calls=%async_computation | async-start | bytes 1966080 | tf_op jit(solution)/shard_map/all_to_all | solution.py:62
  87.5 60.8 %reduce-scatter.2.cloned.1.call-start = ((), (), s32[]{:S(2)}) async-start(), calls=%async_computation.4 | async-start | bytes 3538944 | tf_op jit(solution)/shard_map/reduce_scatter | solution.py:72
  93.7 54.6 %copy-start = (f32[1,128,1536]{2,1,0:T(8,128)S(1)}, f32[1,128,1536]{2,1,0:T(8,128)}, u32[]{:S(2)}) copy-start(f32[1,128,1536]{2,1,0:T(8,128)} %param.10) | copy-start | bytes 2359300
  93.7 54.6 %copy-start.1 = (f32[1,128,1536]{2,1,0:T(8,128)S(1)}, f32[1,128,1536]{2,1,0:T(8,128)}, u32[]{:S(2)}) copy-start(f32[1,128,1536]{2,1,0:T(8,128)} %param.9) | copy-start | bytes 2359300
  93.7 54.6 %copy-start.2 = (f32[1,128,1536]{2,1,0:T(8,128)S(1)}, f32[1,128,1536]{2,1,0:T(8,128)}, u32[]{:S(2)}) copy-start(f32[1,128,1536]{2,1,0:T(8,128)} %param.8) | copy-start | bytes 2359300
  103.1 106.5 %all-gather.4.cloned.1.call-start = ((), (), s32[]{:S(2)}) async-start(), calls=%async_computation.5 | async-start | bytes 3538944 | tf_op jit(solution)/shard_map/all_gather | solution.py:76
  151.4 21.0 %collective-permute-start = (bf16[8,40,1536]{2,1,0:T(8,128)(2,1)}, bf16[8,40,1536]{2,1,0:T(8,128)(2,1)S(1)}, u32[]{:S(2)}, u32[]{:S(2)}) collective-permute-start(bf16[8,40,1536]{2,1,0:T(8,128)(2,1)} %all-to-all-done), channel_id=1, source_target_pairs={{0,64},{64,128},{128,192},{192,0},{1,65},{65,129},{129,193},{193,1... | collective-permute-start | bytes 2949128 | tf_op jit(solution)/shard_map/ppermute | solution.py:67
  152.6 42.2 %collective-permute-start.1 = (bf16[8,40,1536]{2,1,0:T(8,128)(2,1)}, bf16[8,40,1536]{2,1,0:T(8,128)(2,1)S(1)}, u32[]{:S(2)}, u32[]{:S(2)}) collective-permute-start(bf16[8,40,1536]{2,1,0:T(8,128)(2,1)} %all-to-all-done), channel_id=1, source_target_pairs={{0,128},{64,192},{128,0},{192,64},{1,129},{65,193},{129,1},{193,65... | collective-permute-start | bytes 2949128 | tf_op jit(solution)/shard_map/ppermute | solution.py:67
  155.2 42.1 %collective-permute-start.2 = (bf16[8,40,1536]{2,1,0:T(8,128)(2,1)}, bf16[8,40,1536]{2,1,0:T(8,128)(2,1)S(1)}, u32[]{:S(2)}, u32[]{:S(2)}) collective-permute-start(bf16[8,40,1536]{2,1,0:T(8,128)(2,1)} %all-to-all-done), channel_id=1, source_target_pairs={{0,192},{64,0},{128,64},{192,128},{1,193},{65,1},{129,65},{193,129... | collective-permute-start | bytes 2949128 | tf_op jit(solution)/shard_map/ppermute | solution.py:67
  218.5 8.9 %copy-start.4 = (f32[128,2]{0,1:T(2,128)S(1)}, f32[128,2]{0,1:T(2,128)}, u32[]{:S(2)}) copy-start(f32[128,2]{0,1:T(2,128)} %param.15) | copy-start | bytes 3076
  218.5 42.6 %all-to-all-start.2 = ((bf16[32,40,1024]{2,1,0:T(8,128)(2,1)}), bf16[32,40,1024]{2,1,0:T(8,128)(2,1)S(1)}, u32[]{:S(2)}, u32[]{:S(2)}) async-start(bf16[32,40,1024]{2,1,0:T(8,128)(2,1)} %bitcast.65), calls=%async_computation.3 | async-start | bytes 5242880 | tf_op jit(solution)/shard_map/all_to_all | solution.py:80
Sparse Core Ops, SparseCore 0:
  9.8 83.8 all-gather.5
  103.2 44.9 reduce-scatter.1
  151.5 46.9 all-gather.3

commit v3 on v1

--- a/solution.py
+++ b/solution.py
@@ -28,29 +28,32 @@
     return (flat, place)
 
 
+CHUNKS = 2
+
+
 def body(master, moment_one, moment_two, saved_rows, saved_grads, slot_rows, routes, gates):
     n_hi = lax.axis_size("dy")
     n_lo = lax.axis_size("dz")
     experts = lax.axis_size("expert")
+    chunks = CHUNKS
 
     rows_here = saved_rows[0]
     grads_here = saved_grads[0]
     saved, d_model = grads_here.shape
     group_width = d_model // n_hi
+    own = group_width // n_lo
+    piece = own // chunks
     rows_group = lax.all_gather(rows_here, "dy", axis=0, tiled=True)
-    grads_group = lax.all_to_all(
-        grads_here.reshape(saved, n_hi, group_width).transpose(1, 0, 2),
-        "dy",
-        split_axis=0,
-        concat_axis=0,
-        tiled=True,
-    ).reshape(n_hi * saved, group_width)
-    partial = lax.dot_general(
-        grads_group, rows_group, (((0,), (0,)), ((), ())), preferred_element_type=jnp.float32
-    ).astype(jnp.bfloat16)
-    grad = lax.psum_scatter(partial, "dz", scatter_dimension=0, tiled=True).astype(jnp.float32)
-    master_new, m_new, v_new = adam_update(master[0], moment_one[0], moment_two[0], grad)
-    weights_shard = master_new.astype(jnp.bfloat16)
+    grads_sorted = grads_here.reshape(saved, n_hi, n_lo, chunks, piece).transpose(1, 3, 0, 2, 4)
+    grads_group = lax.all_to_all(grads_sorted, "dy", split_axis=0, concat_axis=0, tiled=True)
+    partials = []
+    for h in range(chunks):
+        cols = grads_group[:, h].reshape(n_hi * saved, n_lo * piece)
+        partials.append(
+            lax.dot_general(
+                cols, rows_group, (((0,), (0,)), ((), ())), preferred_element_type=jnp.float32
+            ).astype(jnp.bfloat16)
+        )
 
     tok_count, top_count, width = slot_rows.shape
     capacity = tok_count * top_count * 5 // (4 * experts)
@@ -63,29 +66,55 @@
         preferred_element_type=jnp.float32,
     ).astype(jnp.bfloat16).reshape(experts, capacity, width)
     received = lax.all_to_all(outgoing, "expert", split_axis=0, concat_axis=0, tiled=True)
-    slots_group = lax.all_gather(received, "dy", axis=0, tiled=True).reshape(-1, width)
-
-    weights_group = lax.all_gather(weights_shard, "dz", axis=0, tiled=True)
-    product = lax.dot_general(
-        slots_group, weights_group, (((1,), (1,)), ((), ())), preferred_element_type=jnp.float32
-    ).astype(jnp.bfloat16)
-    returned = lax.all_to_all(
-        product, ("dy", "expert"), split_axis=0, concat_axis=0, tiled=True
-    ).reshape(n_hi, experts * capacity, group_width)
+    received, partials = lax.optimization_barrier((received, partials))
+    me_hi = lax.axis_index("dy")
+    slots_group = jnp.zeros((n_hi,) + received.shape, received.dtype)
+    slots_group = lax.dynamic_update_slice(slots_group, received[None], (me_hi, 0, 0, 0))
+    for step in range(1, n_hi):
+        pairs = [(j, (j + step) % n_hi) for j in range(n_hi)]
+        arrived = lax.ppermute(received, "dy", pairs)
+        slots_group = lax.dynamic_update_slice(
+            slots_group, arrived[None], ((me_hi - step) % n_hi, 0, 0, 0)
+        )
+    slots_group = slots_group.reshape(-1, width)
 
     slot_pairs = slot_id.reshape(tok_count, top_count)
     combine = jnp.sum(
         (slot_pairs[:, :, None] == table[None, None, :]).astype(jnp.float32) * gates[:, :, None],
         axis=1,
     )
-    mixed = jnp.einsum(
-        "ts,hsf->thf",
-        combine,
-        returned.astype(jnp.float32),
-        precision=lax.Precision.HIGHEST,
-        preferred_element_type=jnp.float32,
-    )
-    mixed = mixed.reshape(tok_count, n_hi * group_width).astype(jnp.bfloat16)
+
+    masters, firsts, seconds, mixes = [], [], [], []
+    for h in range(chunks):
+        grad = lax.psum_scatter(partials[h], "dz", scatter_dimension=0, tiled=True)
+        rows = slice(h * piece, (h + 1) * piece)
+        master_new, m_new, v_new = adam_update(
+            master[0, rows], moment_one[0, rows], moment_two[0, rows], grad.astype(jnp.float32)
+        )
+        masters.append(master_new)
+        firsts.append(m_new)
+        seconds.append(v_new)
+        weights_piece = lax.all_gather(master_new.astype(jnp.bfloat16), "dz", axis=0, tiled=True)
+        product = lax.dot_general(
+            slots_group, weights_piece, (((1,), (1,)), ((), ())),
+            preferred_element_type=jnp.float32,
+        ).astype(jnp.bfloat16)
+        returned = lax.all_to_all(
+            product, ("dy", "expert"), split_axis=0, concat_axis=0, tiled=True
+        ).reshape(n_hi, experts * capacity, n_lo, piece)
+        mixes.append(
+            jnp.einsum(
+                "ts,hszr->thzr",
+                combine,
+                returned.astype(jnp.float32),
+                precision=lax.Precision.HIGHEST,
+                preferred_element_type=jnp.float32,
+            )
+        )
+    mixed = jnp.stack(mixes, axis=3).reshape(tok_count, d_model).astype(jnp.bfloat16)
+    master_new = jnp.concatenate(masters, axis=0)
+    m_new = jnp.concatenate(firsts, axis=0)
+    v_new = jnp.concatenate(seconds, axis=0)
     return (master_new[None], m_new[None], v_new[None], mixed)
 
 

time: 309 us -> 324 us (1.049)
  blocking collectives: 82.1 us -> 0 us
  starting transfers between devices: 8.39 us -> 41.9 us
  local copies, waits for them, and re-layouts: 9.6 us -> 35.6 us
  waiting for transfers between devices: 169 us -> 193 us
  matrix products: 21.4 us -> 31 us
    all_to_all x2 -> x0, blocking collectives: 82.1 us -> none  [the longest x1 63.1 us: body(): lax.all_to_all(grads_here.reshape(saved, n_hi, group_width).transpose(1,...]
    all_gather x2, waiting for transfers between devices: 96.9 us -> 15.7 us  [body(): lax.all_gather(master_new.astype(jnp.bfloat16), 'dz', axis=0, tiled=True)]
    reduce_scatter x1 -> x2, waiting for transfers between devices: 23.2 us -> 79.1 us  [body(): grad = lax.psum_scatter(partials[h], 'dz', scatter_dimension=0, tiled=True)]
    all_to_all x0 -> x2, waiting for transfers between devices: none -> 51.5 us  [the longest x1 51.5 us: body(): lax.all_to_all(grads_sorted, 'dy', split_axis=0, concat_axis=0, tiled=True)]
    ppermute x0 -> x3, waiting for transfers between devices: none -> 33.2 us  [body(): arrived = lax.ppermute(received, 'dy', pairs)]
    all_to_all x1 -> x2, waiting for transfers between devices: 33.7 us -> 9.63 us  [body(): lax.all_to_all(product, ('dy', 'expert'), split_axis=0, concat_axis=0, ti...]
    all_to_all x0 -> x2, starting transfers between devices: none -> 16.6 us  [the longest x1 11.5 us: body(): lax.all_to_all(outgoing, 'expert', split_axis=0, concat_axis=0, tiled=True)]
    reshape x0 -> x5, local copies, waits for them, and re-layouts: none -> 12.6 us  [the longest x4 12.4 us: body(): returned = lax.all_to_all(product, ('dy', 'expert'), split_axis=0, concat...]
  transfers between devices with their start and end apart: 5 -> 12, of which waited for: 5 -> 9; matrix products, arithmetic and copies ran while one was open for 4% -> 18% of each run, Pallas kernels for 0% -> 0%
where the time goes in v3:
time: 324 us; the launch traced here: 323 us
  waiting for transfers between devices  193 us (60%)
  starting transfers between devices  41.9 us (13%)
  local copies, waits for them, and re-layouts  35.6 us (11%)
  matrix products  31 us (10%)
  between operations  13.9 us (4%)
  other arithmetic  7.06 us (2%)
    reduce_scatter x2, waiting for transfers between devices, body(): grad = lax.psum_scatter(partials[h], 'dz', scatter_dimension=0, tiled=True)  79.1 us
    all_to_all x1, waiting for transfers between devices, body(): lax.all_to_all(grads_sorted, 'dy', split_axis=0, concat_axis=0, tiled=True)  51.5 us
    ppermute x3, waiting for transfers between devices, body(): arrived = lax.ppermute(received, 'dy', pairs)  33.2 us
    all_to_all x2, starting transfers between devices, body(): lax.all_to_all(product, ('dy', 'expert'), split_axis=0, concat_axis=0, ti...  20.2 us
    all_gather x2, waiting for transfers between devices, body(): lax.all_gather(master_new.astype(jnp.bfloat16), 'dz', axis=0, tiled=True)  15.7 us
    reshape x4, local copies, waits for them, and re-layouts, body(): returned = lax.all_to_all(product, ('dy', 'expert'), split_axis=0, concat...  12.4 us
    dot_general x2, matrix products, body(): lax.dot_general(cols, rows_group, (((0,), (0,)), ((), ())), preferred_ele...  12.1 us
    dot_general x2, matrix products, body(): lax.dot_general(slots_group, weights_piece, (((1,), (1,)), ((), ())), pre...  11.9 us
  transfers between devices with their start and end apart: 12, of which 9 were waited for; matrix products, arithmetic and copies ran while one was open for 18% of the time, Pallas kernels for 0%

profile of v3, /device:TPU:1, one launch (start us, length us, event | category | flops | bytes accessed | tf_op | source)
XLA Modules:
  0.0 323.0 jit_solution(5386313768353381033)
XLA Ops:
  7.9 4.7 %copy.40 = bf16[1,384,4096]{1,2,0:T(8,128)(2,1)} copy(bf16[1,384,4096]{2,1,0:T(8,128)(2,1)} %param.12) | data formatting | bytes 6291456 | tf_op args[4]
  12.6 5.1 %all-to-all-start.1 = ((bf16[4,2,384,8,64]{2,4,1,3,0:T(8,128)(2,1)}), bf16[4,2,384,8,64]{2,4,1,3,0:T(8,128)(2,1)S(1)}, u32[]{:S(2)}, u32[]{:S(2)}) async-start(bf16[4,2,384,8,64]{2,4,1,3,0:T(8,128)(2,1)} %bitcast.90), calls=%async_computation.1 | async-start | bytes 6291456 | tf_op jit(solution)/shard_map/all_to_all | solution.py:48
  18.2 3.0 reshape.76
  24.6 51.5 %all-to-all-done.1 = bf16[4,2,384,8,64]{2,4,1,3,0:T(8,128)(2,1)S(1)} async-done(((bf16[4,2,384,8,64]{2,4,1,3,0:T(8,128)(2,1)}), bf16[4,2,384,8,64]{2,4,1,3,0:T(8,128)(2,1)S(1)}, u32[]{:S(2)}, u32[]{:S(2)}) %all-to-all-start.1) | async-done | bytes 3145760 | tf_op jit(solution)/shard_map/all_to_all | solution.py:48
  76.1 11.5 %all-to-all-start = ((bf16[8,40,1536]{2,1,0:T(8,128)(2,1)}), bf16[8,40,1536]{2,1,0:T(8,128)(2,1)}, u32[]{:S(2)}, u32[]{:S(2)}) async-start(bf16[8,40,1536]{2,1,0:T(8,128)(2,1)} %bitcast.98), calls=%async_computation | async-start | bytes 1966080 | tf_op jit(solution)/shard_map/all_to_all | solution.py:68
  90.9 2.8 all-gather.9.cloned.1.call-done
  93.7 6.0 %fusion.4 = bf16[512,1536]{1,0:T(8,128)(2,1)} fusion(bf16[1536,512]{0,1:T(8,128)(2,1)S(1)} %bitcast.99, bf16[1,1536,1536]{2,1,0:T(8,128)(2,1)} %all-gather.9.cloned.1.call-done), kind=kOutput, calls=%fused_computation.4 | convolution fusion | flops 2416705536 | bytes 7864320 | tf_op jit(solution)/shard_map/dot_general | solution.py:53
  99.7 6.1 %fusion.7 = bf16[512,1536]{1,0:T(8,128)(2,1)} fusion(bf16[1536,512]{0,1:T(8,128)(2,1)S(1)} %bitcast.100, bf16[1,1536,1536]{2,1,0:T(8,128)(2,1)} %all-gather.9.cloned.1.call-done), kind=kOutput, calls=%fused_computation.5 | convolution fusion | flops 2416705536 | bytes 7864320 | tf_op jit(solution)/shard_map/dot_general | solution.py:53
  106.6 37.2 %reduce-scatter.3.cloned.1.call-done = bf16[64,1536]{1,0:T(8,128)(2,1)} async-done(((bf16[512,1536]{1,0:T(8,128)(2,1)}), bf16[64,1536]{1,0:T(8,128)(2,1)}) %reduce-scatter.3.cloned.1.call-update) | async-done | bytes 196624 | tf_op jit(solution)/shard_map/reduce_scatter | solution.py:89
  143.9 41.9 %reduce-scatter.5.cloned.1.call-done = bf16[64,1536]{1,0:T(8,128)(2,1)} async-done(((bf16[512,1536]{1,0:T(8,128)(2,1)}), bf16[64,1536]{1,0:T(8,128)(2,1)}) %reduce-scatter.5.cloned.1.call-update) | async-done | bytes 196624 | tf_op jit(solution)/shard_map/reduce_scatter | solution.py:89
  185.7 2.8 fusion.18
  198.0 10.9 %collective-permute-done = bf16[8,40,1536]{2,1,0:T(8,128)(2,1)S(1)} collective-permute-done((bf16[8,40,1536]{2,1,0:T(8,128)(2,1)}, bf16[8,40,1536]{2,1,0:T(8,128)(2,1)S(1)}, u32[]{:S(2)}, u32[]{:S(2)}) %collective-permute-start) | collective-permute-done | bytes 983072 | tf_op jit(solution)/shard_map/ppermute | solution.py:75
  209.9 21.1 %collective-permute-done.1 = bf16[8,40,1536]{2,1,0:T(8,128)(2,1)} collective-permute-done((bf16[8,40,1536]{2,1,0:T(8,128)(2,1)}, bf16[8,40,1536]{2,1,0:T(8,128)(2,1)}, u32[]{:S(2)}, u32[]{:S(2)}) %collective-permute-start.1) | collective-permute-done | bytes 983072 | tf_op jit(solution)/shard_map/ppermute | solution.py:75
  236.8 6.0 %convolution_convert_fusion = bf16[1280,512]{1,0:T(8,128)(2,1)} fusion(bf16[1280,1536]{1,0:T(8,128)(2,1)} %bitcast.19, bf16[512,1536]{1,0:T(8,128)(2,1)} %all-gather.7.cloned.1.call-done), kind=kOutput, calls=%fused_computation.6 | convolution fusion | flops 2013921280 | bytes 6815744 | tf_op jit(solution)/shard_map/dot_general | solution.py:98
  242.8 8.8 %all-to-all-start.3 = ((bf16[32,40,512]{2,1,0:T(8,128)(2,1)}), bf16[32,40,512]{2,1,0:T(8,128)(2,1)S(1)}, u32[]{:S(2)}, u32[]{:S(2)}) async-start(bf16[32,40,512]{2,1,0:T(8,128)(2,1)} %bitcast.102), calls=%async_computation.5 | async-start | bytes 2621440 | tf_op jit(solution)/shard_map/all_to_all | solution.py:102
  251.6 15.7 %all-gather.5.cloned.1.call-done = bf16[512,1536]{1,0:T(8,128)(2,1)} async-done(((bf16[64,1536]{1,0:T(8,128)(2,1)}), bf16[512,1536]{1,0:T(8,128)(2,1)}) %all-gather.5.cloned.1.call-update) | async-done | bytes 1572880 | tf_op jit(solution)/shard_map/all_gather | solution.py:97
  267.3 5.9 %convolution_convert_fusion.1 = bf16[1280,512]{1,0:T(8,128)(2,1)} fusion(bf16[1280,1536]{1,0:T(8,128)(2,1)} %bitcast.19, bf16[512,1536]{1,0:T(8,128)(2,1)} %all-gather.5.cloned.1.call-done), kind=kOutput, calls=%fused_computation.7 | convolution fusion | flops 2013921280 | bytes 6815744 | tf_op jit(solution)/shard_map/dot_general | solution.py:98
  273.2 11.4 %all-to-all-start.2 = ((bf16[32,40,512]{2,1,0:T(8,128)(2,1)}), bf16[32,40,512]{2,1,0:T(8,128)(2,1)}, u32[]{:S(2)}, u32[]{:S(2)}) async-start(bf16[32,40,512]{2,1,0:T(8,128)(2,1)} %bitcast.101), calls=%async_computation.4 | async-start | bytes 2621440 | tf_op jit(solution)/shard_map/all_to_all | solution.py:102
  288.1 3.1 reshape.80
  291.2 3.1 copy.45
  294.4 9.6 %all-to-all-done.2 = bf16[32,40,512]{2,1,0:T(8,128)(2,1)} async-done(((bf16[32,40,512]{2,1,0:T(8,128)(2,1)}), bf16[32,40,512]{2,1,0:T(8,128)(2,1)}, u32[]{:S(2)}, u32[]{:S(2)}) %all-to-all-start.2) | async-done | bytes 1310752 | tf_op jit(solution)/shard_map/all_to_all | solution.py:102
  304.0 3.1 reshape.79
  307.1 3.1 copy.44
  310.2 3.0 fusion.26
  (59 shorter events, 31.5 us)
Async XLA Ops:
  7.2 86.6 %all-gather.9.cloned.1.call-start = ((), (), s32[]{:S(2)}) async-start(), calls=%async_computation.10 | async-start | bytes 5898240 | tf_op jit(solution)/shard_map/all_gather | solution.py:46
  12.6 5.1 %copy-start.3 = (s32[128,2]{0,1:T(2,128)S(1)}, s32[128,2]{0,1:T(2,128)}, u32[]{:S(2)}) copy-start(s32[128,2]{0,1:T(2,128)} %param.14) | copy-start | bytes 3076
  12.6 63.4 %all-to-all-start.1 = ((bf16[4,2,384,8,64]{2,4,1,3,0:T(8,128)(2,1)}), bf16[4,2,384,8,64]{2,4,1,3,0:T(8,128)(2,1)S(1)}, u32[]{:S(2)}, u32[]{:S(2)}) async-start(bf16[4,2,384,8,64]{2,4,1,3,0:T(8,128)(2,1)} %bitcast.90), calls=%async_computation.1 | async-start | bytes 6291456 | tf_op jit(solution)/shard_map/all_to_all | solution.py:48
  76.1 29.7 %all-to-all-start = ((bf16[8,40,1536]{2,1,0:T(8,128)(2,1)}), bf16[8,40,1536]{2,1,0:T(8,128)(2,1)}, u32[]{:S(2)}, u32[]{:S(2)}) async-start(bf16[8,40,1536]{2,1,0:T(8,128)(2,1)} %bitcast.98), calls=%async_computation | async-start | bytes 1966080 | tf_op jit(solution)/shard_map/all_to_all | solution.py:68
  87.6 56.3 %reduce-scatter.3.cloned.1.call-start = ((), (), s32[]{:S(2)}) async-start(), calls=%async_computation.6 | async-start | bytes 1769472 | tf_op jit(solution)/shard_map/reduce_scatter | solution.py:89
  105.8 79.9 %copy-start.2 = (f32[1,128,1536]{2,1,0:T(8,128)S(1)}, f32[1,128,1536]{2,1,0:T(8,128)}, u32[]{:S(2)}) copy-start(f32[1,128,1536]{2,1,0:T(8,128)} %param.8) | copy-start | bytes 2359300
  105.8 79.9 %reduce-scatter.5.cloned.1.call-start = ((), (), s32[]{:S(2)}) async-start(), calls=%async_computation.7 | async-start | bytes 1769472 | tf_op jit(solution)/shard_map/reduce_scatter | solution.py:89
  106.6 130.2 %all-gather.7.cloned.1.call-start = ((), (), s32[]{:S(2)}) async-start(), calls=%async_computation.9 | async-start | bytes 1769472 | tf_op jit(solution)/shard_map/all_gather | solution.py:97
  188.5 78.8 %all-gather.5.cloned.1.call-start = ((), (), s32[]{:S(2)}) async-start(), calls=%async_computation.8 | async-start | bytes 1769472 | tf_op jit(solution)/shard_map/all_gather | solution.py:97
  188.6 20.3 %collective-permute-start = (bf16[8,40,1536]{2,1,0:T(8,128)(2,1)}, bf16[8,40,1536]{2,1,0:T(8,128)(2,1)S(1)}, u32[]{:S(2)}, u32[]{:S(2)}) collective-permute-start(bf16[8,40,1536]{2,1,0:T(8,128)(2,1)} %all-to-all-done), channel_id=1, source_target_pairs={{0,64},{64,128},{128,192},{192,0},{1,65},{65,129},{129,193},{193,1... | collective-permute-start | bytes 2949128 | tf_op jit(solution)/shard_map/ppermute | solution.py:75
  189.8 41.2 %collective-permute-start.1 = (bf16[8,40,1536]{2,1,0:T(8,128)(2,1)}, bf16[8,40,1536]{2,1,0:T(8,128)(2,1)}, u32[]{:S(2)}, u32[]{:S(2)}) collective-permute-start(bf16[8,40,1536]{2,1,0:T(8,128)(2,1)} %all-to-all-done), channel_id=1, source_target_pairs={{0,128},{64,192},{128,0},{192,64},{1,129},{65,193},{129,1},{193,65... | collective-permute-start | bytes 2949128 | tf_op jit(solution)/shard_map/ppermute | solution.py:75
  192.3 42.2 %collective-permute-start.2 = (bf16[8,40,1536]{2,1,0:T(8,128)(2,1)}, bf16[8,40,1536]{2,1,0:T(8,128)(2,1)}, u32[]{:S(2)}, u32[]{:S(2)}) collective-permute-start(bf16[8,40,1536]{2,1,0:T(8,128)(2,1)} %all-to-all-done), channel_id=1, source_target_pairs={{0,192},{64,0},{128,64},{192,128},{1,193},{65,1},{129,65},{193,129... | collective-permute-start | bytes 2949128 | tf_op jit(solution)/shard_map/ppermute | solution.py:75
  242.8 30.5 %all-to-all-start.3 = ((bf16[32,40,512]{2,1,0:T(8,128)(2,1)}), bf16[32,40,512]{2,1,0:T(8,128)(2,1)S(1)}, u32[]{:S(2)}, u32[]{:S(2)}) async-start(bf16[32,40,512]{2,1,0:T(8,128)(2,1)} %bitcast.102), calls=%async_computation.5 | async-start | bytes 2621440 | tf_op jit(solution)/shard_map/all_to_all | solution.py:102
  273.2 11.6 %copy-start.4 = (f32[128,2]{0,1:T(2,128)S(1)}, f32[128,2]{0,1:T(2,128)}, u32[]{:S(2)}) copy-start(f32[128,2]{0,1:T(2,128)} %param.15) | copy-start | bytes 3076
  273.2 13.6 %copy-start.1 = (bf16[32,40,512]{2,1,0:T(8,128)(2,1)}, bf16[32,40,512]{2,1,0:T(8,128)(2,1)S(1)}, u32[]{:S(2)}) copy-start(bf16[32,40,512]{2,1,0:T(8,128)(2,1)S(1)} %all-to-all-done.3) | copy-start | bytes 3932164
  273.2 30.8 %all-to-all-start.2 = ((bf16[32,40,512]{2,1,0:T(8,128)(2,1)}), bf16[32,40,512]{2,1,0:T(8,128)(2,1)}, u32[]{:S(2)}, u32[]{:S(2)}) async-start(bf16[32,40,512]{2,1,0:T(8,128)(2,1)} %bitcast.101), calls=%async_computation.4 | async-start | bytes 2621440 | tf_op jit(solution)/shard_map/all_to_all | solution.py:102
  310.2 3.0 copy-start
Sparse Core Ops, SparseCore 0:
  9.8 83.9 all-gather.8
  106.0 37.8 reduce-scatter.2
  146.4 39.2 reduce-scatter.4
  188.7 37.8 all-gather.6
  228.7 38.5 all-gather.4

commit v4 on v1

--- a/solution.py
+++ b/solution.py
@@ -29,28 +29,27 @@
 
 
 def body(master, moment_one, moment_two, saved_rows, saved_grads, slot_rows, routes, gates):
-    n_hi = lax.axis_size("dy")
-    n_lo = lax.axis_size("dz")
+    ny_hi, ny_lo = lax.axis_size("yh"), lax.axis_size("yl")
+    nz_hi, nz_lo = lax.axis_size("zh"), lax.axis_size("zl")
     experts = lax.axis_size("expert")
+    near = ("yl", "zl")
+    far = ("yh", "zh")
+    n_near = ny_lo * nz_lo
 
     rows_here = saved_rows[0]
     grads_here = saved_grads[0]
     saved, d_model = grads_here.shape
-    group_width = d_model // n_hi
-    rows_group = lax.all_gather(rows_here, "dy", axis=0, tiled=True)
+    own = d_model // (ny_hi * ny_lo * nz_hi * nz_lo)
+    rows_group = lax.all_gather(rows_here, near, axis=0, tiled=True)
+    grads_sorted = grads_here.reshape(saved, ny_hi, ny_lo, nz_hi, nz_lo, own).transpose(
+        2, 4, 0, 1, 3, 5
+    ).reshape(n_near, saved, ny_hi * nz_hi * own)
     grads_group = lax.all_to_all(
-        grads_here.reshape(saved, n_hi, group_width).transpose(1, 0, 2),
-        "dy",
-        split_axis=0,
-        concat_axis=0,
-        tiled=True,
-    ).reshape(n_hi * saved, group_width)
+        grads_sorted, near, split_axis=0, concat_axis=0, tiled=True
+    ).reshape(n_near * saved, ny_hi * nz_hi * own)
     partial = lax.dot_general(
         grads_group, rows_group, (((0,), (0,)), ((), ())), preferred_element_type=jnp.float32
     ).astype(jnp.bfloat16)
-    grad = lax.psum_scatter(partial, "dz", scatter_dimension=0, tiled=True).astype(jnp.float32)
-    master_new, m_new, v_new = adam_update(master[0], moment_one[0], moment_two[0], grad)
-    weights_shard = master_new.astype(jnp.bfloat16)
 
     tok_count, top_count, width = slot_rows.shape
     capacity = tok_count * top_count * 5 // (4 * experts)
@@ -63,15 +62,29 @@
         preferred_element_type=jnp.float32,
     ).astype(jnp.bfloat16).reshape(experts, capacity, width)
     received = lax.all_to_all(outgoing, "expert", split_axis=0, concat_axis=0, tiled=True)
-    slots_group = lax.all_gather(received, "dy", axis=0, tiled=True).reshape(-1, width)
+    received, partial = lax.optimization_barrier((received, partial))
+    me_near = lax.axis_index("yl") * nz_lo + lax.axis_index("zl")
+    slots_group = jnp.zeros((n_near,) + received.shape, received.dtype)
+    slots_group = lax.dynamic_update_slice(slots_group, received[None], (me_near, 0, 0, 0))
+    for flip in range(1, n_near):
+        pairs = [(j, j ^ flip) for j in range(n_near)]
+        arrived = lax.ppermute(received, near, pairs)
+        slots_group = lax.dynamic_update_slice(
+            slots_group, arrived[None], (me_near ^ flip, 0, 0, 0)
+        )
+    slots_group = slots_group.reshape(-1, width)
 
-    weights_group = lax.all_gather(weights_shard, "dz", axis=0, tiled=True)
+    grad = lax.psum_scatter(partial, far, scatter_dimension=0, tiled=True).astype(jnp.float32)
+    master_new, m_new, v_new = adam_update(master[0], moment_one[0], moment_two[0], grad)
+    weights_shard = master_new.astype(jnp.bfloat16)
+
+    weights_group = lax.all_gather(weights_shard, far, axis=0, tiled=True)
     product = lax.dot_general(
         slots_group, weights_group, (((1,), (1,)), ((), ())), preferred_element_type=jnp.float32
     ).astype(jnp.bfloat16)
     returned = lax.all_to_all(
-        product, ("dy", "expert"), split_axis=0, concat_axis=0, tiled=True
-    ).reshape(n_hi, experts * capacity, group_width)
+        product, near + ("expert",), split_axis=0, concat_axis=0, tiled=True
+    ).reshape(ny_lo, nz_lo, experts * capacity, ny_hi, nz_hi, own)
 
     slot_pairs = slot_id.reshape(tok_count, top_count)
     combine = jnp.sum(
@@ -79,13 +92,13 @@
         axis=1,
     )
     mixed = jnp.einsum(
-        "ts,hsf->thf",
+        "ts,abshzr->thazbr",
         combine,
         returned.astype(jnp.float32),
         precision=lax.Precision.HIGHEST,
         preferred_element_type=jnp.float32,
     )
-    mixed = mixed.reshape(tok_count, n_hi * group_width).astype(jnp.bfloat16)
+    mixed = mixed.reshape(tok_count, d_model).astype(jnp.bfloat16)
     return (master_new[None], m_new[None], v_new[None], mixed)
 
 
@@ -94,17 +107,21 @@
     dp_size, ex_size = devices.shape
     column = devices[:, 0]
     try:
-        n_hi = len({d.coords[1] for d in column})
+        n_y = len({d.coords[1] for d in column})
     except Exception:
-        n_hi = 1
-    if n_hi < 1 or dp_size % n_hi:
-        n_hi = 1
-    return Mesh(devices.reshape(n_hi, dp_size // n_hi, ex_size), ("dy", "dz", "expert"))
+        n_y = 1
+    if n_y < 1 or dp_size % n_y:
+        n_y = 1
+    n_z = dp_size // n_y
+    y_lo = 2 if n_y % 2 == 0 else 1
+    z_lo = 2 if n_z % 2 == 0 else 1
+    shape = (n_y // y_lo, y_lo, n_z // z_lo, z_lo, ex_size)
+    return Mesh(devices.reshape(shape), ("yh", "yl", "zh", "zl", "expert"))
 
 
 def solution(mesh):
     inner = split_mesh(mesh)
-    dp = ("dy", "dz")
+    dp = ("yh", "yl", "zh", "zl")
     placed = (
         P("expert", dp, None),
         P("expert", dp, None),

time: 309 us -> 396 us (1.28)
  waiting for transfers between devices: 169 us -> 302 us
  blocking collectives: 82.1 us -> 0 us
  starting transfers between devices: 8.39 us -> 25.5 us
  local copies, waits for them, and re-layouts: 9.6 us -> 24.6 us
  matrix products: 21.4 us -> 25.9 us
    all_to_all x2 -> x0, blocking collectives: 82.1 us -> none  [the longest x1 63.1 us: body(): lax.all_to_all(grads_here.reshape(saved, n_hi, group_width).transpose(1,...]
    reduce_scatter x1, waiting for transfers between devices: 23.2 us -> 96.5 us  [body(): lax.psum_scatter(partial, far, scatter_dimension=0, tiled=True)]
    ppermute x0 -> x3, waiting for transfers between devices: none -> 61.6 us  [body(): arrived = lax.ppermute(received, near, pairs)]
    all_gather x3 -> x2, waiting for transfers between devices: 112 us -> 58.2 us  [the longest x1 40.7 us: body(): rows_group = lax.all_gather(rows_here, near, axis=0, tiled=True)]
    all_to_all x1 -> x3, waiting for transfers between devices: 33.7 us -> 84.6 us  [the longest x1 50.1 us: body(): lax.all_to_all(grads_sorted, near, split_axis=0, concat_axis=0, tiled=True)]
    all_to_all x1 -> x3, starting transfers between devices: 8.23 us -> 22.4 us  [the longest x1 12.1 us: body(): lax.all_to_all(outgoing, 'expert', split_axis=0, concat_axis=0, tiled=True)]
    dynamic_update_slice x0 -> x4, local copies, waits for them, and re-layouts: none -> 5.32 us  [the longest x3 3.1 us: body(): lax.dynamic_update_slice(slots_group, arrived[None], (me_near ^ flip, 0,...]
  transfers between devices with their start and end apart: 5 -> 9, of which waited for: 5 -> 7; matrix products, arithmetic and copies ran while one was open for 4% -> 8% of each run, Pallas kernels for 0% -> 0%
where the time goes in v4:
time: 396 us; the launch traced here: 395 us
  waiting for transfers between devices  302 us (76%)
  matrix products  25.9 us (7%)
  starting transfers between devices  25.5 us (6%)
  local copies, waits for them, and re-layouts  24.6 us (6%)
  between operations  13.8 us (3%)
    reduce_scatter x1, waiting for transfers between devices, body(): lax.psum_scatter(partial, far, scatter_dimension=0, tiled=True)  96.5 us
    ppermute x3, waiting for transfers between devices, body(): arrived = lax.ppermute(received, near, pairs)  61.6 us
    all_to_all x1, waiting for transfers between devices, body(): lax.all_to_all(grads_sorted, near, split_axis=0, concat_axis=0, tiled=True)  50.1 us
    all_gather x1, waiting for transfers between devices, body(): rows_group = lax.all_gather(rows_here, near, axis=0, tiled=True)  40.7 us
    all_to_all x1, waiting for transfers between devices, body(): lax.all_to_all(product, near + ('expert',), split_axis=0, concat_axis=0,...  34.5 us
    all_gather x1, waiting for transfers between devices, body(): weights_group = lax.all_gather(weights_shard, far, axis=0, tiled=True)  17.5 us
    all_to_all x1, starting transfers between devices, body(): lax.all_to_all(outgoing, 'expert', split_axis=0, concat_axis=0, tiled=True)  12.1 us
    dot_general x1, matrix products, body(): lax.dot_general(grads_group, rows_group, (((0,), (0,)), ((), ())), prefer...  9.26 us
  transfers between devices with their start and end apart: 9, of which 7 were waited for; matrix products, arithmetic and copies ran while one was open for 8% of the time, Pallas kernels for 0%

profile of v4, /device:TPU:1, one launch (start us, length us, event | category | flops | bytes accessed | tf_op | source)
XLA Modules:
  0.0 395.2 jit_solution(5109721794799932367)
XLA Ops:
  7.9 3.4 copy.46
  11.3 2.0 copy.47
  13.3 4.9 %all-to-all-start.1 = ((bf16[4,384,1024]{1,2,0:T(8,128)(2,1)}), bf16[4,384,1024]{1,2,0:T(8,128)(2,1)S(1)}, u32[]{:S(2)}, u32[]{:S(2)}) async-start(bf16[4,384,1024]{1,2,0:T(8,128)(2,1)} %bitcast.63), calls=%async_computation.1 | async-start | bytes 6291456 | tf_op jit(solution)/shard_map/all_to_all | solution.py:47
  18.6 3.0 reshape.72
  22.5 2.5 convolution_convert_fusion.1
  25.0 50.1 %all-to-all-done.1 = bf16[4,384,1024]{1,2,0:T(8,128)(2,1)S(1)} async-done(((bf16[4,384,1024]{1,2,0:T(8,128)(2,1)}), bf16[4,384,1024]{1,2,0:T(8,128)(2,1)S(1)}, u32[]{:S(2)}, u32[]{:S(2)}) %all-to-all-start.1) | async-done | bytes 3145760 | tf_op jit(solution)/shard_map/all_to_all | solution.py:47
  75.1 12.1 %all-to-all-start = ((bf16[8,40,1536]{2,1,0:T(8,128)(2,1)}), bf16[8,40,1536]{2,1,0:T(8,128)(2,1)}, u32[]{:S(2)}, u32[]{:S(2)}) async-start(bf16[8,40,1536]{2,1,0:T(8,128)(2,1)} %bitcast.66), calls=%async_computation | async-start | bytes 1966080 | tf_op jit(solution)/shard_map/all_to_all | solution.py:64
  87.2 3.0 copy.48
  90.2 40.7 %all-gather.6.cloned.1.call-done = bf16[1,1536,1536]{2,1,0:T(8,128)(2,1)} async-done(((bf16[1,384,1536]{2,1,0:T(8,128)(2,1)}), bf16[1,1536,1536]{2,1,0:T(8,128)(2,1)}) %all-gather.6.cloned.1.call-update) | async-done | bytes 4718608 | tf_op jit(solution)/shard_map/all_gather | solution.py:43
  130.9 9.3 %fusion.2 = bf16[1024,1536]{1,0:T(8,128)(2,1)} fusion(bf16[1536,1024]{1,0:T(8,128)(2,1)} %bitcast.67, bf16[1,1536,1536]{2,1,0:T(8,128)(2,1)} %all-gather.6.cloned.1.call-done), kind=kOutput, calls=%fused_computation.2 | convolution fusion | flops 4833411072 | bytes 11010048 | tf_op jit(solution)/shard_map/dot_general | solution.py:50
  140.2 96.5 %reduce-scatter.2.cloned.1.call-done = bf16[128,1536]{1,0:T(8,128)(2,1)} async-done(((bf16[1024,1536]{1,0:T(8,128)(2,1)}), bf16[128,1536]{1,0:T(8,128)(2,1)}) %reduce-scatter.2.cloned.1.call-update) | async-done | bytes 393232 | tf_op jit(solution)/shard_map/reduce_scatter | solution.py:77
  236.7 3.1 fusion.22
  239.8 1.7 collective-permute-start
  242.8 2.2 broadcast_in_dim.32
  245.0 2.2 bitcast_dynamic-update-slice_fusion.3
  247.3 25.5 %collective-permute-done = bf16[8,40,1536]{2,1,0:T(8,128)(2,1)S(1)} collective-permute-done((bf16[8,40,1536]{2,1,0:T(8,128)(2,1)}, bf16[8,40,1536]{2,1,0:T(8,128)(2,1)S(1)}, u32[]{:S(2)}, u32[]{:S(2)}) %collective-permute-start) | collective-permute-done | bytes 983072 | tf_op jit(solution)/shard_map/ppermute | solution.py:71
  274.9 36.1 %collective-permute-done.2 = bf16[8,40,1536]{2,1,0:T(8,128)(2,1)S(1)} collective-permute-done((bf16[8,40,1536]{2,1,0:T(8,128)(2,1)}, bf16[8,40,1536]{2,1,0:T(8,128)(2,1)S(1)}, u32[]{:S(2)}, u32[]{:S(2)}) %collective-permute-start.2) | collective-permute-done | bytes 983072 | tf_op jit(solution)/shard_map/ppermute | solution.py:71
  312.0 17.5 %all-gather.4.cloned.1.call-done = bf16[1024,1536]{1,0:T(8,128)(2,1)} async-done(((bf16[128,1536]{1,0:T(8,128)(2,1)}), bf16[1024,1536]{1,0:T(8,128)(2,1)}) %all-gather.4.cloned.1.call-update) | async-done | bytes 3145744 | tf_op jit(solution)/shard_map/all_gather | solution.py:81
  329.5 8.9 %convolution_convert_fusion = bf16[1280,1024]{1,0:T(8,128)(2,1)} fusion(bf16[1280,1536]{1,0:T(8,128)(2,1)} %bitcast.18, bf16[1024,1536]{1,0:T(8,128)(2,1)} %all-gather.4.cloned.1.call-done), kind=kOutput, calls=%fused_computation.3 | convolution fusion | flops 4027842560 | bytes 9699328 | tf_op jit(solution)/shard_map/dot_general | solution.py:82
  338.4 5.5 %all-to-all-start.2 = ((bf16[32,40,1024]{2,1,0:T(8,128)(2,1)}), bf16[32,40,1024]{2,1,0:T(8,128)(2,1)S(1)}, u32[]{:S(2)}, u32[]{:S(2)}) async-start(bf16[32,40,1024]{2,1,0:T(8,128)(2,1)} %bitcast.68), calls=%async_computation.3 | async-start | bytes 5242880 | tf_op jit(solution)/shard_map/all_to_all | solution.py:85
  344.2 34.5 %all-to-all-done.2 = bf16[32,40,1024]{2,1,0:T(8,128)(2,1)S(1)} async-done(((bf16[32,40,1024]{2,1,0:T(8,128)(2,1)}), bf16[32,40,1024]{2,1,0:T(8,128)(2,1)S(1)}, u32[]{:S(2)}, u32[]{:S(2)}) %all-to-all-start.2) | async-done | bytes 2621472 | tf_op jit(solution)/shard_map/all_to_all | solution.py:85
  378.6 3.5 reshape.77
  382.1 5.2 %fusion.10 = bf16[128,2,2,4,2,128]{0,5,3,1,4,2:T(8,128)(2,1)S(1)} fusion(bf16[2,2,320,2,4,128]{5,4,3,2,1,0:T(4,128)(2,1)} %reshape.77, f32[128,320]{0,1:T(8,128)S(1)} %select_reduce_fusion), kind=kOutput, calls=%fused_computation.8 | convolution fusion | flops 2013790208 | bytes 3833856 | tf_op jit(solution)/shard_map/ts,abshzr->thazbr/dot_general | solution.py:94
  387.4 1.3 copy.52
  (38 shorter events, 6.9 us)
Async XLA Ops:
  7.2 123.7 %all-gather.6.cloned.1.call-start = ((), (), s32[]{:S(2)}) async-start(), calls=%async_computation.6 | async-start | bytes 5898240 | tf_op jit(solution)/shard_map/all_gather | solution.py:43
  13.3 4.9 %copy-start.3 = (s32[128,2]{0,1:T(2,128)S(1)}, s32[128,2]{0,1:T(2,128)}, u32[]{:S(2)}) copy-start(s32[128,2]{0,1:T(2,128)} %param.14) | copy-start | bytes 3076
  13.3 61.8 %all-to-all-start.1 = ((bf16[4,384,1024]{1,2,0:T(8,128)(2,1)}), bf16[4,384,1024]{1,2,0:T(8,128)(2,1)S(1)}, u32[]{:S(2)}, u32[]{:S(2)}) async-start(bf16[4,384,1024]{1,2,0:T(8,128)(2,1)} %bitcast.63), calls=%async_computation.1 | async-start | bytes 6291456 | tf_op jit(solution)/shard_map/all_to_all | solution.py:47
  75.1 65.0 %all-to-all-start = ((bf16[8,40,1536]{2,1,0:T(8,128)(2,1)}), bf16[8,40,1536]{2,1,0:T(8,128)(2,1)}, u32[]{:S(2)}, u32[]{:S(2)}) async-start(bf16[8,40,1536]{2,1,0:T(8,128)(2,1)} %bitcast.66), calls=%async_computation | async-start | bytes 1966080 | tf_op jit(solution)/shard_map/all_to_all | solution.py:64
  87.2 149.5 %reduce-scatter.2.cloned.1.call-start = ((), (), s32[]{:S(2)}) async-start(), calls=%async_computation.4 | async-start | bytes 3538944 | tf_op jit(solution)/shard_map/reduce_scatter | solution.py:77
  140.2 96.6 %copy-start = (f32[1,128,1536]{2,1,0:T(8,128)S(1)}, f32[1,128,1536]{2,1,0:T(8,128)}, u32[]{:S(2)}) copy-start(f32[1,128,1536]{2,1,0:T(8,128)} %param.10) | copy-start | bytes 2359300
  140.2 96.6 %copy-start.1 = (f32[1,128,1536]{2,1,0:T(8,128)S(1)}, f32[1,128,1536]{2,1,0:T(8,128)}, u32[]{:S(2)}) copy-start(f32[1,128,1536]{2,1,0:T(8,128)} %param.9) | copy-start | bytes 2359300
  140.2 96.6 %copy-start.2 = (f32[1,128,1536]{2,1,0:T(8,128)S(1)}, f32[1,128,1536]{2,1,0:T(8,128)}, u32[]{:S(2)}) copy-start(f32[1,128,1536]{2,1,0:T(8,128)} %param.8) | copy-start | bytes 2359300
  140.2 189.3 %all-gather.4.cloned.1.call-start = ((), (), s32[]{:S(2)}) async-start(), calls=%async_computation.5 | async-start | bytes 3538944 | tf_op jit(solution)/shard_map/all_gather | solution.py:81
  239.8 32.9 %collective-permute-start = (bf16[8,40,1536]{2,1,0:T(8,128)(2,1)}, bf16[8,40,1536]{2,1,0:T(8,128)(2,1)S(1)}, u32[]{:S(2)}, u32[]{:S(2)}) collective-permute-start(bf16[8,40,1536]{2,1,0:T(8,128)(2,1)} %all-to-all-done), channel_id=1, source_target_pairs={{0,8},{8,0},{64,72},{72,64},{1,9},{9,1},{65,73},{73,65},{2,10},{10... | collective-permute-start | bytes 2949128 | tf_op jit(solution)/shard_map/ppermute | solution.py:71
  241.5 32.3 %collective-permute-start.1 = (bf16[8,40,1536]{2,1,0:T(8,128)(2,1)}, bf16[8,40,1536]{2,1,0:T(8,128)(2,1)S(1)}, u32[]{:S(2)}, u32[]{:S(2)}) collective-permute-start(bf16[8,40,1536]{2,1,0:T(8,128)(2,1)} %all-to-all-done), channel_id=1, source_target_pairs={{0,64},{8,72},{64,0},{72,8},{1,65},{9,73},{65,1},{73,9},{2,66},{10... | collective-permute-start | bytes 2949128 | tf_op jit(solution)/shard_map/ppermute | solution.py:71
  242.1 68.9 %collective-permute-start.2 = (bf16[8,40,1536]{2,1,0:T(8,128)(2,1)}, bf16[8,40,1536]{2,1,0:T(8,128)(2,1)S(1)}, u32[]{:S(2)}, u32[]{:S(2)}) collective-permute-start(bf16[8,40,1536]{2,1,0:T(8,128)(2,1)} %all-to-all-done), channel_id=1, source_target_pairs={{0,72},{8,64},{64,8},{72,0},{1,73},{9,65},{65,9},{73,1},{2,74},{10... | collective-permute-start | bytes 2949128 | tf_op jit(solution)/shard_map/ppermute | solution.py:71
  338.4 5.7 %copy-start.4 = (f32[128,2]{0,1:T(2,128)S(1)}, f32[128,2]{0,1:T(2,128)}, u32[]{:S(2)}) copy-start(f32[128,2]{0,1:T(2,128)} %param.15) | copy-start | bytes 3076
  338.4 40.2 %all-to-all-start.2 = ((bf16[32,40,1024]{2,1,0:T(8,128)(2,1)}), bf16[32,40,1024]{2,1,0:T(8,128)(2,1)S(1)}, u32[]{:S(2)}, u32[]{:S(2)}) async-start(bf16[32,40,1024]{2,1,0:T(8,128)(2,1)} %bitcast.68), calls=%async_computation.3 | async-start | bytes 5242880 | tf_op jit(solution)/shard_map/all_to_all | solution.py:85
Sparse Core Ops, SparseCore 0:
  9.8 121.0 all-gather.5
  140.3 96.3 reduce-scatter.1
  240.0 89.4 all-gather.3

commit v5 on v2

--- a/solution.py
+++ b/solution.py
@@ -66,17 +66,20 @@
         pairs = [(j, (j + step) % n_hi) for j in range(n_hi)]
         shifted.append(lax.ppermute(received, "dy", pairs))
     me_hi = lax.axis_index("dy")
-    order = (me_hi - jnp.arange(n_hi, dtype=jnp.int32)) % n_hi
-    slots_group = jnp.take(jnp.stack(shifted), order, axis=0).reshape(-1, width)
 
     grad = lax.psum_scatter(partial, "dz", scatter_dimension=0, tiled=True).astype(jnp.float32)
     master_new, m_new, v_new = adam_update(master[0], moment_one[0], moment_two[0], grad)
     weights_shard = master_new.astype(jnp.bfloat16)
 
     weights_group = lax.all_gather(weights_shard, "dz", axis=0, tiled=True)
-    product = lax.dot_general(
-        slots_group, weights_group, (((1,), (1,)), ((), ())), preferred_element_type=jnp.float32
-    ).astype(jnp.bfloat16)
+    product = jnp.zeros((n_hi, experts * capacity, group_width), jnp.bfloat16)
+    for step in range(n_hi):
+        block = shifted[step].reshape(-1, width)
+        part = lax.dot_general(
+            block, weights_group, (((1,), (1,)), ((), ())), preferred_element_type=jnp.float32
+        ).astype(jnp.bfloat16)
+        product = lax.dynamic_update_slice(product, part[None], ((me_hi - step) % n_hi, 0, 0))
+    product = product.reshape(-1, group_width)
     returned = lax.all_to_all(
         product, ("dy", "expert"), split_axis=0, concat_axis=0, tiled=True
     ).reshape(n_hi, experts * capacity, group_width)

time: 271 us -> 260 us (0.959)
  other arithmetic: 11.5 us -> 3.87 us
  local copies, waits for them, and re-layouts: 16.7 us -> 13.5 us
    all_gather x1, waiting for transfers between devices: 0.01 us -> 42.1 us  [body(): weights_group = lax.all_gather(weights_shard, 'dz', axis=0, tiled=True)]
    ppermute x3, waiting for transfers between devices: 40.8 us -> 0.01 us  [body(): shifted.append(lax.ppermute(received, 'dy', pairs))]
    gather x1 -> x0, local copies, waits for them, and re-layouts: 4.79 us -> none  [body(): slots_group = jnp.take(jnp.stack(shifted), order, axis=0).reshape(-1, width)]
    select_n x2 -> x0, other arithmetic: 4.43 us -> none  [body(): slots_group = jnp.take(jnp.stack(shifted), order, axis=0).reshape(-1, width)]
    another operation x3 -> x2, other arithmetic: 3.76 us -> 0.62 us  [the longest x1 3.14 us: body(): slots_group = jnp.take(jnp.stack(shifted), order, axis=0).reshape(-1, width)]
    dot_general x1 -> x4, matrix products: 8.86 us -> 7.18 us  [body(): lax.dot_general(block, weights_group, (((1,), (1,)), ((), ())), preferred...]
    unnamed x12 -> x16, local copies, waits for them, and re-layouts: 4.8 us -> 6.32 us
  transfers between devices with their start and end apart: 9 -> 9, of which waited for: 7 -> 5; matrix products, arithmetic and copies ran while one was open for 14% -> 12% of each run, Pallas kernels for 0% -> 0%
where the time goes in v5:
time: 260 us; the launch traced here: 259 us
  waiting for transfers between devices  176 us (68%)
  starting transfers between devices  29.9 us (12%)
  matrix products  21.8 us (8%)
  between operations  13.9 us (5%)
  local copies, waits for them, and re-layouts  13.5 us (5%)
  other arithmetic  3.87 us (1%)
    all_to_all x1, waiting for transfers between devices, body(): lax.all_to_all(grads_here.reshape(saved, n_hi, group_width).transpose(1,...  51.4 us
    reduce_scatter x1, waiting for transfers between devices, body(): lax.psum_scatter(partial, 'dz', scatter_dimension=0, tiled=True)  45.1 us
    all_gather x1, waiting for transfers between devices, body(): weights_group = lax.all_gather(weights_shard, 'dz', axis=0, tiled=True)  42.1 us
    all_to_all x1, waiting for transfers between devices, body(): lax.all_to_all(product, ('dy', 'expert'), split_axis=0, concat_axis=0, ti...  33.7 us
    all_to_all x1, starting transfers between devices, body(): lax.all_to_all(outgoing, 'expert', split_axis=0, concat_axis=0, tiled=True)  11.5 us
    dot_general x1, matrix products, body(): lax.dot_general(grads_group, rows_group, (((0,), (0,)), ((), ())), prefer...  9.25 us
    all_to_all x1, starting transfers between devices, body(): lax.all_to_all(product, ('dy', 'expert'), split_axis=0, concat_axis=0, ti...  8.23 us
    dot_general x4, matrix products, body(): lax.dot_general(block, weights_group, (((1,), (1,)), ((), ())), preferred...  7.18 us
  transfers between devices with their start and end apart: 9, of which 5 were waited for; matrix products, arithmetic and copies ran while one was open for 12% of the time, Pallas kernels for 0%

profile of v5, /device:TPU:1, one launch (start us, length us, event | category | flops | bytes accessed | tf_op | source)
XLA Modules:
  0.0 259.3 jit_solution(5019273427832935785)
XLA Ops:
  7.2 0.7 all-gather.6.cloned.1.call-update
  7.9 4.7 %copy.37 = bf16[1,384,4096]{1,2,0:T(8,128)(2,1)} copy(bf16[1,384,4096]{2,1,0:T(8,128)(2,1)} %param.12) | data formatting | bytes 6291456 | tf_op args[4]
  12.6 5.1 %all-to-all-start.1 = ((bf16[4,384,1024]{1,2,0:T(8,128)(2,1)}), bf16[4,384,1024]{1,2,0:T(8,128)(2,1)S(1)}, u32[]{:S(2)}, u32[]{:S(2)}) async-start(bf16[4,384,1024]{1,2,0:T(8,128)(2,1)} %bitcast.78), calls=%async_computation.1 | async-start | bytes 6291456 | tf_op jit(solution)/shard_map/all_to_all | solution.py:41
  19.0 3.0 %reshape.80 = bf16[256,1536]{1,0:T(8,128)(2,1)} reshape(bf16[128,2,1536]{2,1,0:T(2,128)(2,1)} %param.13) | data formatting | bytes 1572864 | tf_op jit(solution)/shard_map/reshape | solution.py:59
  22.0 2.5 convolution_convert_fusion.1
  24.5 51.4 %all-to-all-done.1 = bf16[4,384,1024]{1,2,0:T(8,128)(2,1)S(1)} async-done(((bf16[4,384,1024]{1,2,0:T(8,128)(2,1)}), bf16[4,384,1024]{1,2,0:T(8,128)(2,1)S(1)}, u32[]{:S(2)}, u32[]{:S(2)}) %all-to-all-start.1) | async-done | bytes 3145760 | tf_op jit(solution)/shard_map/all_to_all | solution.py:41
  76.0 11.5 %all-to-all-start = ((bf16[8,40,1536]{2,1,0:T(8,128)(2,1)}), bf16[8,40,1536]{2,1,0:T(8,128)(2,1)}, u32[]{:S(2)}, u32[]{:S(2)}) async-start(bf16[8,40,1536]{2,1,0:T(8,128)(2,1)} %bitcast.82), calls=%async_computation | async-start | bytes 1966080 | tf_op jit(solution)/shard_map/all_to_all | solution.py:62
  87.5 3.0 %copy.38 = bf16[4,384,1024]{2,1,0:T(8,128)(2,1)} copy(bf16[4,384,1024]{1,2,0:T(8,128)(2,1)S(1)} %all-to-all-done.1) | data formatting | bytes 6291456 | tf_op jit(solution)/shard_map/all_to_all | solution.py:41
  90.5 3.2 %all-gather.6.cloned.1.call-done = bf16[1,1536,1536]{2,1,0:T(8,128)(2,1)} async-done(((bf16[1,384,1536]{2,1,0:T(8,128)(2,1)}), bf16[1,1536,1536]{2,1,0:T(8,128)(2,1)}) %all-gather.6.cloned.1.call-update) | async-done | bytes 4718608 | tf_op jit(solution)/shard_map/all_gather | solution.py:40
  93.7 9.3 %fusion.2 = bf16[1024,1536]{1,0:T(8,128)(2,1)} fusion(bf16[1536,1024]{1,0:T(8,128)(2,1)} %bitcast.83, bf16[1,1536,1536]{2,1,0:T(8,128)(2,1)} %all-gather.6.cloned.1.call-done), kind=kOutput, calls=%fused_computation.3 | convolution fusion | flops 4833411072 | bytes 11010048 | tf_op jit(solution)/shard_map/dot_general | solution.py:48
  103.0 45.1 %reduce-scatter.2.cloned.1.call-done = bf16[128,1536]{1,0:T(8,128)(2,1)} async-done(((bf16[1024,1536]{1,0:T(8,128)(2,1)}), bf16[128,1536]{1,0:T(8,128)(2,1)}) %reduce-scatter.2.cloned.1.call-update) | async-done | bytes 393232 | tf_op jit(solution)/shard_map/reduce_scatter | solution.py:70
  148.1 3.1 %fusion.21 = (bf16[128,1536]{1,0:T(8,128)(2,1)}, f32[128,1536]{1,0:T(8,128)}, f32[1,128,1536]{2,1,0:T(8,128)}, f32[1,128,1536]{2,1,0:T(8,128)}) fusion(f32[1,128,1536]{2,1,0:T(8,128)S(1)} %copy-done.1, bf16[128,1536]{1,0:T(8,128)(2,1)} %reduce-scatter.2.cloned.1.call-done, f32[1,128,1536]{2,1,0:T(8,128)S(1)} %copy-done.2, f32[1,128,1536]{2,1,0:T(8,128)S(1)} %copy-done.3), kind=kLoop, calls=%fused_computation.37 | loop fusion | flops 2949120 | bytes 5505024 | tf_op jit(solution)/shard_map/convert_element_type | solution.py:72
  151.3 1.2 collective-permute-start
  152.5 2.5 collective-permute-start.1
  154.9 1.3 collective-permute-start.2
  156.2 42.1 %all-gather.4.cloned.1.call-done = bf16[1024,1536]{1,0:T(8,128)(2,1)} async-done(((bf16[128,1536]{1,0:T(8,128)(2,1)}), bf16[1024,1536]{1,0:T(8,128)(2,1)}) %all-gather.4.cloned.1.call-update) | async-done | bytes 3145744 | tf_op jit(solution)/shard_map/all_gather | solution.py:74
  198.7 3.5 %fusion.6 = bf16[4,320,1024]{2,1,0:T(8,128)(2,1)S(1)} fusion(bf16[4,320,1024]{2,1,0:T(8,128)(2,1)S(1)} %broadcast_in_dim.32, s32[]{:T(128)S(6)} %select_n.32, bf16[320,1536]{1,0:T(8,128)(2,1)} %bitcast.13, bf16[1024,1536]{1,0:T(8,128)(2,1)} %all-gather.4.cloned.1.call-done), kind=kOutput, calls=%fused_computation.10 | convolution fusion | flops 1006960640 | bytes 4784132 | tf_op jit(solution)/shard_map/dot_general | solution.py:78
  202.3 1.2 fusion.8
  203.5 1.2 fusion.10
  204.7 1.2 fusion.12
  205.9 1.5 copy-done
  207.4 8.2 %all-to-all-start.2 = ((bf16[32,40,1024]{2,1,0:T(8,128)(2,1)}), bf16[32,40,1024]{2,1,0:T(8,128)(2,1)S(1)}, u32[]{:S(2)}, u32[]{:S(2)}) async-start(bf16[32,40,1024]{2,1,0:T(8,128)(2,1)} %bitcast.80), calls=%async_computation.3 | async-start | bytes 5242880 | tf_op jit(solution)/shard_map/all_to_all | solution.py:83
  216.0 33.7 %all-to-all-done.2 = bf16[32,40,1024]{2,1,0:T(8,128)(2,1)S(1)} async-done(((bf16[32,40,1024]{2,1,0:T(8,128)(2,1)}), bf16[32,40,1024]{2,1,0:T(8,128)(2,1)S(1)}, u32[]{:S(2)}, u32[]{:S(2)}) %all-to-all-start.2) | async-done | bytes 2621472 | tf_op jit(solution)/shard_map/all_to_all | solution.py:83
  249.9 2.8 %convolution_convert_fusion = bf16[128,4096]{1,0:T(8,128)(2,1)} fusion(f32[128,320]{0,1:T(8,128)S(1)} %select_reduce_fusion, bf16[4096,320]{0,1:T(8,128)(2,1)S(1)} %bitcast.81), kind=kOutput, calls=%fused_computation | convolution fusion | flops 2013790208 | bytes 3833856 | tf_op jit(solution)/shard_map/ts,hsf->thf/dot_general | solution.py:92
  (38 shorter events, 2.3 us)
Async XLA Ops:
  7.2 86.5 %all-gather.6.cloned.1.call-start = ((), (), s32[]{:S(2)}) async-start(), calls=%async_computation.6 | async-start | bytes 5898240 | tf_op jit(solution)/shard_map/all_gather | solution.py:40
  12.6 5.1 %copy-start.4 = (s32[128,2]{0,1:T(2,128)S(1)}, s32[128,2]{0,1:T(2,128)}, u32[]{:S(2)}) copy-start(s32[128,2]{0,1:T(2,128)} %param.14) | copy-start | bytes 3076
  12.6 63.4 %all-to-all-start.1 = ((bf16[4,384,1024]{1,2,0:T(8,128)(2,1)}), bf16[4,384,1024]{1,2,0:T(8,128)(2,1)S(1)}, u32[]{:S(2)}, u32[]{:S(2)}) async-start(bf16[4,384,1024]{1,2,0:T(8,128)(2,1)} %bitcast.78), calls=%async_computation.1 | async-start | bytes 6291456 | tf_op jit(solution)/shard_map/all_to_all | solution.py:41
  76.0 27.0 %all-to-all-start = ((bf16[8,40,1536]{2,1,0:T(8,128)(2,1)}), bf16[8,40,1536]{2,1,0:T(8,128)(2,1)}, u32[]{:S(2)}, u32[]{:S(2)}) async-start(bf16[8,40,1536]{2,1,0:T(8,128)(2,1)} %bitcast.82), calls=%async_computation | async-start | bytes 1966080 | tf_op jit(solution)/shard_map/all_to_all | solution.py:62
  87.5 60.7 %reduce-scatter.2.cloned.1.call-start = ((), (), s32[]{:S(2)}) async-start(), calls=%async_computation.4 | async-start | bytes 3538944 | tf_op jit(solution)/shard_map/reduce_scatter | solution.py:70
  102.9 45.2 %copy-start.1 = (f32[1,128,1536]{2,1,0:T(8,128)S(1)}, f32[1,128,1536]{2,1,0:T(8,128)}, u32[]{:S(2)}) copy-start(f32[1,128,1536]{2,1,0:T(8,128)} %param.10) | copy-start | bytes 2359300
  102.9 45.2 %copy-start.2 = (f32[1,128,1536]{2,1,0:T(8,128)S(1)}, f32[1,128,1536]{2,1,0:T(8,128)}, u32[]{:S(2)}) copy-start(f32[1,128,1536]{2,1,0:T(8,128)} %param.9) | copy-start | bytes 2359300
  102.9 45.2 %copy-start.3 = (f32[1,128,1536]{2,1,0:T(8,128)S(1)}, f32[1,128,1536]{2,1,0:T(8,128)}, u32[]{:S(2)}) copy-start(f32[1,128,1536]{2,1,0:T(8,128)} %param.8) | copy-start | bytes 2359300
  103.0 95.4 %all-gather.4.cloned.1.call-start = ((), (), s32[]{:S(2)}) async-start(), calls=%async_computation.5 | async-start | bytes 3538944 | tf_op jit(solution)/shard_map/all_gather | solution.py:74
  151.3 51.0 %collective-permute-start = (bf16[8,40,1536]{2,1,0:T(8,128)(2,1)}, bf16[8,40,1536]{2,1,0:T(8,128)(2,1)S(1)}, u32[]{:S(2)}, u32[]{:S(2)}) collective-permute-start(bf16[8,40,1536]{2,1,0:T(8,128)(2,1)} %all-to-all-done), channel_id=1, source_target_pairs={{0,64},{64,128},{128,192},{192,0},{1,65},{65,129},{129,193},{193,1... | collective-permute-start | bytes 2949128 | tf_op jit(solution)/shard_map/ppermute | solution.py:67
  152.5 51.0 %collective-permute-start.1 = (bf16[8,40,1536]{2,1,0:T(8,128)(2,1)}, bf16[8,40,1536]{2,1,0:T(8,128)(2,1)S(1)}, u32[]{:S(2)}, u32[]{:S(2)}) collective-permute-start(bf16[8,40,1536]{2,1,0:T(8,128)(2,1)} %all-to-all-done), channel_id=1, source_target_pairs={{0,128},{64,192},{128,0},{192,64},{1,129},{65,193},{129,1},{193,65... | collective-permute-start | bytes 2949128 | tf_op jit(solution)/shard_map/ppermute | solution.py:67
  154.9 49.8 %collective-permute-start.2 = (bf16[8,40,1536]{2,1,0:T(8,128)(2,1)}, bf16[8,40,1536]{2,1,0:T(8,128)(2,1)S(1)}, u32[]{:S(2)}, u32[]{:S(2)}) collective-permute-start(bf16[8,40,1536]{2,1,0:T(8,128)(2,1)} %all-to-all-done), channel_id=1, source_target_pairs={{0,192},{64,0},{128,64},{192,128},{1,193},{65,1},{129,65},{193,129... | collective-permute-start | bytes 2949128 | tf_op jit(solution)/shard_map/ppermute | solution.py:67
  198.7 3.6 %copy-start.6 = (bf16[1024,1536]{1,0:T(8,128)(2,1)S(1)}, bf16[1024,1536]{1,0:T(8,128)(2,1)}, u32[]{:S(2)}) copy-start(bf16[1024,1536]{1,0:T(8,128)(2,1)} %all-gather.4.cloned.1.call-done) | copy-start | bytes 9437188
  205.9 1.5 copy-start
  207.4 8.5 %copy-start.5 = (f32[128,2]{0,1:T(2,128)S(1)}, f32[128,2]{0,1:T(2,128)}, u32[]{:S(2)}) copy-start(f32[128,2]{0,1:T(2,128)} %param.15) | copy-start | bytes 3076
  207.4 42.2 %all-to-all-start.2 = ((bf16[32,40,1024]{2,1,0:T(8,128)(2,1)}), bf16[32,40,1024]{2,1,0:T(8,128)(2,1)S(1)}, u32[]{:S(2)}, u32[]{:S(2)}) async-start(bf16[32,40,1024]{2,1,0:T(8,128)(2,1)} %bitcast.80), calls=%async_computation.3 | async-start | bytes 5242880 | tf_op jit(solution)/shard_map/all_to_all | solution.py:83
Sparse Core Ops, SparseCore 0:
  9.8 83.8 all-gather.5
  103.1 45.0 reduce-scatter.1
  151.4 46.9 all-gather.3

commit v6 on v2

--- a/solution.py
+++ b/solution.py
@@ -37,6 +37,7 @@
     grads_here = saved_grads[0]
     saved, d_model = grads_here.shape
     group_width = d_model // n_hi
+    own = group_width // n_lo
     rows_group = lax.all_gather(rows_here, "dy", axis=0, tiled=True)
     grads_group = lax.all_to_all(
         grads_here.reshape(saved, n_hi, group_width).transpose(1, 0, 2),
@@ -66,34 +67,66 @@
         pairs = [(j, (j + step) % n_hi) for j in range(n_hi)]
         shifted.append(lax.ppermute(received, "dy", pairs))
     me_hi = lax.axis_index("dy")
-    order = (me_hi - jnp.arange(n_hi, dtype=jnp.int32)) % n_hi
-    slots_group = jnp.take(jnp.stack(shifted), order, axis=0).reshape(-1, width)
 
     grad = lax.psum_scatter(partial, "dz", scatter_dimension=0, tiled=True).astype(jnp.float32)
     master_new, m_new, v_new = adam_update(master[0], moment_one[0], moment_two[0], grad)
     weights_shard = master_new.astype(jnp.bfloat16)
 
-    weights_group = lax.all_gather(weights_shard, "dz", axis=0, tiled=True)
-    product = lax.dot_general(
-        slots_group, weights_group, (((1,), (1,)), ((), ())), preferred_element_type=jnp.float32
-    ).astype(jnp.bfloat16)
-    returned = lax.all_to_all(
-        product, ("dy", "expert"), split_axis=0, concat_axis=0, tiled=True
-    ).reshape(n_hi, experts * capacity, group_width)
+    me_lo = lax.axis_index("dz")
+    ahead = [(j, (j + 1) % n_lo) for j in range(n_lo)]
+    behind = [(j, (j - 1) % n_lo) for j in range(n_lo)]
+    blocks, owners = [weights_shard], [0]
+    forward = backward = weights_shard
+    for hop in range(1, n_lo // 2 + 1):
+        forward = lax.ppermute(forward, "dz", ahead)
+        blocks.append(forward)
+        owners.append(-hop)
+        if hop < n_lo - hop:
+            backward = lax.ppermute(backward, "dz", behind)
+            blocks.append(backward)
+            owners.append(hop)
+    split = min(len(blocks), 5)
+    groups = [(0, split), (split, len(blocks))] if split < len(blocks) else [(0, split)]
 
     slot_pairs = slot_id.reshape(tok_count, top_count)
     combine = jnp.sum(
         (slot_pairs[:, :, None] == table[None, None, :]).astype(jnp.float32) * gates[:, :, None],
         axis=1,
     )
+    pieces = []
+    for first, last in groups:
+        weights_group = jnp.concatenate(blocks[first:last], axis=0)
+        count = last - first
+        product = jnp.zeros((n_hi, experts * capacity, count * own), jnp.bfloat16)
+        for step in range(n_hi):
+            block = shifted[step].reshape(-1, width)
+            part = lax.dot_general(
+                block, weights_group, (((1,), (1,)), ((), ())), preferred_element_type=jnp.float32
+            ).astype(jnp.bfloat16)
+            product = lax.dynamic_update_slice(product, part[None], ((me_hi - step) % n_hi, 0, 0))
+        returned = lax.all_to_all(
+            product.reshape(-1, count * own), ("dy", "expert"), split_axis=0, concat_axis=0, tiled=True
+        ).reshape(n_hi, experts * capacity, count, own)
+        pieces.append(
+            jnp.einsum(
+                "ts,hsjr->thjr",
+                combine,
+                returned.astype(jnp.float32),
+                precision=lax.Precision.HIGHEST,
+                preferred_element_type=jnp.float32,
+            )
+        )
+    gathered = jnp.concatenate(pieces, axis=2)
+    where = (me_lo + jnp.asarray(owners, jnp.int32)) % n_lo
+    placing = (where[:, None] == jnp.arange(n_lo, dtype=jnp.int32)[None, :]).astype(jnp.float32)
     mixed = jnp.einsum(
-        "ts,hsf->thf",
-        combine,
-        returned.astype(jnp.float32),
+        "thjr,jb->thbr",
+        gathered,
+        placing,
         precision=lax.Precision.HIGHEST,
         preferred_element_type=jnp.float32,
     )
-    mixed = mixed.reshape(tok_count, n_hi * group_width).astype(jnp.bfloat16)
+    mixed = mixed.reshape(tok_count, d_model).astype(jnp.bfloat16)
     return (master_new[None], m_new[None], v_new[None], mixed)
 
 

time: 271 us -> 273 us (level)
  waiting for transfers between devices: 175 us -> 149 us
  starting transfers between devices: 30.3 us -> 44.6 us
  local copies, waits for them, and re-layouts: 16.7 us -> 25.5 us
  matrix products: 23.6 us -> 32.2 us
  other arithmetic: 11.5 us -> 5.79 us
    all_to_all x1 -> x2, waiting for transfers between devices: 33.7 us -> 12.1 us  [body(): lax.all_to_all(product.reshape(-1, count * own), ('dy', 'expert'), split_...]
    ppermute x3, waiting for transfers between devices: 40.8 us -> 22.1 us  [body(): shifted.append(lax.ppermute(received, 'dy', pairs))]
    ppermute x0 -> x7, waiting for transfers between devices: none -> 14.7 us  [the longest x4 14.7 us: body(): forward = lax.ppermute(forward, 'dz', ahead)]
    dot_general x2 -> x11, matrix products: 11.7 us -> 20.5 us  [the longest x8 14.8 us: body(): lax.dot_general(block, weights_group, (((1,), (1,)), ((), ())), preferred...]
    all_to_all x1 -> x2, starting transfers between devices: 8.67 us -> 16 us  [body(): lax.all_to_all(product.reshape(-1, count * own), ('dy', 'expert'), split_...]
    ppermute x0 -> x7, starting transfers between devices: none -> 6.89 us  [the longest x3 4.95 us: body(): backward = lax.ppermute(backward, 'dz', behind)]
    reshape x0 -> x2, local copies, waits for them, and re-layouts: none -> 6.09 us  [body(): returned = lax.all_to_all(product.reshape(-1, count * own), ('dy', 'exper...]
    gather x1 -> x0, local copies, waits for them, and re-layouts: 4.79 us -> none  [body(): slots_group = jnp.take(jnp.stack(shifted), order, axis=0).reshape(-1, width)]
  transfers between devices with their start and end apart: 9 -> 16, of which waited for: 7 -> 10; matrix products, arithmetic and copies ran while one was open for 14% -> 20% of each run, Pallas kernels for 0% -> 0%
where the time goes in v6:
time: 273 us; the launch traced here: 272 us
  waiting for transfers between devices  149 us (55%)
  starting transfers between devices  44.6 us (16%)
  matrix products  32.2 us (12%)
  local copies, waits for them, and re-layouts  25.5 us (9%)
  between operations  14.3 us (5%)
  other arithmetic  5.79 us (2%)
    all_to_all x1, waiting for transfers between devices, body(): lax.all_to_all(grads_here.reshape(saved, n_hi, group_width).transpose(1,...  51.4 us
    reduce_scatter x1, waiting for transfers between devices, body(): lax.psum_scatter(partial, 'dz', scatter_dimension=0, tiled=True)  44.8 us
    ppermute x3, waiting for transfers between devices, body(): shifted.append(lax.ppermute(received, 'dy', pairs))  22.1 us
    all_to_all x2, starting transfers between devices, body(): lax.all_to_all(product.reshape(-1, count * own), ('dy', 'expert'), split_...  16 us
    dot_general x8, matrix products, body(): lax.dot_general(block, weights_group, (((1,), (1,)), ((), ())), preferred...  14.8 us
    ppermute x4, waiting for transfers between devices, body(): forward = lax.ppermute(forward, 'dz', ahead)  14.7 us
    all_to_all x2, waiting for transfers between devices, body(): lax.all_to_all(product.reshape(-1, count * own), ('dy', 'expert'), split_...  12.1 us
    all_to_all x1, starting transfers between devices, body(): lax.all_to_all(outgoing, 'expert', split_axis=0, concat_axis=0, tiled=True)  11.5 us
  transfers between devices with their start and end apart: 16, of which 10 were waited for; matrix products, arithmetic and copies ran while one was open for 20% of the time, Pallas kernels for 0%

profile of v6, /device:TPU:1, one launch (start us, length us, event | category | flops | bytes accessed | tf_op | source)
XLA Modules:
  0.0 271.5 jit_solution(9376554412036872971)
XLA Ops:
  7.9 4.7 %copy.42 = bf16[1,384,4096]{1,2,0:T(8,128)(2,1)} copy(bf16[1,384,4096]{2,1,0:T(8,128)(2,1)} %param.13) | data formatting | bytes 6291456 | tf_op args[4]
  12.6 5.1 %all-to-all-start.1 = ((bf16[4,384,1024]{1,2,0:T(8,128)(2,1)}), bf16[4,384,1024]{1,2,0:T(8,128)(2,1)S(1)}, u32[]{:S(2)}, u32[]{:S(2)}) async-start(bf16[4,384,1024]{1,2,0:T(8,128)(2,1)} %bitcast.114), calls=%async_computation.1 | async-start | bytes 6291456 | tf_op jit(solution)/shard_map/all_to_all | solution.py:42
  18.9 3.0 %reshape.93 = bf16[256,1536]{1,0:T(8,128)(2,1)} reshape(bf16[128,2,1536]{2,1,0:T(2,128)(2,1)} %param.14) | data formatting | bytes 1572864 | tf_op jit(solution)/shard_map/reshape | solution.py:60
  22.0 2.5 convolution_convert_fusion
  24.5 51.4 %all-to-all-done.1 = bf16[4,384,1024]{1,2,0:T(8,128)(2,1)S(1)} async-done(((bf16[4,384,1024]{1,2,0:T(8,128)(2,1)}), bf16[4,384,1024]{1,2,0:T(8,128)(2,1)S(1)}, u32[]{:S(2)}, u32[]{:S(2)}) %all-to-all-start.1) | async-done | bytes 3145760 | tf_op jit(solution)/shard_map/all_to_all | solution.py:42
  75.9 11.5 %all-to-all-start = ((bf16[8,40,1536]{2,1,0:T(8,128)(2,1)}), bf16[8,40,1536]{2,1,0:T(8,128)(2,1)}, u32[]{:S(2)}, u32[]{:S(2)}) async-start(bf16[8,40,1536]{2,1,0:T(8,128)(2,1)} %bitcast.116), calls=%async_computation | async-start | bytes 1966080 | tf_op jit(solution)/shard_map/all_to_all | solution.py:63
  87.4 2.9 %copy.43 = bf16[4,384,1024]{2,1,0:T(8,128)(2,1)} copy(bf16[4,384,1024]{1,2,0:T(8,128)(2,1)S(1)} %all-to-all-done.1) | data formatting | bytes 6291456 | tf_op jit(solution)/shard_map/all_to_all | solution.py:42
  90.3 3.3 %all-gather.3.cloned.1.call-done = bf16[1,1536,1536]{2,1,0:T(8,128)(2,1)} async-done(((bf16[1,384,1536]{2,1,0:T(8,128)(2,1)}), bf16[1,1536,1536]{2,1,0:T(8,128)(2,1)}) %all-gather.3.cloned.1.call-update) | async-done | bytes 4718608 | tf_op jit(solution)/shard_map/all_gather | solution.py:41
  93.6 9.3 %fusion.2 = bf16[1024,1536]{1,0:T(8,128)(2,1)} fusion(bf16[1536,1024]{1,0:T(8,128)(2,1)} %bitcast.117, bf16[1,1536,1536]{2,1,0:T(8,128)(2,1)} %all-gather.3.cloned.1.call-done), kind=kOutput, calls=%fused_computation.2 | convolution fusion | flops 4833411072 | bytes 11010048 | tf_op jit(solution)/shard_map/dot_general | solution.py:49
  103.2 44.8 %reduce-scatter.2.cloned.1.call-done = bf16[128,1536]{1,0:T(8,128)(2,1)} async-done(((bf16[1024,1536]{1,0:T(8,128)(2,1)}), bf16[128,1536]{1,0:T(8,128)(2,1)}) %reduce-scatter.2.cloned.1.call-update) | async-done | bytes 393232 | tf_op jit(solution)/shard_map/reduce_scatter | solution.py:71
  154.5 2.6 collective-permute-start.5
  158.4 2.7 collective-permute-start.3
  161.1 6.2 %collective-permute-done.2 = bf16[128,1536]{1,0:T(8,128)(2,1)} collective-permute-done((bf16[128,1536]{1,0:T(8,128)(2,1)S(1)}, bf16[128,1536]{1,0:T(8,128)(2,1)}, u32[]{:S(2)}, u32[]{:S(2)}) %collective-permute-start.2) | collective-permute-done | bytes 393248 | tf_op jit(solution)/shard_map/ppermute | solution.py:81
  170.8 2.9 %fusion.13 = bf16[4,320,640]{2,1,0:T(8,128)(2,1)} fusion(bf16[4,320,640]{2,1,0:T(8,128)(2,1)} %broadcast_in_dim.49, s32[]{:T(128)S(6)} %select_n.51, bf16[320,1536]{1,0:T(8,128)(2,1)} %bitcast.17, bf16[640,1536]{1,0:T(8,128)(2,1)S(1)} %constant_dynamic-update-slice_fusion), kind=kOutput, calls=%fused_computation.15 | convolution fusion | flops 629350400 | bytes 3358724 | tf_op jit(solution)/shard_map/dot_general | solution.py:103
  175.4 20.6 %collective-permute-done.5 = bf16[8,40,1536]{2,1,0:T(8,128)(2,1)S(1)} collective-permute-done((bf16[8,40,1536]{2,1,0:T(8,128)(2,1)}, bf16[8,40,1536]{2,1,0:T(8,128)(2,1)S(1)}, u32[]{:S(2)}, u32[]{:S(2)}) %collective-permute-start.5) | collective-permute-done | bytes 983072 | tf_op jit(solution)/shard_map/ppermute | solution.py:68
  200.9 10.4 %all-to-all-start.2 = ((bf16[32,40,640]{2,1,0:T(8,128)(2,1)}), bf16[32,40,640]{2,1,0:T(8,128)(2,1)S(1)}, u32[]{:S(2)}, u32[]{:S(2)}) async-start(bf16[32,40,640]{2,1,0:T(8,128)(2,1)} %bitcast.25), calls=%async_computation.3 | async-start | bytes 3276800 | tf_op jit(solution)/shard_map/all_to_all | solution.py:107
  215.0 8.3 %collective-permute-done.9 = bf16[128,1536]{1,0:T(8,128)(2,1)S(1)} collective-permute-done((bf16[128,1536]{1,0:T(8,128)(2,1)}, bf16[128,1536]{1,0:T(8,128)(2,1)S(1)}, u32[]{:S(2)}, u32[]{:S(2)}) %collective-permute-start.9) | collective-permute-done | bytes 393248 | tf_op jit(solution)/shard_map/ppermute | solution.py:81
  224.4 2.6 fusion.21
  231.1 3.8 %all-to-all-done.2 = bf16[32,40,640]{2,1,0:T(8,128)(2,1)S(1)} async-done(((bf16[32,40,640]{2,1,0:T(8,128)(2,1)}), bf16[32,40,640]{2,1,0:T(8,128)(2,1)S(1)}, u32[]{:S(2)}, u32[]{:S(2)}) %all-to-all-start.2) | async-done | bytes 1638432 | tf_op jit(solution)/shard_map/all_to_all | solution.py:107
  235.0 5.6 %all-to-all-start.3 = ((bf16[32,40,384]{2,1,0:T(8,128)(2,1)}), bf16[32,40,384]{2,1,0:T(8,128)(2,1)}, u32[]{:S(2)}, u32[]{:S(2)}) async-start(bf16[32,40,384]{2,1,0:T(8,128)(2,1)} %bitcast.31), calls=%async_computation.4 | async-start | bytes 1966080 | tf_op jit(solution)/shard_map/all_to_all | solution.py:107
  243.0 3.4 %reshape.100 = bf16[4,320,5,128]{3,2,1,0:T(8,128)(2,1)S(1)} reshape(bf16[32,40,640]{2,1,0:T(8,128)(2,1)} %copy-done) | data formatting | bytes 3276800 | tf_op jit(solution)/shard_map/reshape | solution.py:109
  248.8 8.3 %all-to-all-done.3 = bf16[32,40,384]{2,1,0:T(8,128)(2,1)} async-done(((bf16[32,40,384]{2,1,0:T(8,128)(2,1)}), bf16[32,40,384]{2,1,0:T(8,128)(2,1)}, u32[]{:S(2)}, u32[]{:S(2)}) %all-to-all-start.3) | async-done | bytes 983072 | tf_op jit(solution)/shard_map/all_to_all | solution.py:107
  257.1 2.6 reshape.101
  260.8 2.5 fusion.9
  (84 shorter events, 35.9 us)
Async XLA Ops:
  7.2 86.5 %all-gather.3.cloned.1.call-start = ((), (), s32[]{:S(2)}) async-start(), calls=%async_computation.6 | async-start | bytes 5898240 | tf_op jit(solution)/shard_map/all_gather | solution.py:41
  12.6 5.1 %copy-start.5 = (s32[128,2]{0,1:T(2,128)S(1)}, s32[128,2]{0,1:T(2,128)}, u32[]{:S(2)}) copy-start(s32[128,2]{0,1:T(2,128)} %param.15) | copy-start | bytes 3076
  12.6 63.4 %all-to-all-start.1 = ((bf16[4,384,1024]{1,2,0:T(8,128)(2,1)}), bf16[4,384,1024]{1,2,0:T(8,128)(2,1)S(1)}, u32[]{:S(2)}, u32[]{:S(2)}) async-start(bf16[4,384,1024]{1,2,0:T(8,128)(2,1)} %bitcast.114), calls=%async_computation.1 | async-start | bytes 6291456 | tf_op jit(solution)/shard_map/all_to_all | solution.py:42
  75.9 27.0 %all-to-all-start = ((bf16[8,40,1536]{2,1,0:T(8,128)(2,1)}), bf16[8,40,1536]{2,1,0:T(8,128)(2,1)}, u32[]{:S(2)}, u32[]{:S(2)}) async-start(bf16[8,40,1536]{2,1,0:T(8,128)(2,1)} %bitcast.116), calls=%async_computation | async-start | bytes 1966080 | tf_op jit(solution)/shard_map/all_to_all | solution.py:63
  87.4 60.7 %reduce-scatter.2.cloned.1.call-start = ((), (), s32[]{:S(2)}) async-start(), calls=%async_computation.5 | async-start | bytes 3538944 | tf_op jit(solution)/shard_map/reduce_scatter | solution.py:71
  102.9 45.2 %copy-start.2 = (f32[1,128,1536]{2,1,0:T(8,128)S(1)}, f32[1,128,1536]{2,1,0:T(8,128)}, u32[]{:S(2)}) copy-start(f32[1,128,1536]{2,1,0:T(8,128)} %param.11) | copy-start | bytes 2359300
  102.9 45.2 %copy-start.3 = (f32[1,128,1536]{2,1,0:T(8,128)S(1)}, f32[1,128,1536]{2,1,0:T(8,128)}, u32[]{:S(2)}) copy-start(f32[1,128,1536]{2,1,0:T(8,128)} %param.10) | copy-start | bytes 2359300
  102.9 45.2 %copy-start.4 = (f32[1,128,1536]{2,1,0:T(8,128)S(1)}, f32[1,128,1536]{2,1,0:T(8,128)}, u32[]{:S(2)}) copy-start(f32[1,128,1536]{2,1,0:T(8,128)} %param.9) | copy-start | bytes 2359300
  103.2 50.0 %copy-start.13 = (s32[8]{0:T(128)S(1)}, s32[8]{0:T(128)}, u32[]{:S(2)}) copy-start(s32[8]{0:T(128)} %constant.99.clone) | copy-start | bytes 100
  150.6 7.8 %collective-permute-start = (bf16[128,1536]{1,0:T(8,128)(2,1)S(1)}, bf16[128,1536]{1,0:T(8,128)(2,1)S(1)}, u32[]{:S(2)}, u32[]{:S(2)}) collective-permute-start(bf16[128,1536]{1,0:T(8,128)(2,1)S(1)} %get-tuple-element.9), channel_id=1, source_target_pairs={{0,8},{8,16},{16,24},{24,32},{32,40},{40,48},{48,56},{56,0},{1,9},... | collective-permute-start | bytes 1179656 | tf_op jit(solution)/shard_map/ppermute | solution.py:81
  151.0 7.4 %collective-permute-start.1 = (bf16[128,1536]{1,0:T(8,128)(2,1)S(1)}, bf16[128,1536]{1,0:T(8,128)(2,1)S(1)}, u32[]{:S(2)}, u32[]{:S(2)}) collective-permute-start(bf16[128,1536]{1,0:T(8,128)(2,1)S(1)} %get-tuple-element.9), channel_id=1, source_target_pairs={{0,56},{8,0},{16,8},{24,16},{32,24},{40,32},{48,40},{56,48},{1,57}... | collective-permute-start | bytes 1179656 | tf_op jit(solution)/shard_map/ppermute | solution.py:85
  153.3 20.5 %collective-permute-start.4 = (bf16[8,40,1536]{2,1,0:T(8,128)(2,1)}, bf16[8,40,1536]{2,1,0:T(8,128)(2,1)S(1)}, u32[]{:S(2)}, u32[]{:S(2)}) collective-permute-start(bf16[8,40,1536]{2,1,0:T(8,128)(2,1)} %all-to-all-done), channel_id=1, source_target_pairs={{0,64},{64,128},{128,192},{192,0},{1,65},{65,129},{129,193},{193,1... | collective-permute-start | bytes 2949128 | tf_op jit(solution)/shard_map/ppermute | solution.py:68
  154.5 41.6 %collective-permute-start.5 = (bf16[8,40,1536]{2,1,0:T(8,128)(2,1)}, bf16[8,40,1536]{2,1,0:T(8,128)(2,1)S(1)}, u32[]{:S(2)}, u32[]{:S(2)}) collective-permute-start(bf16[8,40,1536]{2,1,0:T(8,128)(2,1)} %all-to-all-done), channel_id=1, source_target_pairs={{0,128},{64,192},{128,0},{192,64},{1,129},{65,193},{129,1},{193,65... | collective-permute-start | bytes 2949128 | tf_op jit(solution)/shard_map/ppermute | solution.py:68
  157.2 42.1 %collective-permute-start.6 = (bf16[8,40,1536]{2,1,0:T(8,128)(2,1)}, bf16[8,40,1536]{2,1,0:T(8,128)(2,1)S(1)}, u32[]{:S(2)}, u32[]{:S(2)}) collective-permute-start(bf16[8,40,1536]{2,1,0:T(8,128)(2,1)} %all-to-all-done), channel_id=1, source_target_pairs={{0,192},{64,0},{128,64},{192,128},{1,193},{65,1},{129,65},{193,129... | collective-permute-start | bytes 2949128 | tf_op jit(solution)/shard_map/ppermute | solution.py:68
  158.4 9.0 %collective-permute-start.2 = (bf16[128,1536]{1,0:T(8,128)(2,1)S(1)}, bf16[128,1536]{1,0:T(8,128)(2,1)}, u32[]{:S(2)}, u32[]{:S(2)}) collective-permute-start(bf16[128,1536]{1,0:T(8,128)(2,1)S(1)} %collective-permute-done), channel_id=1, source_target_pairs={{0,8},{8,16},{16,24},{24,32},{32,40},{40,48},{48,56},{56,0},{1,9},... | collective-permute-start | bytes 1179656 | tf_op jit(solution)/shard_map/ppermute | solution.py:81
  158.4 10.0 %collective-permute-start.3 = (bf16[128,1536]{1,0:T(8,128)(2,1)S(1)}, bf16[128,1536]{1,0:T(8,128)(2,1)}, u32[]{:S(2)}, u32[]{:S(2)}) collective-permute-start(bf16[128,1536]{1,0:T(8,128)(2,1)S(1)} %collective-permute-done.1), channel_id=1, source_target_pairs={{0,56},{8,0},{16,8},{24,16},{32,24},{40,32},{48,40},{56,48},{1,57}... | collective-permute-start | bytes 1179656 | tf_op jit(solution)/shard_map/ppermute | solution.py:85
  167.4 44.0 %collective-permute-start.7 = (bf16[128,1536]{1,0:T(8,128)(2,1)}, bf16[128,1536]{1,0:T(8,128)(2,1)}, u32[]{:S(2)}, u32[]{:S(2)}) collective-permute-start(bf16[128,1536]{1,0:T(8,128)(2,1)} %collective-permute-done.2), channel_id=1, source_target_pairs={{0,8},{8,16},{16,24},{24,32},{32,40},{40,48},{48,56},{56,0},{1,9},... | collective-permute-start | bytes 1179656 | tf_op jit(solution)/shard_map/ppermute | solution.py:81
  197.8 16.2 %collective-permute-start.8 = (bf16[128,1536]{1,0:T(8,128)(2,1)}, bf16[128,1536]{1,0:T(8,128)(2,1)}, u32[]{:S(2)}, u32[]{:S(2)}) collective-permute-start(bf16[128,1536]{1,0:T(8,128)(2,1)} %collective-permute-done.3), channel_id=1, source_target_pairs={{0,56},{8,0},{16,8},{24,16},{32,24},{40,32},{48,40},{56,48},{1,57}... | collective-permute-start | bytes 1179656 | tf_op jit(solution)/shard_map/ppermute | solution.py:85
  200.9 34.0 %all-to-all-start.2 = ((bf16[32,40,640]{2,1,0:T(8,128)(2,1)}), bf16[32,40,640]{2,1,0:T(8,128)(2,1)S(1)}, u32[]{:S(2)}, u32[]{:S(2)}) async-start(bf16[32,40,640]{2,1,0:T(8,128)(2,1)} %bitcast.25), calls=%async_computation.3 | async-start | bytes 3276800 | tf_op jit(solution)/shard_map/all_to_all | solution.py:107
  211.4 11.9 %collective-permute-start.9 = (bf16[128,1536]{1,0:T(8,128)(2,1)}, bf16[128,1536]{1,0:T(8,128)(2,1)S(1)}, u32[]{:S(2)}, u32[]{:S(2)}) collective-permute-start(bf16[128,1536]{1,0:T(8,128)(2,1)} %collective-permute-done.7), channel_id=1, source_target_pairs={{0,8},{8,16},{16,24},{24,32},{32,40},{40,48},{48,56},{56,0},{1,9},... | collective-permute-start | bytes 1179656 | tf_op jit(solution)/shard_map/ppermute | solution.py:81
  229.8 10.8 %copy-start.6 = (f32[128,2]{0,1:T(2,128)S(1)}, f32[128,2]{0,1:T(2,128)}, u32[]{:S(2)}) copy-start(f32[128,2]{0,1:T(2,128)} %param.16) | copy-start | bytes 3076
  235.0 5.7 %copy-start = (bf16[32,40,640]{2,1,0:T(8,128)(2,1)}, bf16[32,40,640]{2,1,0:T(8,128)(2,1)S(1)}, u32[]{:S(2)}) copy-start(bf16[32,40,640]{2,1,0:T(8,128)(2,1)S(1)} %all-to-all-done.2) | copy-start | bytes 4915204
  235.0 22.1 %all-to-all-start.3 = ((bf16[32,40,384]{2,1,0:T(8,128)(2,1)}), bf16[32,40,384]{2,1,0:T(8,128)(2,1)}, u32[]{:S(2)}, u32[]{:S(2)}) async-start(bf16[32,40,384]{2,1,0:T(8,128)(2,1)} %bitcast.31), calls=%async_computation.4 | async-start | bytes 1966080 | tf_op jit(solution)/shard_map/all_to_all | solution.py:107
  248.8 11.8 %copy-start.1 = (f32[128,4,5,128]{3,0,2,1:T(8,128)S(1)}, f32[128,4,5,128]{3,0,2,1:T(8,128)}, u32[]{:S(2)}) copy-start(f32[128,4,5,128]{3,0,2,1:T(8,128)} %fusion.7) | copy-start | bytes 3932164
  (6 other events, 11.6 us)
Sparse Core Ops, SparseCore 0:
  9.8 83.8 all-gather.2
  103.1 44.9 reduce-scatter.1

commit v7 on v5

--- a/solution.py
+++ b/solution.py
@@ -38,13 +38,21 @@
     saved, d_model = grads_here.shape
     group_width = d_model // n_hi
     rows_group = lax.all_gather(rows_here, "dy", axis=0, tiled=True)
-    grads_group = lax.all_to_all(
-        grads_here.reshape(saved, n_hi, group_width).transpose(1, 0, 2),
-        "dy",
-        split_axis=0,
-        concat_axis=0,
-        tiled=True,
-    ).reshape(n_hi * saved, group_width)
+    me_hi = lax.axis_index("dy")
+    grads_split = grads_here.reshape(saved, n_hi, group_width)
+    grads_group = jnp.zeros((n_hi, saved, group_width), grads_here.dtype)
+    grads_group = lax.dynamic_update_slice(
+        grads_group, lax.dynamic_index_in_dim(grads_split, me_hi, axis=1, keepdims=False)[None],
+        (me_hi, 0, 0),
+    )
+    for step in range(1, n_hi):
+        pairs = [(j, (j + step) % n_hi) for j in range(n_hi)]
+        sent = lax.dynamic_index_in_dim(grads_split, (me_hi + step) % n_hi, axis=1, keepdims=False)
+        arrived = lax.ppermute(sent, "dy", pairs)
+        grads_group = lax.dynamic_update_slice(
+            grads_group, arrived[None], ((me_hi - step) % n_hi, 0, 0)
+        )
+    grads_group = grads_group.reshape(n_hi * saved, group_width)
     partial = lax.dot_general(
         grads_group, rows_group, (((0,), (0,)), ((), ())), preferred_element_type=jnp.float32
     ).astype(jnp.bfloat16)
@@ -65,7 +73,6 @@
     for step in range(1, n_hi):
         pairs = [(j, (j + step) % n_hi) for j in range(n_hi)]
         shifted.append(lax.ppermute(received, "dy", pairs))
-    me_hi = lax.axis_index("dy")
 
     grad = lax.psum_scatter(partial, "dz", scatter_dimension=0, tiled=True).astype(jnp.float32)
     master_new, m_new, v_new = adam_update(master[0], moment_one[0], moment_two[0], grad)

time: 260 us -> 265 us (1.019)
  local copies, waits for them, and re-layouts: 13.5 us -> 23.3 us
  starting transfers between devices: 29.9 us -> 24.7 us
    all_to_all x1 -> x0, waiting for transfers between devices: 51.4 us -> none  [body(): lax.all_to_all(grads_here.reshape(saved, n_hi, group_width).transpose(1,...]
    ppermute x0 -> x3, waiting for transfers between devices: none -> 39.3 us  [body(): arrived = lax.ppermute(sent, 'dy', pairs)]
    all_gather x1, waiting for transfers between devices: 3.22 us -> 13.3 us  [body(): rows_group = lax.all_gather(rows_here, 'dy', axis=0, tiled=True)]
    dynamic_update_slice x0 -> x4, local copies, waits for them, and re-layouts: none -> 7.35 us  [the longest x3 6.31 us: body(): lax.dynamic_update_slice(grads_group, arrived[None], ((me_hi - step) % n_...]
    dynamic_slice x0 -> x5, local copies, waits for them, and re-layouts: none -> 7.12 us  [the longest x4 6.83 us: body(): lax.dynamic_index_in_dim(grads_split, (me_hi + step) % n_hi, axis=1, keep...]
    ppermute x0 -> x3, starting transfers between devices: none -> 5.88 us  [body(): arrived = lax.ppermute(sent, 'dy', pairs)]
    all_to_all x1, starting transfers between devices: 11.5 us -> 5.81 us  [body(): lax.all_to_all(outgoing, 'expert', split_axis=0, concat_axis=0, tiled=True)]
    all_to_all x1 -> x0, starting transfers between devices: 5.13 us -> none  [body(): lax.all_to_all(grads_here.reshape(saved, n_hi, group_width).transpose(1,...]
  transfers between devices with their start and end apart: 9 -> 11, of which waited for: 5 -> 6; matrix products, arithmetic and copies ran while one was open for 12% -> 15% of each run, Pallas kernels for 0% -> 0%
where the time goes in v7:
time: 265 us
  waiting for transfers between devices  176 us (66%)
  starting transfers between devices  24.7 us (9%)
  local copies, waits for them, and re-layouts  23.3 us (9%)
  matrix products  22.7 us (9%)
  between operations  14 us (5%)
  other arithmetic  3.88 us (1%)
    reduce_scatter x1, waiting for transfers between devices, body(): lax.psum_scatter(partial, 'dz', scatter_dimension=0, tiled=True)  47 us
    all_gather x1, waiting for transfers between devices, body(): weights_group = lax.all_gather(weights_shard, 'dz', axis=0, tiled=True)  42.2 us
    ppermute x3, waiting for transfers between devices, body(): arrived = lax.ppermute(sent, 'dy', pairs)  39.3 us
    all_to_all x1, waiting for transfers between devices, body(): lax.all_to_all(product, ('dy', 'expert'), split_axis=0, concat_axis=0, ti...  33.7 us
    all_gather x1, waiting for transfers between devices, body(): rows_group = lax.all_gather(rows_here, 'dy', axis=0, tiled=True)  13.3 us
    dot_general x4, matrix products, body(): lax.dot_general(block, weights_group, (((1,), (1,)), ((), ())), preferred...  9.29 us
    dot_general x1, matrix products, body(): lax.dot_general(grads_group, rows_group, (((0,), (0,)), ((), ())), prefer...  9.26 us
    all_to_all x1, starting transfers between devices, body(): lax.all_to_all(product, ('dy', 'expert'), split_axis=0, concat_axis=0, ti...  8.23 us
  transfers between devices with their start and end apart: 11, of which 6 were waited for; matrix products, arithmetic and copies ran while one was open for 15% of the time, Pallas kernels for 0%

profile of v7, /device:TPU:1, one launch (start us, length us, event | category | flops | bytes accessed | tf_op | source)
XLA Modules:
  0.0 264.8 jit_solution(13966395903736864234)
XLA Ops:
  7.9 3.4 %copy.43 = bf16[1,384,4096]{1,2,0:T(8,128)(2,1)S(1)} copy(bf16[1,384,4096]{2,1,0:T(8,128)(2,1)} %param.12) | data formatting | bytes 6291456 | tf_op args[4]
  13.2 2.4 copy.45
  15.7 2.1 collective-permute-start
  17.8 2.3 copy.46
  20.1 2.6 collective-permute-start.1
  27.2 5.8 %all-to-all-start = ((bf16[8,40,1536]{2,1,0:T(8,128)(2,1)}), bf16[8,40,1536]{2,1,0:T(8,128)(2,1)S(1)}, u32[]{:S(2)}, u32[]{:S(2)}) async-start(bf16[8,40,1536]{2,1,0:T(8,128)(2,1)} %bitcast.4), calls=%async_computation | async-start | bytes 1966080 | tf_op jit(solution)/shard_map/all_to_all | solution.py:70
  33.3 2.1 broadcast_in_dim.44
  36.5 4.1 %collective-permute-done = bf16[384,1024]{1,0:T(8,128)(2,1)} collective-permute-done((bf16[384,1024]{1,0:T(8,128)(2,1)}, bf16[384,1024]{1,0:T(8,128)(2,1)}, u32[]{:S(2)}, u32[]{:S(2)}) %collective-permute-start) | collective-permute-done | bytes 786464 | tf_op jit(solution)/shard_map/ppermute | solution.py:51
  40.6 2.1 bitcast_dynamic-update-slice_fusion.2
  42.7 35.2 %collective-permute-done.1 = bf16[384,1024]{1,0:T(8,128)(2,1)} collective-permute-done((bf16[384,1024]{1,0:T(8,128)(2,1)}, bf16[384,1024]{1,0:T(8,128)(2,1)}, u32[]{:S(2)}, u32[]{:S(2)}) %collective-permute-start.1) | collective-permute-done | bytes 786464 | tf_op jit(solution)/shard_map/ppermute | solution.py:51
  77.9 2.1 bitcast_dynamic-update-slice_fusion.1
  79.9 2.2 bitcast_dynamic-update-slice_fusion
  82.1 13.3 %all-gather.6.cloned.1.call-done = bf16[1,1536,1536]{2,1,0:T(8,128)(2,1)} async-done(((bf16[1,384,1536]{2,1,0:T(8,128)(2,1)}), bf16[1,1536,1536]{2,1,0:T(8,128)(2,1)}) %all-gather.6.cloned.1.call-update) | async-done | bytes 4718608 | tf_op jit(solution)/shard_map/all_gather | solution.py:40
  95.4 9.3 %fusion.2 = bf16[1024,1536]{1,0:T(8,128)(2,1)} fusion(bf16[1536,1024]{1,0:T(8,128)(2,1)} %bitcast.13, bf16[1,1536,1536]{2,1,0:T(8,128)(2,1)} %all-gather.6.cloned.1.call-done), kind=kOutput, calls=%fused_computation.3 | convolution fusion | flops 4833411072 | bytes 11010048 | tf_op jit(solution)/shard_map/dot_general | solution.py:56
  104.7 47.0 %reduce-scatter.2.cloned.1.call-done = bf16[128,1536]{1,0:T(8,128)(2,1)} async-done(((bf16[1024,1536]{1,0:T(8,128)(2,1)}), bf16[128,1536]{1,0:T(8,128)(2,1)}) %reduce-scatter.2.cloned.1.call-update) | async-done | bytes 393232 | tf_op jit(solution)/shard_map/reduce_scatter | solution.py:77
  151.8 3.1 %fusion.21 = (bf16[128,1536]{1,0:T(8,128)(2,1)}, f32[128,1536]{1,0:T(8,128)}, f32[1,128,1536]{2,1,0:T(8,128)}, f32[1,128,1536]{2,1,0:T(8,128)}) fusion(f32[1,128,1536]{2,1,0:T(8,128)S(1)} %copy-done.4, bf16[128,1536]{1,0:T(8,128)(2,1)} %reduce-scatter.2.cloned.1.call-done, f32[1,128,1536]{2,1,0:T(8,128)S(1)} %copy-done.5, f32[1,128,1536]{2,1,0:T(8,128)S(1)} %copy-done.6), kind=kLoop, calls=%fused_computation.45 | loop fusion | flops 2949120 | bytes 5505024 | tf_op jit(solution)/shard_map/convert_element_type | solution.py:79
  156.0 2.2 collective-permute-start.4
  159.5 42.2 %all-gather.4.cloned.1.call-done = bf16[1024,1536]{1,0:T(8,128)(2,1)} async-done(((bf16[128,1536]{1,0:T(8,128)(2,1)}), bf16[1024,1536]{1,0:T(8,128)(2,1)}) %all-gather.4.cloned.1.call-update) | async-done | bytes 3145744 | tf_op jit(solution)/shard_map/all_gather | solution.py:81
  202.1 3.3 %fusion.6 = bf16[4,320,1024]{2,1,0:T(8,128)(2,1)S(1)} fusion(bf16[4,320,1024]{2,1,0:T(8,128)(2,1)S(1)} %broadcast_in_dim.52, s32[]{:T(128)S(6)} %select_n.80, bf16[320,1536]{1,0:T(8,128)(2,1)S(1)} %bitcast.91, bf16[1024,1536]{1,0:T(8,128)(2,1)} %all-gather.4.cloned.1.call-done), kind=kOutput, calls=%fused_computation.10 | convolution fusion | flops 1006960640 | bytes 4784132 | tf_op jit(solution)/shard_map/dot_general | solution.py:85
  205.4 2.4 fusion.8
  209.0 2.4 fusion.12
  213.0 8.2 %all-to-all-start.1 = ((bf16[32,40,1024]{2,1,0:T(8,128)(2,1)}), bf16[32,40,1024]{2,1,0:T(8,128)(2,1)S(1)}, u32[]{:S(2)}, u32[]{:S(2)}) async-start(bf16[32,40,1024]{2,1,0:T(8,128)(2,1)} %bitcast.89), calls=%async_computation.2 | async-start | bytes 5242880 | tf_op jit(solution)/shard_map/all_to_all | solution.py:90
  221.5 33.7 %all-to-all-done.1 = bf16[32,40,1024]{2,1,0:T(8,128)(2,1)S(1)} async-done(((bf16[32,40,1024]{2,1,0:T(8,128)(2,1)}), bf16[32,40,1024]{2,1,0:T(8,128)(2,1)S(1)}, u32[]{:S(2)}, u32[]{:S(2)}) %all-to-all-start.1) | async-done | bytes 2621472 | tf_op jit(solution)/shard_map/all_to_all | solution.py:90
  255.5 2.8 %convolution_convert_fusion = bf16[128,4096]{1,0:T(8,128)(2,1)} fusion(f32[128,320]{0,1:T(8,128)S(1)} %select_reduce_fusion, bf16[4096,320]{0,1:T(8,128)(2,1)S(1)} %bitcast.90), kind=kOutput, calls=%fused_computation | convolution fusion | flops 2013790208 | bytes 3833856 | tf_op jit(solution)/shard_map/ts,hsf->thf/dot_general | solution.py:99
  (57 shorter events, 14.5 us)
Async XLA Ops:
  7.2 88.2 %all-gather.6.cloned.1.call-start = ((), (), s32[]{:S(2)}) async-start(), calls=%async_computation.5 | async-start | bytes 5898240 | tf_op jit(solution)/shard_map/all_gather | solution.py:40
  13.2 9.4 %copy-start.2 = (bf16[384,1,1024]{0,2,1:T(8,128)(2,1)S(1)}, bf16[384,1,1024]{0,2,1:T(8,128)(2,1)}, u32[]{:S(2)}) copy-start(bf16[384,1,1024]{0,2,1:T(8,128)(2,1)} %get-tuple-element.10) | copy-start | bytes 2359300
  13.2 10.9 %copy-start.7 = (s32[128,2]{0,1:T(2,128)S(1)}, s32[128,2]{0,1:T(2,128)}, u32[]{:S(2)}) copy-start(s32[128,2]{0,1:T(2,128)} %param.14) | copy-start | bytes 3076
  13.2 12.2 %copy-start.3 = (bf16[128,2,1536]{2,1,0:T(2,128)(2,1)S(1)}, bf16[128,2,1536]{2,1,0:T(2,128)(2,1)}, u32[]{:S(2)}) copy-start(bf16[128,2,1536]{2,1,0:T(2,128)(2,1)} %param.13) | copy-start | bytes 2359300
  15.7 25.0 %collective-permute-start = (bf16[384,1024]{1,0:T(8,128)(2,1)}, bf16[384,1024]{1,0:T(8,128)(2,1)}, u32[]{:S(2)}, u32[]{:S(2)}) collective-permute-start(bf16[384,1024]{1,0:T(8,128)(2,1)} %bitcast.7), channel_id=1, source_target_pairs={{0,64},{64,128},{128,192},{192,0},{1,65},{65,129},{129,193},{193,1... | collective-permute-start | bytes 2359304 | tf_op jit(solution)/shard_map/ppermute | solution.py:51
  20.1 57.8 %collective-permute-start.1 = (bf16[384,1024]{1,0:T(8,128)(2,1)}, bf16[384,1024]{1,0:T(8,128)(2,1)}, u32[]{:S(2)}, u32[]{:S(2)}) collective-permute-start(bf16[384,1024]{1,0:T(8,128)(2,1)} %bitcast.9), channel_id=1, source_target_pairs={{0,128},{64,192},{128,0},{192,64},{1,129},{65,193},{129,1},{193,65... | collective-permute-start | bytes 2359304 | tf_op jit(solution)/shard_map/ppermute | solution.py:51
  23.0 10.0 %copy-start.1 = (bf16[384,1,1024]{0,2,1:T(8,128)(2,1)S(1)}, bf16[384,1,1024]{0,2,1:T(8,128)(2,1)}, u32[]{:S(2)}) copy-start(bf16[384,1,1024]{0,2,1:T(8,128)(2,1)} %get-tuple-element.13) | copy-start | bytes 2359300
  23.0 57.0 %collective-permute-start.2 = (bf16[384,1024]{1,0:T(8,128)(2,1)S(1)}, bf16[384,1024]{1,0:T(8,128)(2,1)}, u32[]{:S(2)}, u32[]{:S(2)}) collective-permute-start(bf16[384,1024]{1,0:T(8,128)(2,1)S(1)} %bitcast.92), channel_id=1, source_target_pairs={{0,192},{64,0},{128,64},{192,128},{1,193},{65,1},{129,65},{193,129... | collective-permute-start | bytes 2359304 | tf_op jit(solution)/shard_map/ppermute | solution.py:51
  27.2 77.5 %all-to-all-start = ((bf16[8,40,1536]{2,1,0:T(8,128)(2,1)}), bf16[8,40,1536]{2,1,0:T(8,128)(2,1)S(1)}, u32[]{:S(2)}, u32[]{:S(2)}) async-start(bf16[8,40,1536]{2,1,0:T(8,128)(2,1)} %bitcast.4), calls=%async_computation | async-start | bytes 1966080 | tf_op jit(solution)/shard_map/all_to_all | solution.py:70
  33.0 118.8 %reduce-scatter.2.cloned.1.call-start = ((), (), s32[]{:S(2)}) async-start(), calls=%async_computation.3 | async-start | bytes 3538944 | tf_op jit(solution)/shard_map/reduce_scatter | solution.py:77
  104.6 47.1 %copy-start.4 = (f32[1,128,1536]{2,1,0:T(8,128)S(1)}, f32[1,128,1536]{2,1,0:T(8,128)}, u32[]{:S(2)}) copy-start(f32[1,128,1536]{2,1,0:T(8,128)} %param.10) | copy-start | bytes 2359300
  104.6 47.1 %copy-start.5 = (f32[1,128,1536]{2,1,0:T(8,128)S(1)}, f32[1,128,1536]{2,1,0:T(8,128)}, u32[]{:S(2)}) copy-start(f32[1,128,1536]{2,1,0:T(8,128)} %param.9) | copy-start | bytes 2359300
  104.6 47.1 %copy-start.6 = (f32[1,128,1536]{2,1,0:T(8,128)S(1)}, f32[1,128,1536]{2,1,0:T(8,128)}, u32[]{:S(2)}) copy-start(f32[1,128,1536]{2,1,0:T(8,128)} %param.8) | copy-start | bytes 2359300
  104.7 97.1 %all-gather.4.cloned.1.call-start = ((), (), s32[]{:S(2)}) async-start(), calls=%async_computation.4 | async-start | bytes 3538944 | tf_op jit(solution)/shard_map/all_gather | solution.py:81
  154.9 50.5 %collective-permute-start.3 = (bf16[8,40,1536]{2,1,0:T(8,128)(2,1)S(1)}, bf16[8,40,1536]{2,1,0:T(8,128)(2,1)}, u32[]{:S(2)}, u32[]{:S(2)}) collective-permute-start(bf16[8,40,1536]{2,1,0:T(8,128)(2,1)S(1)} %all-to-all-done), channel_id=1, source_target_pairs={{0,64},{64,128},{128,192},{192,0},{1,65},{65,129},{129,193},{193,1... | collective-permute-start | bytes 2949128 | tf_op jit(solution)/shard_map/ppermute | solution.py:75
  156.0 51.8 %collective-permute-start.4 = (bf16[8,40,1536]{2,1,0:T(8,128)(2,1)S(1)}, bf16[8,40,1536]{2,1,0:T(8,128)(2,1)S(1)}, u32[]{:S(2)}, u32[]{:S(2)}) collective-permute-start(bf16[8,40,1536]{2,1,0:T(8,128)(2,1)S(1)} %all-to-all-done), channel_id=1, source_target_pairs={{0,128},{64,192},{128,0},{192,64},{1,129},{65,193},{129,1},{193,65... | collective-permute-start | bytes 2949128 | tf_op jit(solution)/shard_map/ppermute | solution.py:75
  158.3 50.8 %collective-permute-start.5 = (bf16[8,40,1536]{2,1,0:T(8,128)(2,1)S(1)}, bf16[8,40,1536]{2,1,0:T(8,128)(2,1)}, u32[]{:S(2)}, u32[]{:S(2)}) collective-permute-start(bf16[8,40,1536]{2,1,0:T(8,128)(2,1)S(1)} %all-to-all-done), channel_id=1, source_target_pairs={{0,192},{64,0},{128,64},{192,128},{1,193},{65,1},{129,65},{193,129... | collective-permute-start | bytes 2949128 | tf_op jit(solution)/shard_map/ppermute | solution.py:75
  202.1 3.3 %copy-start.9 = (bf16[1024,1536]{1,0:T(8,128)(2,1)S(1)}, bf16[1024,1536]{1,0:T(8,128)(2,1)}, u32[]{:S(2)}) copy-start(bf16[1024,1536]{1,0:T(8,128)(2,1)} %all-gather.4.cloned.1.call-done) | copy-start | bytes 9437188
  211.5 1.5 copy-start
  213.0 8.5 %copy-start.8 = (f32[128,2]{0,1:T(2,128)S(1)}, f32[128,2]{0,1:T(2,128)}, u32[]{:S(2)}) copy-start(f32[128,2]{0,1:T(2,128)} %param.15) | copy-start | bytes 3076
  213.0 42.2 %all-to-all-start.1 = ((bf16[32,40,1024]{2,1,0:T(8,128)(2,1)}), bf16[32,40,1024]{2,1,0:T(8,128)(2,1)S(1)}, u32[]{:S(2)}, u32[]{:S(2)}) async-start(bf16[32,40,1024]{2,1,0:T(8,128)(2,1)} %bitcast.89), calls=%async_computation.2 | async-start | bytes 5242880 | tf_op jit(solution)/shard_map/all_to_all | solution.py:90
Sparse Core Ops, SparseCore 0:
  9.8 85.5 all-gather.5
  104.8 46.9 reduce-scatter.1
  155.0 46.7 all-gather.3

commit v8 on v5

--- a/solution.py
+++ b/solution.py
@@ -68,8 +68,9 @@
     me_hi = lax.axis_index("dy")
 
     grad = lax.psum_scatter(partial, "dz", scatter_dimension=0, tiled=True).astype(jnp.float32)
-    master_new, m_new, v_new = adam_update(master[0], moment_one[0], moment_two[0], grad)
-    weights_shard = master_new.astype(jnp.bfloat16)
+    weights_shard = adam_update(master[0], moment_one[0], moment_two[0], grad)[0].astype(jnp.bfloat16)
+    state = lax.optimization_barrier((master[0], moment_one[0], moment_two[0], grad))
+    master_new, m_new, v_new = adam_update(*state)
 
     weights_group = lax.all_gather(weights_shard, "dz", axis=0, tiled=True)
     product = jnp.zeros((n_hi, experts * capacity, group_width), jnp.bfloat16)

time: 260 us -> 260 us (level)
  waiting for transfers between devices: 176 us -> 171 us
  other arithmetic: 3.87 us -> 8.14 us
    all_to_all x1, waiting for transfers between devices: 33.7 us -> 28.6 us  [body(): lax.all_to_all(product, ('dy', 'expert'), split_axis=0, concat_axis=0, ti...]
    broadcast_in_dim x0 -> x1, other arithmetic: none -> 3.3 us  [body(): return (master_new[None], m_new[None], v_new[None], mixed)]
    unnamed x16 -> x18, local copies, waits for them, and re-layouts: 6.32 us -> 6.32 us
  transfers between devices with their start and end apart: 9 -> 9, of which waited for: 5 -> 5; matrix products, arithmetic and copies ran while one was open for 12% -> 14% of each run, Pallas kernels for 0% -> 0%
where the time goes in v8:
time: 260 us
  waiting for transfers between devices  171 us (66%)
  starting transfers between devices  29.9 us (12%)
  matrix products  23 us (9%)
  between operations  13.9 us (5%)
  local copies, waits for them, and re-layouts  13.5 us (5%)
  other arithmetic  8.14 us (3%)
    all_to_all x1, waiting for transfers between devices, body(): lax.all_to_all(grads_here.reshape(saved, n_hi, group_width).transpose(1,...  51.4 us
    reduce_scatter x1, waiting for transfers between devices, body(): lax.psum_scatter(partial, 'dz', scatter_dimension=0, tiled=True)  45.2 us
    all_gather x1, waiting for transfers between devices, body(): weights_group = lax.all_gather(weights_shard, 'dz', axis=0, tiled=True)  42.1 us
    all_to_all x1, waiting for transfers between devices, body(): lax.all_to_all(product, ('dy', 'expert'), split_axis=0, concat_axis=0, ti...  28.6 us
    all_to_all x1, starting transfers between devices, body(): lax.all_to_all(outgoing, 'expert', split_axis=0, concat_axis=0, tiled=True)  11.5 us
    dot_general x1, matrix products, body(): lax.dot_general(grads_group, rows_group, (((0,), (0,)), ((), ())), prefer...  9.26 us
    dot_general x4, matrix products, body(): lax.dot_general(block, weights_group, (((1,), (1,)), ((), ())), preferred...  8.38 us
    all_to_all x1, starting transfers between devices, body(): lax.all_to_all(product, ('dy', 'expert'), split_axis=0, concat_axis=0, ti...  8.24 us
  transfers between devices with their start and end apart: 9, of which 5 were waited for; matrix products, arithmetic and copies ran while one was open for 14% of the time, Pallas kernels for 0%

profile of v8, /device:TPU:1, one launch (start us, length us, event | category | flops | bytes accessed | tf_op | source)
XLA Modules:
  0.0 259.7 jit_solution(3011816081376222149)
XLA Ops:
  7.9 4.7 %copy.37 = bf16[1,384,4096]{1,2,0:T(8,128)(2,1)} copy(bf16[1,384,4096]{2,1,0:T(8,128)(2,1)} %param.12) | data formatting | bytes 6291456 | tf_op args[4]
  12.6 5.1 %all-to-all-start.1 = ((bf16[4,384,1024]{1,2,0:T(8,128)(2,1)}), bf16[4,384,1024]{1,2,0:T(8,128)(2,1)S(1)}, u32[]{:S(2)}, u32[]{:S(2)}) async-start(bf16[4,384,1024]{1,2,0:T(8,128)(2,1)} %bitcast.68), calls=%async_computation.1 | async-start | bytes 6291456 | tf_op jit(solution)/shard_map/all_to_all | solution.py:41
  19.0 3.0 %reshape.76 = bf16[256,1536]{1,0:T(8,128)(2,1)} reshape(bf16[128,2,1536]{2,1,0:T(2,128)(2,1)} %param.13) | data formatting | bytes 1572864 | tf_op jit(solution)/shard_map/reshape | solution.py:59
  22.0 2.5 convolution_convert_fusion.1
  24.5 51.4 %all-to-all-done.1 = bf16[4,384,1024]{1,2,0:T(8,128)(2,1)S(1)} async-done(((bf16[4,384,1024]{1,2,0:T(8,128)(2,1)}), bf16[4,384,1024]{1,2,0:T(8,128)(2,1)S(1)}, u32[]{:S(2)}, u32[]{:S(2)}) %all-to-all-start.1) | async-done | bytes 3145760 | tf_op jit(solution)/shard_map/all_to_all | solution.py:41
  76.0 11.5 %all-to-all-start = ((bf16[8,40,1536]{2,1,0:T(8,128)(2,1)}), bf16[8,40,1536]{2,1,0:T(8,128)(2,1)}, u32[]{:S(2)}, u32[]{:S(2)}) async-start(bf16[8,40,1536]{2,1,0:T(8,128)(2,1)} %bitcast.72), calls=%async_computation | async-start | bytes 1966080 | tf_op jit(solution)/shard_map/all_to_all | solution.py:62
  87.5 3.0 %copy.38 = bf16[4,384,1024]{2,1,0:T(8,128)(2,1)} copy(bf16[4,384,1024]{1,2,0:T(8,128)(2,1)S(1)} %all-to-all-done.1) | data formatting | bytes 6291456 | tf_op jit(solution)/shard_map/all_to_all | solution.py:41
  90.4 3.2 %all-gather.6.cloned.1.call-done = bf16[1,1536,1536]{2,1,0:T(8,128)(2,1)} async-done(((bf16[1,384,1536]{2,1,0:T(8,128)(2,1)}), bf16[1,1536,1536]{2,1,0:T(8,128)(2,1)}) %all-gather.6.cloned.1.call-update) | async-done | bytes 4718608 | tf_op jit(solution)/shard_map/all_gather | solution.py:40
  93.7 9.3 %fusion.2 = bf16[1024,1536]{1,0:T(8,128)(2,1)} fusion(bf16[1536,1024]{1,0:T(8,128)(2,1)} %bitcast.73, bf16[1,1536,1536]{2,1,0:T(8,128)(2,1)} %all-gather.6.cloned.1.call-done), kind=kOutput, calls=%fused_computation.3 | convolution fusion | flops 4833411072 | bytes 11010048 | tf_op jit(solution)/shard_map/dot_general | solution.py:48
  103.0 45.2 %reduce-scatter.2.cloned.1.call-done = bf16[128,1536]{1,0:T(8,128)(2,1)} async-done(((bf16[1024,1536]{1,0:T(8,128)(2,1)}), bf16[128,1536]{1,0:T(8,128)(2,1)}) %reduce-scatter.2.cloned.1.call-update) | async-done | bytes 393232 | tf_op jit(solution)/shard_map/reduce_scatter | solution.py:70
  148.2 2.3 fusion.21
  150.5 1.2 collective-permute-start
  151.8 2.5 collective-permute-start.1
  154.3 1.2 collective-permute-start.2
  155.4 42.1 %all-gather.4.cloned.1.call-done = bf16[1024,1536]{1,0:T(8,128)(2,1)} async-done(((bf16[128,1536]{1,0:T(8,128)(2,1)}), bf16[1024,1536]{1,0:T(8,128)(2,1)}) %all-gather.4.cloned.1.call-update) | async-done | bytes 3145744 | tf_op jit(solution)/shard_map/all_gather | solution.py:75
  197.9 3.5 %fusion.6 = bf16[4,320,1024]{2,1,0:T(8,128)(2,1)S(1)} fusion(bf16[4,320,1024]{2,1,0:T(8,128)(2,1)S(1)} %broadcast_in_dim.32, s32[]{:T(128)S(6)} %select_n.32, bf16[320,1536]{1,0:T(8,128)(2,1)} %bitcast.13, bf16[1024,1536]{1,0:T(8,128)(2,1)} %all-gather.4.cloned.1.call-done), kind=kOutput, calls=%fused_computation.10 | convolution fusion | flops 1006960640 | bytes 4784132 | tf_op jit(solution)/shard_map/dot_general | solution.py:79
  201.5 1.2 fusion.8
  202.7 1.2 fusion.10
  204.0 2.4 fusion.12
  206.4 1.5 copy-done
  207.9 8.2 %all-to-all-start.2 = ((bf16[32,40,1024]{2,1,0:T(8,128)(2,1)}), bf16[32,40,1024]{2,1,0:T(8,128)(2,1)S(1)}, u32[]{:S(2)}, u32[]{:S(2)}) async-start(bf16[32,40,1024]{2,1,0:T(8,128)(2,1)} %bitcast.70), calls=%async_computation.3 | async-start | bytes 5242880 | tf_op jit(solution)/shard_map/all_to_all | solution.py:84
  218.1 3.3 %fusion.23 = (f32[1,128,1536]{2,1,0:T(8,128)}, f32[1,128,1536]{2,1,0:T(8,128)}, f32[1,128,1536]{2,1,0:T(8,128)}) fusion(f32[128,1536]{1,0:T(8,128)S(1)} %convert_element_type.41, f32[128,1536]{1,0:T(8,128)S(1)} %bitcast.74, f32[128,1536]{1,0:T(8,128)} %bitcast.75, f32[128,1536]{1,0:T(8,128)} %bitcast.76), kind=kLoop, calls=%fused_computation.34 | loop fusion | flops 2555904 | bytes 5505024 | tf_op jit(solution)/shard_map/broadcast_in_dim | solution.py:101
  221.5 28.6 %all-to-all-done.2 = bf16[32,40,1024]{2,1,0:T(8,128)(2,1)S(1)} async-done(((bf16[32,40,1024]{2,1,0:T(8,128)(2,1)}), bf16[32,40,1024]{2,1,0:T(8,128)(2,1)S(1)}, u32[]{:S(2)}, u32[]{:S(2)}) %all-to-all-start.2) | async-done | bytes 2621472 | tf_op jit(solution)/shard_map/all_to_all | solution.py:84
  250.4 2.8 %convolution_convert_fusion = bf16[128,4096]{1,0:T(8,128)(2,1)} fusion(f32[128,320]{0,1:T(8,128)S(1)} %copy-done.4, bf16[4096,320]{0,1:T(8,128)(2,1)S(1)} %bitcast.71), kind=kOutput, calls=%fused_computation | convolution fusion | flops 2013790208 | bytes 3833856 | tf_op jit(solution)/shard_map/ts,hsf->thf/dot_general | solution.py:93
  (42 shorter events, 4.7 us)
Async XLA Ops:
  7.2 86.5 %all-gather.6.cloned.1.call-start = ((), (), s32[]{:S(2)}) async-start(), calls=%async_computation.6 | async-start | bytes 5898240 | tf_op jit(solution)/shard_map/all_gather | solution.py:40
  12.6 5.1 %copy-start.5 = (s32[128,2]{0,1:T(2,128)S(1)}, s32[128,2]{0,1:T(2,128)}, u32[]{:S(2)}) copy-start(s32[128,2]{0,1:T(2,128)} %param.14) | copy-start | bytes 3076
  12.6 63.4 %all-to-all-start.1 = ((bf16[4,384,1024]{1,2,0:T(8,128)(2,1)}), bf16[4,384,1024]{1,2,0:T(8,128)(2,1)S(1)}, u32[]{:S(2)}, u32[]{:S(2)}) async-start(bf16[4,384,1024]{1,2,0:T(8,128)(2,1)} %bitcast.68), calls=%async_computation.1 | async-start | bytes 6291456 | tf_op jit(solution)/shard_map/all_to_all | solution.py:41
  76.0 27.0 %all-to-all-start = ((bf16[8,40,1536]{2,1,0:T(8,128)(2,1)}), bf16[8,40,1536]{2,1,0:T(8,128)(2,1)}, u32[]{:S(2)}, u32[]{:S(2)}) async-start(bf16[8,40,1536]{2,1,0:T(8,128)(2,1)} %bitcast.72), calls=%async_computation | async-start | bytes 1966080 | tf_op jit(solution)/shard_map/all_to_all | solution.py:62
  87.5 60.7 %reduce-scatter.2.cloned.1.call-start = ((), (), s32[]{:S(2)}) async-start(), calls=%async_computation.4 | async-start | bytes 3538944 | tf_op jit(solution)/shard_map/reduce_scatter | solution.py:70
  102.9 45.2 %copy-start.1 = (f32[1,128,1536]{2,1,0:T(8,128)S(1)}, f32[1,128,1536]{2,1,0:T(8,128)}, u32[]{:S(2)}) copy-start(f32[1,128,1536]{2,1,0:T(8,128)} %param.10) | copy-start | bytes 2359300
  102.9 45.2 %copy-start.2 = (f32[1,128,1536]{2,1,0:T(8,128)S(1)}, f32[1,128,1536]{2,1,0:T(8,128)}, u32[]{:S(2)}) copy-start(f32[1,128,1536]{2,1,0:T(8,128)} %param.8) | copy-start | bytes 2359300
  102.9 45.2 %copy-start.3 = (f32[1,128,1536]{2,1,0:T(8,128)S(1)}, f32[1,128,1536]{2,1,0:T(8,128)}, u32[]{:S(2)}) copy-start(f32[1,128,1536]{2,1,0:T(8,128)} %param.9) | copy-start | bytes 2359300
  103.0 94.6 %all-gather.4.cloned.1.call-start = ((), (), s32[]{:S(2)}) async-start(), calls=%async_computation.5 | async-start | bytes 3538944 | tf_op jit(solution)/shard_map/all_gather | solution.py:75
  150.5 50.9 %collective-permute-start = (bf16[8,40,1536]{2,1,0:T(8,128)(2,1)}, bf16[8,40,1536]{2,1,0:T(8,128)(2,1)S(1)}, u32[]{:S(2)}, u32[]{:S(2)}) collective-permute-start(bf16[8,40,1536]{2,1,0:T(8,128)(2,1)} %all-to-all-done), channel_id=1, source_target_pairs={{0,64},{64,128},{128,192},{192,0},{1,65},{65,129},{129,193},{193,1... | collective-permute-start | bytes 2949128 | tf_op jit(solution)/shard_map/ppermute | solution.py:67
  151.8 50.9 %collective-permute-start.1 = (bf16[8,40,1536]{2,1,0:T(8,128)(2,1)}, bf16[8,40,1536]{2,1,0:T(8,128)(2,1)S(1)}, u32[]{:S(2)}, u32[]{:S(2)}) collective-permute-start(bf16[8,40,1536]{2,1,0:T(8,128)(2,1)} %all-to-all-done), channel_id=1, source_target_pairs={{0,128},{64,192},{128,0},{192,64},{1,129},{65,193},{129,1},{193,65... | collective-permute-start | bytes 2949128 | tf_op jit(solution)/shard_map/ppermute | solution.py:67
  154.3 49.7 %collective-permute-start.2 = (bf16[8,40,1536]{2,1,0:T(8,128)(2,1)}, bf16[8,40,1536]{2,1,0:T(8,128)(2,1)}, u32[]{:S(2)}, u32[]{:S(2)}) collective-permute-start(bf16[8,40,1536]{2,1,0:T(8,128)(2,1)} %all-to-all-done), channel_id=1, source_target_pairs={{0,192},{64,0},{128,64},{192,128},{1,193},{65,1},{129,65},{193,129... | collective-permute-start | bytes 2949128 | tf_op jit(solution)/shard_map/ppermute | solution.py:67
  197.9 3.6 %copy-start.7 = (bf16[1024,1536]{1,0:T(8,128)(2,1)S(1)}, bf16[1024,1536]{1,0:T(8,128)(2,1)}, u32[]{:S(2)}) copy-start(bf16[1024,1536]{1,0:T(8,128)(2,1)} %all-gather.4.cloned.1.call-done) | copy-start | bytes 9437188
  206.4 1.5 copy-start
  207.9 8.5 %copy-start.6 = (f32[128,2]{0,1:T(2,128)S(1)}, f32[128,2]{0,1:T(2,128)}, u32[]{:S(2)}) copy-start(f32[128,2]{0,1:T(2,128)} %param.15) | copy-start | bytes 3076
  207.9 42.2 %all-to-all-start.2 = ((bf16[32,40,1024]{2,1,0:T(8,128)(2,1)}), bf16[32,40,1024]{2,1,0:T(8,128)(2,1)S(1)}, u32[]{:S(2)}, u32[]{:S(2)}) async-start(bf16[32,40,1024]{2,1,0:T(8,128)(2,1)} %bitcast.70), calls=%async_computation.3 | async-start | bytes 5242880 | tf_op jit(solution)/shard_map/all_to_all | solution.py:84
  221.4 28.9 %copy-start.4 = (f32[128,320]{0,1:T(8,128)S(1)}, f32[128,320]{0,1:T(8,128)}, u32[]{:S(2)}) copy-start(f32[128,320]{0,1:T(8,128)} %select_reduce_fusion) | copy-start | bytes 491524
Sparse Core Ops, SparseCore 0:
  9.8 83.8 all-gather.5
  103.1 45.0 reduce-scatter.1
  150.7 46.8 all-gather.3

commit v9 on v5

--- a/solution.py
+++ b/solution.py
@@ -89,14 +89,15 @@
         (slot_pairs[:, :, None] == table[None, None, :]).astype(jnp.float32) * gates[:, :, None],
         axis=1,
     )
-    mixed = jnp.einsum(
-        "ts,hsf->thf",
-        combine,
-        returned.astype(jnp.float32),
-        precision=lax.Precision.HIGHEST,
-        preferred_element_type=jnp.float32,
-    )
-    mixed = mixed.reshape(tok_count, n_hi * group_width).astype(jnp.bfloat16)
+    high = combine.astype(jnp.bfloat16)
+    low = (combine - high.astype(jnp.float32)).astype(jnp.bfloat16)
+    outputs = returned.transpose(1, 0, 2).reshape(experts * capacity, n_hi * group_width)
+    mixed = sum(
+        lax.dot_general(
+            part, outputs, (((1,), (0,)), ((), ())), preferred_element_type=jnp.float32
+        )
+        for part in (high, low)
+    ).astype(jnp.bfloat16)
     return (master_new[None], m_new[None], v_new[None], mixed)
 
 

time: 260 us -> 259 us (level)
  no operation moved by 1% of the time
where the time goes in v9:
time: 259 us
  waiting for transfers between devices  176 us (68%)
  starting transfers between devices  29.8 us (12%)
  matrix products  21.4 us (8%)
  between operations  13.9 us (5%)
  local copies, waits for them, and re-layouts  13.5 us (5%)
  other arithmetic  3.86 us (1%)
    all_to_all x1, waiting for transfers between devices, body(): lax.all_to_all(grads_here.reshape(saved, n_hi, group_width).transpose(1,...  51.4 us
    reduce_scatter x1, waiting for transfers between devices, body(): lax.psum_scatter(partial, 'dz', scatter_dimension=0, tiled=True)  45.1 us
    all_gather x1, waiting for transfers between devices, body(): weights_group = lax.all_gather(weights_shard, 'dz', axis=0, tiled=True)  42.3 us
    all_to_all x1, waiting for transfers between devices, body(): lax.all_to_all(product, ('dy', 'expert'), split_axis=0, concat_axis=0, ti...  33.7 us
    all_to_all x1, starting transfers between devices, body(): lax.all_to_all(outgoing, 'expert', split_axis=0, concat_axis=0, tiled=True)  11.5 us
    dot_general x1, matrix products, body(): lax.dot_general(grads_group, rows_group, (((0,), (0,)), ((), ())), prefer...  9.25 us
    all_to_all x1, starting transfers between devices, body(): lax.all_to_all(product, ('dy', 'expert'), split_axis=0, concat_axis=0, ti...  8.23 us
    dot_general x4, matrix products, body(): lax.dot_general(block, weights_group, (((1,), (1,)), ((), ())), preferred...  7.18 us
  transfers between devices with their start and end apart: 9, of which 5 were waited for; matrix products, arithmetic and copies ran while one was open for 12% of the time, Pallas kernels for 0%

profile of v9, /device:TPU:1, one launch (start us, length us, event | category | flops | bytes accessed | tf_op | source)
XLA Modules:
  0.0 258.9 jit_solution(4127827692106524829)
XLA Ops:
  7.9 4.7 %copy.37 = bf16[1,384,4096]{1,2,0:T(8,128)(2,1)} copy(bf16[1,384,4096]{2,1,0:T(8,128)(2,1)} %param.12) | data formatting | bytes 6291456 | tf_op args[4]
  12.6 5.1 %all-to-all-start.1 = ((bf16[4,384,1024]{1,2,0:T(8,128)(2,1)}), bf16[4,384,1024]{1,2,0:T(8,128)(2,1)S(1)}, u32[]{:S(2)}, u32[]{:S(2)}) async-start(bf16[4,384,1024]{1,2,0:T(8,128)(2,1)} %bitcast.80), calls=%async_computation.1 | async-start | bytes 6291456 | tf_op jit(solution)/shard_map/all_to_all | solution.py:41
  18.1 3.0 %reshape.81 = bf16[256,1536]{1,0:T(8,128)(2,1)} reshape(bf16[128,2,1536]{2,1,0:T(2,128)(2,1)} %param.13) | data formatting | bytes 1572864 | tf_op jit(solution)/shard_map/reshape | solution.py:59
  22.0 2.5 convolution_convert_fusion
  24.5 51.4 %all-to-all-done.1 = bf16[4,384,1024]{1,2,0:T(8,128)(2,1)S(1)} async-done(((bf16[4,384,1024]{1,2,0:T(8,128)(2,1)}), bf16[4,384,1024]{1,2,0:T(8,128)(2,1)S(1)}, u32[]{:S(2)}, u32[]{:S(2)}) %all-to-all-start.1) | async-done | bytes 3145760 | tf_op jit(solution)/shard_map/all_to_all | solution.py:41
  76.0 11.5 %all-to-all-start = ((bf16[8,40,1536]{2,1,0:T(8,128)(2,1)}), bf16[8,40,1536]{2,1,0:T(8,128)(2,1)}, u32[]{:S(2)}, u32[]{:S(2)}) async-start(bf16[8,40,1536]{2,1,0:T(8,128)(2,1)} %bitcast.83), calls=%async_computation | async-start | bytes 1966080 | tf_op jit(solution)/shard_map/all_to_all | solution.py:62
  87.5 3.0 %copy.38 = bf16[4,384,1024]{2,1,0:T(8,128)(2,1)} copy(bf16[4,384,1024]{1,2,0:T(8,128)(2,1)S(1)} %all-to-all-done.1) | data formatting | bytes 6291456 | tf_op jit(solution)/shard_map/all_to_all | solution.py:41
  90.5 3.2 %all-gather.6.cloned.1.call-done = bf16[1,1536,1536]{2,1,0:T(8,128)(2,1)} async-done(((bf16[1,384,1536]{2,1,0:T(8,128)(2,1)}), bf16[1,1536,1536]{2,1,0:T(8,128)(2,1)}) %all-gather.6.cloned.1.call-update) | async-done | bytes 4718608 | tf_op jit(solution)/shard_map/all_gather | solution.py:40
  93.7 9.3 %fusion.3 = bf16[1024,1536]{1,0:T(8,128)(2,1)} fusion(bf16[1536,1024]{1,0:T(8,128)(2,1)} %bitcast.84, bf16[1,1536,1536]{2,1,0:T(8,128)(2,1)} %all-gather.6.cloned.1.call-done), kind=kOutput, calls=%fused_computation.4 | convolution fusion | flops 4833411072 | bytes 11010048 | tf_op jit(solution)/shard_map/dot_general | solution.py:48
  103.0 45.1 %reduce-scatter.2.cloned.1.call-done = bf16[128,1536]{1,0:T(8,128)(2,1)} async-done(((bf16[1024,1536]{1,0:T(8,128)(2,1)}), bf16[128,1536]{1,0:T(8,128)(2,1)}) %reduce-scatter.2.cloned.1.call-update) | async-done | bytes 393232 | tf_op jit(solution)/shard_map/reduce_scatter | solution.py:70
  148.1 3.1 %fusion.25 = (bf16[128,1536]{1,0:T(8,128)(2,1)}, f32[128,1536]{1,0:T(8,128)}, f32[1,128,1536]{2,1,0:T(8,128)}, f32[1,128,1536]{2,1,0:T(8,128)}) fusion(f32[1,128,1536]{2,1,0:T(8,128)S(1)} %copy-done.1, bf16[128,1536]{1,0:T(8,128)(2,1)} %reduce-scatter.2.cloned.1.call-done, f32[1,128,1536]{2,1,0:T(8,128)S(1)} %copy-done.2, f32[1,128,1536]{2,1,0:T(8,128)S(1)} %copy-done.3), kind=kLoop, calls=%fused_computation.42 | loop fusion | flops 2949120 | bytes 5505024 | tf_op jit(solution)/shard_map/convert_element_type | solution.py:72
  151.3 1.2 collective-permute-start
  152.5 2.4 collective-permute-start.1
  154.9 1.1 collective-permute-start.2
  156.1 42.3 %all-gather.4.cloned.1.call-done = bf16[1024,1536]{1,0:T(8,128)(2,1)} async-done(((bf16[128,1536]{1,0:T(8,128)(2,1)}), bf16[1024,1536]{1,0:T(8,128)(2,1)}) %all-gather.4.cloned.1.call-update) | async-done | bytes 3145744 | tf_op jit(solution)/shard_map/all_gather | solution.py:74
  198.7 3.5 %fusion.7 = bf16[4,320,1024]{2,1,0:T(8,128)(2,1)S(1)} fusion(bf16[4,320,1024]{2,1,0:T(8,128)(2,1)S(1)} %broadcast_in_dim.32, s32[]{:T(128)S(6)} %select_n.32, bf16[320,1536]{1,0:T(8,128)(2,1)} %bitcast.13, bf16[1024,1536]{1,0:T(8,128)(2,1)} %all-gather.4.cloned.1.call-done), kind=kOutput, calls=%fused_computation.11 | convolution fusion | flops 1006960640 | bytes 4784132 | tf_op jit(solution)/shard_map/dot_general | solution.py:78
  202.3 1.2 fusion.9
  203.5 1.2 fusion.11
  204.7 1.2 fusion.13
  205.9 1.5 copy-done
  207.4 8.2 %all-to-all-start.2 = ((bf16[32,40,1024]{2,1,0:T(8,128)(2,1)}), bf16[32,40,1024]{2,1,0:T(8,128)(2,1)S(1)}, u32[]{:S(2)}, u32[]{:S(2)}) async-start(bf16[32,40,1024]{2,1,0:T(8,128)(2,1)} %bitcast.82), calls=%async_computation.3 | async-start | bytes 5242880 | tf_op jit(solution)/shard_map/all_to_all | solution.py:83
  216.0 33.7 %all-to-all-done.2 = bf16[32,40,1024]{2,1,0:T(8,128)(2,1)S(1)} async-done(((bf16[32,40,1024]{2,1,0:T(8,128)(2,1)}), bf16[32,40,1024]{2,1,0:T(8,128)(2,1)S(1)}, u32[]{:S(2)}, u32[]{:S(2)}) %all-to-all-start.2) | async-done | bytes 2621472 | tf_op jit(solution)/shard_map/all_to_all | solution.py:83
  249.9 0.7 fusion.20
  250.7 1.7 fusion
  (39 shorter events, 3.0 us)
Async XLA Ops:
  7.2 86.5 %all-gather.6.cloned.1.call-start = ((), (), s32[]{:S(2)}) async-start(), calls=%async_computation.6 | async-start | bytes 5898240 | tf_op jit(solution)/shard_map/all_gather | solution.py:40
  12.6 5.1 %copy-start.4 = (s32[128,2]{0,1:T(2,128)S(1)}, s32[128,2]{0,1:T(2,128)}, u32[]{:S(2)}) copy-start(s32[128,2]{0,1:T(2,128)} %param.14) | copy-start | bytes 3076
  12.6 63.4 %all-to-all-start.1 = ((bf16[4,384,1024]{1,2,0:T(8,128)(2,1)}), bf16[4,384,1024]{1,2,0:T(8,128)(2,1)S(1)}, u32[]{:S(2)}, u32[]{:S(2)}) async-start(bf16[4,384,1024]{1,2,0:T(8,128)(2,1)} %bitcast.80), calls=%async_computation.1 | async-start | bytes 6291456 | tf_op jit(solution)/shard_map/all_to_all | solution.py:41
  76.0 27.0 %all-to-all-start = ((bf16[8,40,1536]{2,1,0:T(8,128)(2,1)}), bf16[8,40,1536]{2,1,0:T(8,128)(2,1)}, u32[]{:S(2)}, u32[]{:S(2)}) async-start(bf16[8,40,1536]{2,1,0:T(8,128)(2,1)} %bitcast.83), calls=%async_computation | async-start | bytes 1966080 | tf_op jit(solution)/shard_map/all_to_all | solution.py:62
  87.5 60.7 %reduce-scatter.2.cloned.1.call-start = ((), (), s32[]{:S(2)}) async-start(), calls=%async_computation.4 | async-start | bytes 3538944 | tf_op jit(solution)/shard_map/reduce_scatter | solution.py:70
  102.9 45.2 %copy-start.1 = (f32[1,128,1536]{2,1,0:T(8,128)S(1)}, f32[1,128,1536]{2,1,0:T(8,128)}, u32[]{:S(2)}) copy-start(f32[1,128,1536]{2,1,0:T(8,128)} %param.10) | copy-start | bytes 2359300
  102.9 45.2 %copy-start.2 = (f32[1,128,1536]{2,1,0:T(8,128)S(1)}, f32[1,128,1536]{2,1,0:T(8,128)}, u32[]{:S(2)}) copy-start(f32[1,128,1536]{2,1,0:T(8,128)} %param.9) | copy-start | bytes 2359300
  102.9 45.2 %copy-start.3 = (f32[1,128,1536]{2,1,0:T(8,128)S(1)}, f32[1,128,1536]{2,1,0:T(8,128)}, u32[]{:S(2)}) copy-start(f32[1,128,1536]{2,1,0:T(8,128)} %param.8) | copy-start | bytes 2359300
  103.0 95.4 %all-gather.4.cloned.1.call-start = ((), (), s32[]{:S(2)}) async-start(), calls=%async_computation.5 | async-start | bytes 3538944 | tf_op jit(solution)/shard_map/all_gather | solution.py:74
  151.3 51.0 %collective-permute-start = (bf16[8,40,1536]{2,1,0:T(8,128)(2,1)}, bf16[8,40,1536]{2,1,0:T(8,128)(2,1)S(1)}, u32[]{:S(2)}, u32[]{:S(2)}) collective-permute-start(bf16[8,40,1536]{2,1,0:T(8,128)(2,1)} %all-to-all-done), channel_id=1, source_target_pairs={{0,64},{64,128},{128,192},{192,0},{1,65},{65,129},{129,193},{193,1... | collective-permute-start | bytes 2949128 | tf_op jit(solution)/shard_map/ppermute | solution.py:67
  152.5 51.0 %collective-permute-start.1 = (bf16[8,40,1536]{2,1,0:T(8,128)(2,1)}, bf16[8,40,1536]{2,1,0:T(8,128)(2,1)S(1)}, u32[]{:S(2)}, u32[]{:S(2)}) collective-permute-start(bf16[8,40,1536]{2,1,0:T(8,128)(2,1)} %all-to-all-done), channel_id=1, source_target_pairs={{0,128},{64,192},{128,0},{192,64},{1,129},{65,193},{129,1},{193,65... | collective-permute-start | bytes 2949128 | tf_op jit(solution)/shard_map/ppermute | solution.py:67
  154.9 49.8 %collective-permute-start.2 = (bf16[8,40,1536]{2,1,0:T(8,128)(2,1)}, bf16[8,40,1536]{2,1,0:T(8,128)(2,1)S(1)}, u32[]{:S(2)}, u32[]{:S(2)}) collective-permute-start(bf16[8,40,1536]{2,1,0:T(8,128)(2,1)} %all-to-all-done), channel_id=1, source_target_pairs={{0,192},{64,0},{128,64},{192,128},{1,193},{65,1},{129,65},{193,129... | collective-permute-start | bytes 2949128 | tf_op jit(solution)/shard_map/ppermute | solution.py:67
  198.7 3.6 %copy-start.6 = (bf16[1024,1536]{1,0:T(8,128)(2,1)S(1)}, bf16[1024,1536]{1,0:T(8,128)(2,1)}, u32[]{:S(2)}) copy-start(bf16[1024,1536]{1,0:T(8,128)(2,1)} %all-gather.4.cloned.1.call-done) | copy-start | bytes 9437188
  205.9 1.5 copy-start
  207.4 8.5 %copy-start.5 = (f32[128,2]{0,1:T(2,128)S(1)}, f32[128,2]{0,1:T(2,128)}, u32[]{:S(2)}) copy-start(f32[128,2]{0,1:T(2,128)} %param.15) | copy-start | bytes 3076
  207.4 42.2 %all-to-all-start.2 = ((bf16[32,40,1024]{2,1,0:T(8,128)(2,1)}), bf16[32,40,1024]{2,1,0:T(8,128)(2,1)S(1)}, u32[]{:S(2)}, u32[]{:S(2)}) async-start(bf16[32,40,1024]{2,1,0:T(8,128)(2,1)} %bitcast.82), calls=%async_computation.3 | async-start | bytes 5242880 | tf_op jit(solution)/shard_map/all_to_all | solution.py:83
Sparse Core Ops, SparseCore 0:
  9.8 83.8 all-gather.5
  103.1 45.0 reduce-scatter.1
  151.4 46.9 all-gather.3
